TPU v7x, 256 devices: a whole 4x4x8 slice. The times are simulated.
256 devices in a mesh: pipe: 8 (over z_hi, x), expert: 32 (over y, z_lo, core).
Axes of the slice: x: 4, y: 4, z: 8 (z_hi: 2, z_lo: 4; z = z_hi * 4 + z_lo), core: 2. Of those that a mesh axis runs over, the one named last changes fastest.
Arguments:
- grad_out: bfloat16 [8, 4096, 2048], P('pipe', 'expert'), may hold values from -6 to 6
- expert_ids: int32 [8, 4096, 8], P('pipe', 'expert'), may hold values from 0 to 63, as said below
- slot_ids: int32 [8, 4096, 8], P('pipe', 'expert'), may hold values from 0 to 16, as said below
- gate_weights: float32 [8, 4096, 8], P('pipe', 'expert'), may hold values from 0.02 to 0.6
- saved_pre: bfloat16 [8, 64, 512, 1536], P('pipe', 'expert'), may hold values from -6 to 6
- down_weight: bfloat16 [8, 64, 768, 2048], P('pipe', 'expert'), may hold values from -0.21875 to 0.21875
- router_weight: bfloat16 [8, 64, 2048], P('pipe', 'expert'), may hold values from -0.125 to 0.125
Outputs:
- pre_grad: bfloat16 [8, 64, 512, 1536], P('pipe', 'expert')
- grad_inputs: bfloat16 [8, 4096, 2048], P('pipe', 'expert')
Inputs may be any that keep to these rules, and one draw needn't show every extreme that they name: `expert_ids`: each row names 8 different experts. `slot_ids`: for the pair (t, k): the number of earlier pairs (by row, then by k) among the same device's 128 rows of that section that name the same expert, capped at 16; the value 16 marks a pair that is dropped.
All inputs are finite; a program needn't handle non-finite values.
Results may differ from a plain program's by a relative error of at most 0.012.
Values may be sent and summed in bfloat16 or wider, within the bound.
No kernel may reach another device: no remote copies, remote signals or barrier semaphores. Data moves between devices by JAX's collectives and lax.ppermute only.
A program may use at most 128 MiB of HBM per device.

v0:
```python
import jax
import jax.numpy as jnp
from jax import lax
from jax.sharding import PartitionSpec as P


def passed_along(value, axis, by):
    peers = lax.axis_size(axis)
    return lax.ppermute(value, axis, [(i, (i + by) % peers) for i in range(peers)])


def per_device(grad_out, expert_ids, slot_ids, gate_weights, saved_pre, down_weight, router_weight):
    groups = lax.axis_size("expert")
    local_experts = down_weight.shape[1]
    hidden_width = down_weight.shape[2]
    tok_rows = grad_out.shape[1]
    top_count = expert_ids.shape[2]
    expert_total = local_experts * groups
    capacity = tok_rows * top_count // expert_total
    total_rows = expert_total * capacity
    features = grad_out[0]
    route_ids = expert_ids[0]
    kept_pairs = slot_ids[0] < capacity
    destination = (
        route_ids % local_experts * (groups * capacity)
        + route_ids // local_experts * capacity
        + jnp.minimum(slot_ids[0], capacity - 1)
    )
    pair_dest = jnp.where(kept_pairs, destination, total_rows).reshape(-1)
    row_ids = jnp.arange(total_rows, dtype=jnp.int32)
    matches = pair_dest[None, :] == row_ids[:, None]
    pair_token = jnp.arange(tok_rows * top_count, dtype=jnp.int32) // top_count
    slot_token = jnp.sum(jnp.where(matches, pair_token[None, :], 0), axis=1)
    occupied = jnp.any(matches, axis=1)
    gate_low = gate_weights[0].astype(jnp.bfloat16)
    slot_gate = jnp.sum(
        jnp.where(matches, gate_low.reshape(-1).astype(jnp.float32)[None, :], jnp.float32(0.0)),
        axis=1,
    )
    token_rows = jnp.take(features, slot_token, axis=0)
    token_rows = jnp.where(occupied[:, None], token_rows, jnp.zeros_like(token_rows))
    pre_saved = saved_pre[0]
    gate_part = pre_saved[..., :hidden_width].astype(jnp.float32)
    up_part = pre_saved[..., hidden_width:].astype(jnp.float32)
    sigmoid_gate = jax.nn.sigmoid(gate_part)
    silu_gate = gate_part * sigmoid_gate
    hidden = (silu_gate * up_part).astype(jnp.bfloat16)
    weights = down_weight[0]
    expert_out = jnp.einsum(
        "jsf,jfd->jsd", hidden, weights, preferred_element_type=jnp.float32
    ).astype(jnp.bfloat16)
    scaled = (slot_gate[:, None] * token_rows.astype(jnp.float32)).astype(jnp.bfloat16)
    arrived = lax.all_to_all(
        scaled.reshape(local_experts, groups, capacity, -1),
        "expert",
        split_axis=1,
        concat_axis=1,
        tiled=True,
    )
    scaled_rows = arrived.reshape(local_experts, groups * capacity, -1)
    returned = lax.all_to_all(
        expert_out.reshape(local_experts, groups, capacity, -1),
        "expert",
        split_axis=1,
        concat_axis=1,
        tiled=True,
    )
    pair_out = jnp.take(
        returned.reshape(total_rows, -1), pair_dest, axis=0, mode="fill", fill_value=0
    )
    pair_scores = jnp.sum(
        pair_out.reshape(tok_rows, top_count, -1).astype(jnp.float32)
        * features.astype(jnp.float32)[:, None, :],
        axis=-1,
    )
    row_grad = jnp.einsum("jsd,jfd->jsf", scaled_rows, weights, preferred_element_type=jnp.float32)
    gate_grad = row_grad * up_part * sigmoid_gate * (1.0 + gate_part * (1.0 - sigmoid_gate))
    up_grad = row_grad * silu_gate
    pre_grad = jnp.concatenate([gate_grad, up_grad], axis=-1).astype(jnp.bfloat16)
    gate_values = gate_weights[0]
    weighted_sum = jnp.sum(gate_values * pair_scores, axis=-1, keepdims=True)
    select_grad = gate_values * (pair_scores - weighted_sum)
    expert_columns = jnp.arange(expert_total, dtype=jnp.int32)
    chosen = route_ids[:, :, None] == expert_columns[None, None, :]
    logit_grad = jnp.sum(
        jnp.where(chosen, select_grad[:, :, None], jnp.float32(0.0)), axis=1
    ).astype(jnp.bfloat16)
    router_part = jnp.dot(
        logit_grad,
        lax.all_gather(router_weight[0], "expert", axis=0, tiled=True),
        preferred_element_type=jnp.float32,
    )
    section_grad = (features.astype(jnp.float32) + router_part).astype(jnp.bfloat16)
    outgoing = passed_along(section_grad, "pipe", -1)
    return (pre_grad[None], outgoing[None])


def solution(mesh):
    in_specs = (
        P("pipe", "expert", None),
        P("pipe", "expert", None),
        P("pipe", "expert", None),
        P("pipe", "expert", None),
        P("pipe", "expert", None, None),
        P("pipe", "expert", None, None),
        P("pipe", "expert", None),
    )
    out_specs = (P("pipe", "expert", None, None), P("pipe", "expert", None))
    return jax.shard_map(
        per_device, mesh=mesh, in_specs=in_specs, out_specs=out_specs, check_vma=False
    )
```

profile of v0, /device:TPU:6, one launch (start us, length us, event | category | flops | bytes accessed | tf_op | source)
XLA Modules:
  0.0 298.2 jit_solution(13683775158880791183)
XLA Ops:
  0.6 7.4 %fusion.7 = bf16[2,512,2048]{2,1,0:T(8,128)(2,1)S(1)} fusion(bf16[1,2,768,2048]{3,2,1,0:T(8,128)(2,1)} %param.12, bf16[2,512,1536]{2,1,0:T(8,128)(2,1)} %bitcast.59), kind=kOutput, calls=%fused_computation.20 | convolution fusion | flops 3229614080 | bytes 13631488 | tf_op jit(solution)/shard_map/jsf,jfd->jsd/dot_general | solution.py:49
  8.0 2.3 copy.68
  10.3 9.2 %all-to-all-start.1 = ((bf16[2,32,16,2048]{3,2,0,1:T(8,128)(2,1)}), bf16[2,32,16,2048]{3,2,0,1:T(8,128)(2,1)}, u32[]{:S(2)}, u32[]{:S(2)}) async-start(bf16[2,32,16,2048]{3,2,0,1:T(8,128)(2,1)} %copy.68), calls=%async_computation.1 | async-start | bytes 8388608 | tf_op jit(solution)/shard_map/all_to_all | solution.py:61
  19.5 0.0 copy-done.1
  19.5 0.1 copy.58
  19.6 0.0 copy-done.3
  19.6 0.1 copy.57
  19.8 0.1 lt.78
  19.9 0.1 copy.59
  20.0 0.1 min.34
  20.1 0.1 squeeze.23
  20.2 0.5 select_reduce_fusion
  20.7 0.1 reduce_sum.53
  20.8 0.1 copy.60
  20.9 0.1 reshape.385
  21.0 0.5 select_reduce_fusion.1
  21.5 0.1 mul.113
  21.6 0.6 fusion.6
  22.2 0.1 broadcast_in_dim.95
  22.3 0.0 copy-done
  22.4 6.0 %gather_fusion = bf16[1024,2048]{1,0:T(8,128)(2,1)} fusion(bf16[128,2048]{1,0:T(8,128)(2,1)S(1)} %bitcast.49, s32[1024]{0:T(1024)S(1)} %broadcast_clamp_fusion.1), kind=kCustom, calls=%fused_computation | custom fusion | bytes 8392704 | tf_op jit(solution)/shard_map/jit(_take)/gather | solution.py:40
  28.4 4.5 %multiply_convert_fusion = bf16[2,32,16,2048]{3,2,0,1:T(8,128)(2,1)} fusion(bf16[2,32,16,2048]{3,2,1,0:T(8,128)(2,1)} %bitcast.51, f32[2,32,16]{2,0,1:T(2,128)S(1)} %copy.61, pred[2,32,16]{2,0,1:T(4,128)(4,1)S(1)} %copy.63, pred[2,32,16]{2,0,1:T(4,128)(4,1)S(1)} %copy.62), kind=kLoop, calls=%fused_computation.4 | loop fusion | flops 10485760 | bytes 8394752 | tf_op jit(solution)/shard_map/convert_element_type | solution.py:52
  32.9 81.9 %all-to-all-done.1 = bf16[2,32,16,2048]{3,2,0,1:T(8,128)(2,1)} async-done(((bf16[2,32,16,2048]{3,2,0,1:T(8,128)(2,1)}), bf16[2,32,16,2048]{3,2,0,1:T(8,128)(2,1)}, u32[]{:S(2)}, u32[]{:S(2)}) %all-to-all-start.1) | async-done | bytes 4194336 | tf_op jit(solution)/shard_map/all_to_all | solution.py:61
  114.8 4.9 %all-to-all-start = ((bf16[2,32,16,2048]{3,2,0,1:T(8,128)(2,1)}), bf16[2,32,16,2048]{3,2,0,1:T(8,128)(2,1)}, u32[]{:S(2)}, u32[]{:S(2)}) async-start(bf16[2,32,16,2048]{3,2,0,1:T(8,128)(2,1)} %multiply_convert_fusion), calls=%async_computation | async-start | bytes 8388608 | tf_op jit(solution)/shard_map/all_to_all | solution.py:53
  119.6 0.1 lt.85
  119.7 0.1 min.36
  119.8 0.1 squeeze.28
  119.9 0.1 copy.66
  120.0 0.1 copy.67
  120.2 0.1 broadcast_in_dim.103
  120.3 126.0 %all-gather = bf16[1,64,2048]{2,0,1:T(2,128)(2,1)S(1)} all-gather(bf16[1,2,2048]{2,0,1:T(2,128)(2,1)S(1)} %copy.74), channel_id=2, replica_groups=mesh['pipe'=8,'expert'=32] {'expert'}, dimensions={1}, use_global_device_ids=true | all-gather | bytes 270336 | tf_op jit(solution)/shard_map/all_gather | solution.py:90
  246.4 0.1 bitcast_convert_fusion
  246.5 4.7 %copy.69 = bf16[2,32,16,2048]{3,2,1,0:T(8,128)(2,1)} copy(bf16[2,32,16,2048]{3,2,0,1:T(8,128)(2,1)} %all-to-all-done.1) | data formatting | bytes 8388608 | tf_op jit(solution)/shard_map/all_to_all | solution.py:61
  251.2 11.6 %gather_fusion.1 = bf16[1024,2048]{1,0:T(8,128)(2,1)} fusion(bf16[1024,2048]{1,0:T(8,128)(2,1)} %bitcast.50, s32[1024]{0:T(1024)S(1)} %broadcast_clamp_fusion), kind=kCustom, calls=%fused_computation.1 | custom fusion | bytes 8392704 | tf_op jit(solution)/shard_map/jit(_take)/gather | solution.py:68
  262.8 3.2 %fusion = f32[1024]{0:T(1024)S(1)} fusion(f32[128,2048]{1,0:T(8,128)S(1)} %bitcast_convert_fusion, bf16[1024,2048]{1,0:T(8,128)(2,1)} %gather_fusion.1, pred[1024]{0:T(1024)(128)(4,1)S(1)} %broadcast_in_dim.103), kind=kLoop, calls=%fused_computation.3 | loop fusion | flops 8387584 | bytes 5248000 | tf_op jit(solution)/shard_map/reduce_sum | solution.py:71
  266.0 0.1 reduce_sum.56
  266.1 0.1 fusion.25
  266.2 0.1 bitcast_multiply_fusion.1
  266.4 0.1 select_reduce_fusion.2
  266.5 0.3 fusion.18
  266.8 1.1 collective-permute-start
  267.9 0.0 all-to-all-done
  267.9 2.7 copy.65
  270.6 0.5 copy-done.5
  271.0 7.3 %fusion.21 = (bf16[1,2,512,768]{3,2,1,0:T(8,128)(2,1)S(1)}, bf16[1,2,512,768]{3,2,1,0:T(8,128)(2,1)S(1)}) fusion(bf16[2,512,1536]{2,1,0:T(8,128)(2,1)S(1)} %bitcast.60, bf16[2,512,2048]{2,1,0:T(8,128)(2,1)S(1)} %bitcast.52, bf16[1,2,768,2048]{3,2,1,0:T(8,128)(2,1)} %param.12), kind=kOutput, calls=%fused_computation.34 | convolution fusion | flops 3233021952 | bytes 16777216 | tf_op jit(solution)/shard_map/jsd,jfd->jsf/dot_general | solution.py:76
  278.3 1.9 pad_maximum_fusion
  280.2 17.2 %collective-permute-done = bf16[128,2048]{1,0:T(8,128)(2,1)S(1)} collective-permute-done((bf16[128,2048]{1,0:T(8,128)(2,1)S(1)}, bf16[128,2048]{1,0:T(8,128)(2,1)S(1)}, u32[]{:S(2)}, u32[]{:S(2)}) %collective-permute-start) | collective-permute-done | bytes 524320 | tf_op jit(solution)/shard_map/ppermute | solution.py:9
  297.4 0.8 copy.86
  (22 shorter events, 0.3 us)
Async XLA Ops:
  10.3 9.2 %copy-start.1 = (s32[1,128,8]{1,2,0:T(8,128)S(1)}, s32[1,128,8]{1,2,0:T(8,128)}, u32[]{:S(2)}) copy-start(s32[1,128,8]{1,2,0:T(8,128)} %param.8) | copy-start | bytes 12292
  10.3 9.3 %copy-start.3 = (s32[1,128,8]{1,2,0:T(8,128)S(1)}, s32[1,128,8]{1,2,0:T(8,128)}, u32[]{:S(2)}) copy-start(s32[1,128,8]{1,2,0:T(8,128)} %param.9) | copy-start | bytes 12292
  10.3 10.5 %copy-start.2 = (f32[1,128,8]{1,2,0:T(8,128)S(1)}, f32[1,128,8]{1,2,0:T(8,128)}, u32[]{:S(2)}) copy-start(f32[1,128,8]{1,2,0:T(8,128)} %param.10) | copy-start | bytes 12292
  10.3 12.0 %copy-start = (bf16[1,128,2048]{2,1,0:T(8,128)(2,1)S(1)}, bf16[1,128,2048]{2,1,0:T(8,128)(2,1)}, u32[]{:S(2)}) copy-start(bf16[1,128,2048]{2,1,0:T(8,128)(2,1)} %param.7) | copy-start | bytes 1572868
  10.3 104.5 %all-to-all-start.1 = ((bf16[2,32,16,2048]{3,2,0,1:T(8,128)(2,1)}), bf16[2,32,16,2048]{3,2,0,1:T(8,128)(2,1)}, u32[]{:S(2)}, u32[]{:S(2)}) async-start(bf16[2,32,16,2048]{3,2,0,1:T(8,128)(2,1)} %copy.68), calls=%async_computation.1 | async-start | bytes 8388608 | tf_op jit(solution)/shard_map/all_to_all | solution.py:61
  32.9 87.4 %copy-start.4 = (bf16[1,2,2048]{2,1,0:T(2,128)(2,1)S(1)}, bf16[1,2,2048]{2,1,0:T(2,128)(2,1)}, u32[]{:S(2)}) copy-start(bf16[1,2,2048]{2,1,0:T(2,128)(2,1)} %param.13) | copy-start | bytes 24580
  114.8 153.1 %all-to-all-start = ((bf16[2,32,16,2048]{3,2,0,1:T(8,128)(2,1)}), bf16[2,32,16,2048]{3,2,0,1:T(8,128)(2,1)}, u32[]{:S(2)}, u32[]{:S(2)}) async-start(bf16[2,32,16,2048]{3,2,0,1:T(8,128)(2,1)} %multiply_convert_fusion), calls=%async_computation | async-start | bytes 8388608 | tf_op jit(solution)/shard_map/all_to_all | solution.py:53
  266.8 30.6 %collective-permute-start = (bf16[128,2048]{1,0:T(8,128)(2,1)S(1)}, bf16[128,2048]{1,0:T(8,128)(2,1)S(1)}, u32[]{:S(2)}, u32[]{:S(2)}) collective-permute-start(bf16[128,2048]{1,0:T(8,128)(2,1)S(1)} %fusion.18), channel_id=1, source_target_pairs={{0,224},{32,0},{64,32},{96,64},{128,96},{160,128},{192,160},{224,1... | collective-permute-start | bytes 1572872 | tf_op jit(solution)/shard_map/ppermute | solution.py:9
  267.9 3.2 %copy-start.5 = (bf16[1,2,512,1536]{3,2,1,0:T(8,128)(2,1)S(1)}, bf16[1,2,512,1536]{3,2,1,0:T(8,128)(2,1)}, u32[]{:S(2)}) copy-start(bf16[1,2,512,1536]{3,2,1,0:T(8,128)(2,1)} %param.11) | copy-start | bytes 9437188
where the time goes:
time: 299 us; the launch traced here: 298 us
  blocking collectives  126 us (42%)
  waiting for transfers between devices  99.1 us (33%)
  local copies, waits for them, and re-layouts  30.4 us (10%)
  starting transfers between devices  15.1 us (5%)
  matrix products  15 us (5%)
  other arithmetic  11.7 us (4%)
    all_gather x1, blocking collectives, per_device(): lax.all_gather(router_weight[0], 'expert', axis=0, tiled=True)  126 us
    all_to_all x1, waiting for transfers between devices, per_device(): lax.all_to_all(expert_out.reshape(local_experts, groups, capacity, -1), '...  81.9 us
    ppermute x1, waiting for transfers between devices, passed_along(): lax.ppermute(value, axis, [(i, (i + by) % peers) for i in range(peers)])  17.2 us
    gather x1, local copies, waits for them, and re-layouts, per_device(): jnp.take(returned.reshape(total_rows, -1), pair_dest, axis=0, mode='fill'...  11.6 us
    all_to_all x1, starting transfers between devices, per_device(): lax.all_to_all(expert_out.reshape(local_experts, groups, capacity, -1), '...  9.19 us
    dot_general x1, matrix products, per_device(): jnp.einsum('jsf,jfd->jsd', hidden, weights, preferred_element_type=jnp.fl...  7.38 us
    dot_general x1, matrix products, per_device(): jnp.einsum('jsd,jfd->jsf', scaled_rows, weights, preferred_element_type=j...  7.27 us
    gather x1, local copies, waits for them, and re-layouts, per_device(): token_rows = jnp.take(features, slot_token, axis=0)  6.02 us
  transfers between devices with their start and end apart: 3, of which 2 were waited for; matrix products, arithmetic and copies ran while one was open for 15% of the time, Pallas kernels for 0%

commit v1 on v0

--- a/solution.py
+++ b/solution.py
@@ -14,6 +14,7 @@
     local_experts = down_weight.shape[1]
     hidden_width = down_weight.shape[2]
     tok_rows = grad_out.shape[1]
+    width = grad_out.shape[2]
     top_count = expert_ids.shape[2]
     expert_total = local_experts * groups
     capacity = tok_rows * top_count // expert_total
@@ -39,6 +40,36 @@
     )
     token_rows = jnp.take(features, slot_token, axis=0)
     token_rows = jnp.where(occupied[:, None], token_rows, jnp.zeros_like(token_rows))
+
+    gate_out = (
+        slot_gate.reshape(local_experts, groups, capacity)
+        .transpose(1, 0, 2)
+        .reshape(groups, local_experts * capacity)
+        .astype(jnp.bfloat16)
+    )
+    router_out = jnp.broadcast_to(
+        router_weight[0].reshape(1, local_experts * width), (groups, local_experts * width)
+    )
+    small = jnp.concatenate([gate_out, router_out], axis=1)
+    small_in = lax.all_to_all(small, "expert", split_axis=0, concat_axis=0, tiled=True)
+    gate_in = (
+        small_in[:, : local_experts * capacity]
+        .reshape(groups, local_experts, capacity)
+        .transpose(1, 0, 2)
+        .reshape(local_experts, groups * capacity)
+        .astype(jnp.float32)
+    )
+    router_full = small_in[:, local_experts * capacity :].reshape(expert_total, width)
+
+    arrived = lax.all_to_all(
+        token_rows.reshape(local_experts, groups, capacity, -1),
+        "expert",
+        split_axis=1,
+        concat_axis=1,
+        tiled=True,
+    )
+    rows_in = arrived.reshape(local_experts, groups * capacity, -1).astype(jnp.float32)
+
     pre_saved = saved_pre[0]
     gate_part = pre_saved[..., :hidden_width].astype(jnp.float32)
     up_part = pre_saved[..., hidden_width:].astype(jnp.float32)
@@ -49,34 +80,24 @@
     expert_out = jnp.einsum(
         "jsf,jfd->jsd", hidden, weights, preferred_element_type=jnp.float32
     ).astype(jnp.bfloat16)
-    scaled = (slot_gate[:, None] * token_rows.astype(jnp.float32)).astype(jnp.bfloat16)
-    arrived = lax.all_to_all(
-        scaled.reshape(local_experts, groups, capacity, -1),
+    row_scores = jnp.sum(rows_in * lax.optimization_barrier(expert_out).astype(jnp.float32), axis=-1)
+    returned = lax.all_to_all(
+        row_scores.reshape(local_experts, groups, capacity),
         "expert",
         split_axis=1,
         concat_axis=1,
         tiled=True,
     )
-    scaled_rows = arrived.reshape(local_experts, groups * capacity, -1)
-    returned = lax.all_to_all(
-        expert_out.reshape(local_experts, groups, capacity, -1),
-        "expert",
-        split_axis=1,
-        concat_axis=1,
-        tiled=True,
-    )
-    pair_out = jnp.take(
-        returned.reshape(total_rows, -1), pair_dest, axis=0, mode="fill", fill_value=0
-    )
-    pair_scores = jnp.sum(
-        pair_out.reshape(tok_rows, top_count, -1).astype(jnp.float32)
-        * features.astype(jnp.float32)[:, None, :],
-        axis=-1,
-    )
+    pair_scores = jnp.take(
+        returned.reshape(total_rows), pair_dest, axis=0, mode="fill", fill_value=0
+    ).reshape(tok_rows, top_count)
+
+    scaled_rows = (gate_in[..., None] * rows_in).astype(jnp.bfloat16)
     row_grad = jnp.einsum("jsd,jfd->jsf", scaled_rows, weights, preferred_element_type=jnp.float32)
     gate_grad = row_grad * up_part * sigmoid_gate * (1.0 + gate_part * (1.0 - sigmoid_gate))
     up_grad = row_grad * silu_gate
     pre_grad = jnp.concatenate([gate_grad, up_grad], axis=-1).astype(jnp.bfloat16)
+
     gate_values = gate_weights[0]
     weighted_sum = jnp.sum(gate_values * pair_scores, axis=-1, keepdims=True)
     select_grad = gate_values * (pair_scores - weighted_sum)
@@ -85,11 +106,7 @@
     logit_grad = jnp.sum(
         jnp.where(chosen, select_grad[:, :, None], jnp.float32(0.0)), axis=1
     ).astype(jnp.bfloat16)
-    router_part = jnp.dot(
-        logit_grad,
-        lax.all_gather(router_weight[0], "expert", axis=0, tiled=True),
-        preferred_element_type=jnp.float32,
-    )
+    router_part = jnp.dot(logit_grad, router_full, preferred_element_type=jnp.float32)
     section_grad = (features.astype(jnp.float32) + router_part).astype(jnp.bfloat16)
     outgoing = passed_along(section_grad, "pipe", -1)
     return (pre_grad[None], outgoing[None])

time: 299 us -> 188 us (0.63)
  blocking collectives: 126 us -> 0 us
  waiting for transfers between devices: 99.1 us -> 110 us
  local copies, waits for them, and re-layouts: 30.4 us -> 23.5 us
  starting transfers between devices: 15.1 us -> 21.6 us
  matrix products: 15 us -> 19 us
    all_gather x1 -> x0, blocking collectives: 126 us -> none  [per_device(): lax.all_gather(router_weight[0], 'expert', axis=0, tiled=True)]
    all_to_all x2 -> x3, waiting for transfers between devices: 81.9 us -> 90.8 us  [the longest x1 83.5 us: per_device(): lax.all_to_all(token_rows.reshape(local_experts, groups, capacity, -1), '...]
    gather x1 -> x2, local copies, waits for them, and re-layouts: 11.6 us -> 4.6 us  [per_device(): jnp.take(returned.reshape(total_rows), pair_dest, axis=0, mode='fill', fi...]
    all_to_all x2 -> x3, starting transfers between devices: 14 us -> 20.5 us  [the longest x1 8.92 us: per_device(): lax.all_to_all(small, 'expert', split_axis=0, concat_axis=0, tiled=True)]
    all_to_all x2 -> x3, local copies, waits for them, and re-layouts: 7.39 us -> 2.09 us  [the longest x2 2.08 us: per_device(): lax.all_to_all(small, 'expert', split_axis=0, concat_axis=0, tiled=True)]
    convert_element_type x2 -> x1, other arithmetic: 4.63 us -> 0.01 us  [per_device(): gate_in = small_in[:, :local_experts * capacity].reshape(groups, local_ex...]
    select_n x1 -> x2, other arithmetic: 0.05 us -> 3.89 us  [the longest x1 3.85 us: per_device(): jnp.where(occupied[:, None], token_rows, jnp.zeros_like(token_rows))]
    convert_element_type x0 -> x6, local copies, waits for them, and re-layouts: none -> 3.83 us  [the longest x1 3.41 us: per_device(): arrived.reshape(local_experts, groups * capacity, -1).astype(jnp.float32)]
  transfers between devices with their start and end apart: 3 -> 4, of which waited for: 2 -> 4; matrix products, arithmetic and copies ran while one was open for 15% -> 19% of each run, Pallas kernels for 0% -> 0%
where the time goes in v1:
time: 188 us; the launch traced here: 187 us
  waiting for transfers between devices  110 us (59%)
  local copies, waits for them, and re-layouts  23.5 us (12%)
  starting transfers between devices  21.6 us (11%)
  matrix products  19 us (10%)
  other arithmetic  12.6 us (7%)
    all_to_all x1, waiting for transfers between devices, per_device(): lax.all_to_all(token_rows.reshape(local_experts, groups, capacity, -1), '...  83.5 us
    ppermute x1, waiting for transfers between devices, passed_along(): lax.ppermute(value, axis, [(i, (i + by) % peers) for i in range(peers)])  19.2 us
    dot_general x1, matrix products, per_device(): jnp.einsum('jsf,jfd->jsd', hidden, weights, preferred_element_type=jnp.fl...  9.35 us
    dot_general x1, matrix products, per_device(): jnp.einsum('jsd,jfd->jsf', scaled_rows, weights, preferred_element_type=j...  9.31 us
    all_to_all x1, starting transfers between devices, per_device(): lax.all_to_all(small, 'expert', split_axis=0, concat_axis=0, tiled=True)  8.92 us
    all_to_all x1, starting transfers between devices, per_device(): lax.all_to_all(token_rows.reshape(local_experts, groups, capacity, -1), '...  7.69 us
    all_to_all x1, waiting for transfers between devices, per_device(): lax.all_to_all(row_scores.reshape(local_experts, groups, capacity), 'expe...  7.18 us
    gather x1, local copies, waits for them, and re-layouts, per_device(): token_rows = jnp.take(features, slot_token, axis=0)  6.03 us
  transfers between devices with their start and end apart: 4, of which 4 were waited for; matrix products, arithmetic and copies ran while one was open for 19% of the time, Pallas kernels for 0%

profile of v1, /device:TPU:6, one launch (start us, length us, event | category | flops | bytes accessed | tf_op | source)
XLA Modules:
  0.0 187.4 jit_solution(10418243624030112869)
XLA Ops:
  0.6 0.8 copy.67
  1.5 0.7 convert_convert_fusion
  2.2 0.7 copy.89
  2.9 0.1 copy.70
  3.0 0.1 reshape.445
  3.1 0.1 lt.82
  3.2 0.8 copy.68
  4.0 0.1 squeeze.20
  4.1 0.1 min.36
  4.2 0.5 select_reduce_fusion.1
  4.8 0.1 copy.71
  4.9 0.1 copy.72
  5.0 0.1 pad.3.clone
  5.1 0.5 broadcast.496
  5.6 0.7 reduce
  6.3 0.9 reshape.466
  7.2 8.9 %all-to-all-start = ((bf16[32,2,2064]{2,1,0:T(2,128)(2,1)}), bf16[32,2,2064]{2,1,0:T(2,128)(2,1)S(1)}, u32[]{:S(2)}, u32[]{:S(2)}) async-start(bf16[32,2,2064]{2,1,0:T(2,128)(2,1)} %reshape.466), calls=%async_computation | async-start | bytes 557056 | tf_op jit(solution)/shard_map/all_to_all | solution.py:54
  16.2 0.6 fusion.7
  16.7 0.5 select_reduce_fusion
  17.5 6.0 %gather_fusion = bf16[1024,2048]{1,0:T(8,128)(2,1)} fusion(bf16[128,2048]{1,0:T(8,128)(2,1)S(1)} %bitcast.81, s32[1024]{0:T(1024)S(1)} %broadcast_clamp_fusion.1), kind=kCustom, calls=%fused_computation | custom fusion | bytes 8392704 | tf_op jit(solution)/shard_map/jit(_take)/gather | solution.py:41
  23.5 3.8 %fusion.6 = bf16[2,32,16,2048]{3,2,0,1:T(8,128)(2,1)} fusion(bf16[2,32,16,2048]{3,2,1,0:T(8,128)(2,1)} %bitcast.82, pred[2,32,16]{2,0,1:T(4,128)(4,1)S(1)} %copy.77, pred[2,32,16]{2,0,1:T(4,128)(4,1)S(1)} %copy.76), kind=kLoop, calls=%fused_computation.14 | loop fusion | flops 4194304 | bytes 8390656 | tf_op jit(solution)/shard_map/jit(_where)/select_n | solution.py:42
  27.4 0.1 all-to-all-done
  27.5 7.7 %all-to-all-start.1 = ((bf16[2,32,16,2048]{3,2,0,1:T(8,128)(2,1)}), bf16[2,32,16,2048]{3,2,0,1:T(8,128)(2,1)}, u32[]{:S(2)}, u32[]{:S(2)}) async-start(bf16[2,32,16,2048]{3,2,0,1:T(8,128)(2,1)} %fusion.6), calls=%async_computation.1 | async-start | bytes 8388608 | tf_op jit(solution)/shard_map/all_to_all | solution.py:64
  35.2 0.1 lt.89
  35.3 0.1 squeeze.25
  35.4 0.1 min.38
  35.5 9.3 %fusion.8 = bf16[2,512,2048]{2,1,0:T(8,128)(2,1)} fusion(bf16[1,2,768,2048]{3,2,1,0:T(8,128)(2,1)} %param.12, bf16[2,512,1536]{2,1,0:T(8,128)(2,1)} %bitcast.95), kind=kOutput, calls=%fused_computation.21 | convolution fusion | flops 3229614080 | bytes 13631488 | tf_op jit(solution)/shard_map/jsf,jfd->jsd/dot_general | solution.py:80
  44.9 0.3 reshape.467
  45.2 1.6 copy.74
  46.9 0.1 reshape.446
  47.0 83.5 %all-to-all-done.1 = bf16[2,32,16,2048]{3,2,0,1:T(8,128)(2,1)} async-done(((bf16[2,32,16,2048]{3,2,0,1:T(8,128)(2,1)}), bf16[2,32,16,2048]{3,2,0,1:T(8,128)(2,1)}, u32[]{:S(2)}, u32[]{:S(2)}) %all-to-all-start.1) | async-done | bytes 4194336 | tf_op jit(solution)/shard_map/all_to_all | solution.py:64
  130.5 3.4 %copy.79 = f32[2,32,16,2048]{3,2,1,0:T(8,128)S(1)} copy(bf16[2,32,16,2048]{3,2,0,1:T(8,128)(2,1)} %all-to-all-done.1) | data formatting | bytes 12582912 | tf_op jit(solution)/shard_map/convert_element_type | solution.py:71
  133.9 3.4 %fusion.1 = (f32[2,512]{1,0:T(2,128)S(1)}, bf16[2,512,2048]{2,1,0:T(8,128)(2,1)}) fusion(f32[2,32,16,2048]{3,2,1,0:T(8,128)S(1)} %copy.79, bf16[2,512,2048]{2,1,0:T(8,128)(2,1)S(1)} %copy-done.1, f32[2,512]{1,0:T(2,128)S(1)} %reshape.446), kind=kLoop, calls=%fused_computation.5 | loop fusion | flops 10484736 | bytes 16785408 | tf_op jit(solution)/shard_map/reduce_sum | solution.py:83
  137.4 0.6 copy.83
  138.1 3.9 %all-to-all-start.2 = ((f32[2,32,16]{2,0,1:T(2,128)}), f32[2,32,16]{2,0,1:T(2,128)S(1)}, u32[]{:S(2)}, u32[]{:S(2)}) async-start(f32[2,32,16]{2,0,1:T(2,128)} %copy.83), calls=%async_computation.2 | async-start | bytes 65536 | tf_op jit(solution)/shard_map/all_to_all | solution.py:84
  142.0 0.1 copy.82
  142.2 0.3 copy.87
  142.5 0.1 reshape.444
  142.6 7.2 %all-to-all-done.2 = f32[2,32,16]{2,0,1:T(2,128)S(1)} async-done(((f32[2,32,16]{2,0,1:T(2,128)}), f32[2,32,16]{2,0,1:T(2,128)S(1)}, u32[]{:S(2)}, u32[]{:S(2)}) %all-to-all-start.2) | async-done | bytes 4128 | tf_op jit(solution)/shard_map/all_to_all | solution.py:84
  149.9 4.5 %gather_fusion.1 = f32[1024]{0:T(1024)S(1)} fusion(f32[1024]{0:T(1024)S(1)} %reshape.443, s32[1024]{0:T(1024)S(1)} %broadcast_clamp_fusion), kind=kCustom, calls=%fused_computation.1 | custom fusion | bytes 12288 | tf_op jit(solution)/shard_map/jit(_take)/gather | solution.py:91
  154.5 0.2 fusion.29
  154.7 0.1 bitcast_multiply_fusion.2
  154.9 0.3 fusion.19
  155.2 1.1 collective-permute-start
  156.3 9.3 %fusion.22 = (bf16[1,2,512,768]{3,2,1,0:T(8,128)(2,1)S(1)}, bf16[1,2,512,768]{3,2,1,0:T(8,128)(2,1)S(1)}) fusion(bf16[2,512,1536]{2,1,0:T(8,128)(2,1)} %bitcast.96, bf16[2,512,2048]{2,1,0:T(8,128)(2,1)} %get-tuple-element.5, bf16[1,2,768,2048]{3,2,1,0:T(8,128)(2,1)} %param.12), kind=kOutput, calls=%fused_computation.35 | convolution fusion | flops 3233021952 | bytes 16777216 | tf_op jit(solution)/shard_map/jsd,jfd->jsf/dot_general | solution.py:96
  165.6 1.9 %pad_maximum_fusion = bf16[1,2,512,1536]{3,2,1,0:T(8,128)(2,1)} fusion(bf16[1,2,512,768]{3,2,1,0:T(8,128)(2,1)S(1)} %get-tuple-element.7, bf16[1,2,512,768]{3,2,1,0:T(8,128)(2,1)S(1)} %get-tuple-element.6), kind=kLoop, calls=%fused_computation.30 | loop fusion | flops 6291456 | bytes 6291456 | tf_op jit(solution)/shard_map/concatenate | solution.py:99
  167.5 19.2 %collective-permute-done = bf16[128,2048]{1,0:T(8,128)(2,1)S(1)} collective-permute-done((bf16[128,2048]{1,0:T(8,128)(2,1)S(1)}, bf16[128,2048]{1,0:T(8,128)(2,1)S(1)}, u32[]{:S(2)}, u32[]{:S(2)}) %collective-permute-start) | collective-permute-done | bytes 524320 | tf_op jit(solution)/shard_map/ppermute | solution.py:9
  186.7 0.8 copy.95
  (32 shorter events, 1.0 us)
Async XLA Ops:
  0.6 16.9 %copy-start = (bf16[1,128,2048]{2,1,0:T(8,128)(2,1)S(1)}, bf16[1,128,2048]{2,1,0:T(8,128)(2,1)}, u32[]{:S(2)}) copy-start(bf16[1,128,2048]{2,1,0:T(8,128)(2,1)} %param.7) | copy-start | bytes 1572868
  7.2 20.3 %all-to-all-start = ((bf16[32,2,2064]{2,1,0:T(2,128)(2,1)}), bf16[32,2,2064]{2,1,0:T(2,128)(2,1)S(1)}, u32[]{:S(2)}, u32[]{:S(2)}) async-start(bf16[32,2,2064]{2,1,0:T(2,128)(2,1)} %reshape.466), calls=%async_computation | async-start | bytes 557056 | tf_op jit(solution)/shard_map/all_to_all | solution.py:54
  27.5 103.0 %all-to-all-start.1 = ((bf16[2,32,16,2048]{3,2,0,1:T(8,128)(2,1)}), bf16[2,32,16,2048]{3,2,0,1:T(8,128)(2,1)}, u32[]{:S(2)}, u32[]{:S(2)}) async-start(bf16[2,32,16,2048]{3,2,0,1:T(8,128)(2,1)} %fusion.6), calls=%async_computation.1 | async-start | bytes 8388608 | tf_op jit(solution)/shard_map/all_to_all | solution.py:64
  130.5 3.4 %copy-start.1 = (bf16[2,512,2048]{2,1,0:T(8,128)(2,1)S(1)}, bf16[2,512,2048]{2,1,0:T(8,128)(2,1)}, u32[]{:S(2)}) copy-start(bf16[2,512,2048]{2,1,0:T(8,128)(2,1)} %fusion.8) | copy-start | bytes 12582916
  133.9 8.0 %copy-start.2 = (f32[1,128,8]{1,2,0:T(8,128)S(1)}, f32[1,128,8]{1,2,0:T(8,128)}, u32[]{:S(2)}) copy-start(f32[1,128,8]{1,2,0:T(8,128)} %param.10) | copy-start | bytes 12292
  138.1 11.7 %all-to-all-start.2 = ((f32[2,32,16]{2,0,1:T(2,128)}), f32[2,32,16]{2,0,1:T(2,128)S(1)}, u32[]{:S(2)}, u32[]{:S(2)}) async-start(f32[2,32,16]{2,0,1:T(2,128)} %copy.83), calls=%async_computation.2 | async-start | bytes 65536 | tf_op jit(solution)/shard_map/all_to_all | solution.py:84
  142.1 12.7 %copy-start.3 = (s32[1,128,8]{1,2,0:T(8,128)S(1)}, s32[1,128,8]{1,2,0:T(8,128)}, u32[]{:S(2)}) copy-start(s32[1,128,8]{1,2,0:T(8,128)} %param.8) | copy-start | bytes 12292
  155.2 31.5 %collective-permute-start = (bf16[128,2048]{1,0:T(8,128)(2,1)S(1)}, bf16[128,2048]{1,0:T(8,128)(2,1)S(1)}, u32[]{:S(2)}, u32[]{:S(2)}) collective-permute-start(bf16[128,2048]{1,0:T(8,128)(2,1)S(1)} %fusion.19), channel_id=1, source_target_pairs={{0,224},{32,0},{64,32},{96,64},{128,96},{160,128},{192,160},{224,1... | collective-permute-start | bytes 1572872 | tf_op jit(solution)/shard_map/ppermute | solution.py:9

commit v2 on v1

--- a/solution.py
+++ b/solution.py
@@ -20,6 +20,10 @@
     capacity = tok_rows * top_count // expert_total
     total_rows = expert_total * capacity
     features = grad_out[0]
+
+    next_features = passed_along(features, "pipe", -1)
+    next_router = passed_along(router_weight[0], "pipe", -1)
+
     route_ids = expert_ids[0]
     kept_pairs = slot_ids[0] < capacity
     destination = (
@@ -27,39 +31,17 @@
         + route_ids // local_experts * capacity
         + jnp.minimum(slot_ids[0], capacity - 1)
     )
-    pair_dest = jnp.where(kept_pairs, destination, total_rows).reshape(-1)
+    pair_dest = jnp.where(kept_pairs, destination, total_rows)
     row_ids = jnp.arange(total_rows, dtype=jnp.int32)
-    matches = pair_dest[None, :] == row_ids[:, None]
-    pair_token = jnp.arange(tok_rows * top_count, dtype=jnp.int32) // top_count
-    slot_token = jnp.sum(jnp.where(matches, pair_token[None, :], 0), axis=1)
-    occupied = jnp.any(matches, axis=1)
+    token_hit = pair_dest[None, :, :] == row_ids[:, None, None]
+    token_onehot = jnp.any(token_hit, axis=2).astype(jnp.bfloat16)
+    token_rows = jnp.dot(token_onehot, features, preferred_element_type=jnp.float32).astype(jnp.bfloat16)
+    matches = token_hit.reshape(total_rows, tok_rows * top_count)
     gate_low = gate_weights[0].astype(jnp.bfloat16)
     slot_gate = jnp.sum(
         jnp.where(matches, gate_low.reshape(-1).astype(jnp.float32)[None, :], jnp.float32(0.0)),
         axis=1,
     )
-    token_rows = jnp.take(features, slot_token, axis=0)
-    token_rows = jnp.where(occupied[:, None], token_rows, jnp.zeros_like(token_rows))
-
-    gate_out = (
-        slot_gate.reshape(local_experts, groups, capacity)
-        .transpose(1, 0, 2)
-        .reshape(groups, local_experts * capacity)
-        .astype(jnp.bfloat16)
-    )
-    router_out = jnp.broadcast_to(
-        router_weight[0].reshape(1, local_experts * width), (groups, local_experts * width)
-    )
-    small = jnp.concatenate([gate_out, router_out], axis=1)
-    small_in = lax.all_to_all(small, "expert", split_axis=0, concat_axis=0, tiled=True)
-    gate_in = (
-        small_in[:, : local_experts * capacity]
-        .reshape(groups, local_experts, capacity)
-        .transpose(1, 0, 2)
-        .reshape(local_experts, groups * capacity)
-        .astype(jnp.float32)
-    )
-    router_full = small_in[:, local_experts * capacity :].reshape(expert_total, width)
 
     arrived = lax.all_to_all(
         token_rows.reshape(local_experts, groups, capacity, -1),
@@ -68,6 +50,28 @@
         concat_axis=1,
         tiled=True,
     )
+
+    me = lax.axis_index("expert")
+    gate_table = (
+        slot_gate.reshape(local_experts, groups, capacity)
+        .transpose(1, 0, 2)
+        .reshape(1, total_rows)
+        .astype(jnp.bfloat16)
+    )
+    own_block = jnp.concatenate([gate_table, next_router.reshape(1, local_experts * width)], axis=1)
+    blocks = lax.dynamic_update_slice(
+        jnp.zeros((groups, own_block.shape[1]), jnp.bfloat16), own_block, (me, 0)
+    )
+    gathered = lax.psum(blocks, "expert")
+    gate_in = (
+        lax.dynamic_slice_in_dim(gathered[:, :total_rows], me * local_experts * capacity, local_experts * capacity, axis=1)
+        .reshape(groups, local_experts, capacity)
+        .transpose(1, 0, 2)
+        .reshape(local_experts, groups * capacity)
+        .astype(jnp.float32)
+    )
+    next_router_full = gathered[:, total_rows:].reshape(expert_total, width)
+
     rows_in = arrived.reshape(local_experts, groups * capacity, -1).astype(jnp.float32)
 
     pre_saved = saved_pre[0]
@@ -88,8 +92,8 @@
         concat_axis=1,
         tiled=True,
     )
-    pair_scores = jnp.take(
-        returned.reshape(total_rows), pair_dest, axis=0, mode="fill", fill_value=0
+    pair_scores = jnp.sum(
+        jnp.where(matches, returned.reshape(total_rows)[:, None], jnp.float32(0.0)), axis=0
     ).reshape(tok_rows, top_count)
 
     scaled_rows = (gate_in[..., None] * rows_in).astype(jnp.bfloat16)
@@ -106,9 +110,9 @@
     logit_grad = jnp.sum(
         jnp.where(chosen, select_grad[:, :, None], jnp.float32(0.0)), axis=1
     ).astype(jnp.bfloat16)
-    router_part = jnp.dot(logit_grad, router_full, preferred_element_type=jnp.float32)
-    section_grad = (features.astype(jnp.float32) + router_part).astype(jnp.bfloat16)
-    outgoing = passed_along(section_grad, "pipe", -1)
+    next_logit_grad = passed_along(logit_grad, "pipe", -1)
+    router_part = jnp.dot(next_logit_grad, next_router_full, preferred_element_type=jnp.float32)
+    outgoing = (next_features.astype(jnp.float32) + router_part).astype(jnp.bfloat16)
     return (pre_grad[None], outgoing[None])
 
 

time: 188 us -> 472 us (2.51)
  waiting for transfers between devices: 110 us -> 392 us
  between operations: 0.88 us -> 14.3 us
  local copies, waits for them, and re-layouts: 23.5 us -> 16.8 us
  starting transfers between devices: 21.6 us -> 15.6 us
    psum x0 -> x1, waiting for transfers between devices: none -> 300 us  [per_device(): gathered = lax.psum(blocks, 'expert')]
    ppermute x1 -> x3, waiting for transfers between devices: 19.2 us -> 0.01 us  [passed_along(): lax.ppermute(value, axis, [(i, (i + by) % peers) for i in range(peers)])]
    gather x3 -> x0, local copies, waits for them, and re-layouts: 10.6 us -> none  [the longest x1 6.03 us: per_device(): token_rows = jnp.take(features, slot_token, axis=0)]
    all_to_all x1 -> x0, starting transfers between devices: 8.92 us -> none  [per_device(): lax.all_to_all(small, 'expert', split_axis=0, concat_axis=0, tiled=True)]
  transfers between devices with their start and end apart: 4 -> 6, of which waited for: 4 -> 3; matrix products, arithmetic and copies ran while one was open for 19% -> 7% of each run, Pallas kernels for 0% -> 0%
where the time goes in v2:
time: 472 us; the launch traced here: 470 us
  waiting for transfers between devices  392 us (83%)
  matrix products  21.1 us (4%)
  local copies, waits for them, and re-layouts  16.8 us (4%)
  starting transfers between devices  15.6 us (3%)
  between operations  14.3 us (3%)
  other arithmetic  10.9 us (2%)
    psum x1, waiting for transfers between devices, per_device(): gathered = lax.psum(blocks, 'expert')  300 us
    all_to_all x1, waiting for transfers between devices, per_device(): lax.all_to_all(token_rows.reshape(local_experts, groups, capacity, -1), '...  84.5 us
  transfers between devices with their start and end apart: 6, of which 3 were waited for; matrix products, arithmetic and copies ran while one was open for 7% of the time, Pallas kernels for 0%

profile of v2, /device:TPU:6, one launch (start us, length us, event | category | flops | bytes accessed | tf_op | source)
XLA Modules:
  0.0 470.5 jit_solution(9623698709281325380)
XLA Ops:
  7.2 0.7 fusion.27
  7.9 1.9 fusion.6
  9.8 2.3 convolution_convert_fusion
  12.1 2.3 copy.47
  14.4 9.2 %all-to-all-start = ((bf16[2,32,16,2048]{3,2,0,1:T(8,128)(2,1)}), bf16[2,32,16,2048]{3,2,0,1:T(8,128)(2,1)}, u32[]{:S(2)}, u32[]{:S(2)}) async-start(bf16[2,32,16,2048]{3,2,0,1:T(8,128)(2,1)} %copy.47), calls=%async_computation | async-start | bytes 8388608 | tf_op jit(solution)/shard_map/all_to_all | solution.py:46
  23.6 0.9 collective-permute-start
  24.5 0.5 collective-permute-start.1
  25.0 9.3 %fusion.7 = bf16[2,512,2048]{2,1,0:T(8,128)(2,1)} fusion(bf16[1,2,768,2048]{3,2,1,0:T(8,128)(2,1)} %param.12, bf16[2,512,1536]{2,1,0:T(8,128)(2,1)} %bitcast.55), kind=kOutput, calls=%fused_computation.18 | convolution fusion | flops 3229614080 | bytes 13631488 | tf_op jit(solution)/shard_map/jsf,jfd->jsd/dot_general | solution.py:84
  34.3 84.5 %all-to-all-done = bf16[2,32,16,2048]{3,2,0,1:T(8,128)(2,1)} async-done(((bf16[2,32,16,2048]{3,2,0,1:T(8,128)(2,1)}), bf16[2,32,16,2048]{3,2,0,1:T(8,128)(2,1)}, u32[]{:S(2)}, u32[]{:S(2)}) %all-to-all-start) | async-done | bytes 4194336 | tf_op jit(solution)/shard_map/all_to_all | solution.py:46
  118.8 3.4 copy.48
  122.2 3.2 copy-done
  125.4 0.9 fusion.1
  126.3 0.1 reshape.123
  126.4 0.6 copy.50
  127.1 3.9 all-to-all-start.1
  130.9 0.2 all-reduce.2.cloned.1.call-start
  131.2 0.1 copy.42
  131.3 0.1 copy.49
  131.4 0.1 eq.41
  131.5 0.1 copy.43
  131.6 0.1 reshape.126
  131.7 7.1 %all-to-all-done.1 = f32[2,32,16]{2,0,1:T(2,128)S(1)} async-done(((f32[2,32,16]{2,0,1:T(2,128)}), f32[2,32,16]{2,0,1:T(2,128)S(1)}, u32[]{:S(2)}, u32[]{:S(2)}) %all-to-all-start.1) | async-done | bytes 4128 | tf_op jit(solution)/shard_map/all_to_all | solution.py:88
  138.8 0.1 broadcast_in_dim.58
  138.9 1.2 select_reduce_fusion
  140.0 0.1 convert_element_type.104
  140.2 0.1 convert_element_type.106
  140.3 0.6 copy.45
  140.9 0.2 broadcast_in_dim.54
  141.1 2.7 dynamic_update_slice.3
  143.8 0.0 copy-start.1
  143.8 1.0 copy-done.1
  144.8 0.0 all-reduce.2.cloned.1.call-update
  144.9 0.1 reshape.124
  144.9 0.1 fusion.23
  145.1 0.1 bitcast_multiply_fusion.2
  145.2 0.1 select_reduce_fusion.2
  145.3 0.9 collective-permute-start.2
  146.2 300.2 %all-reduce.2.cloned.1.call-done = bf16[32,5120]{0,1:T(8,128)(2,1)} async-done(((bf16[32,5120]{0,1:T(8,128)(2,1)}), bf16[32,5120]{0,1:T(8,128)(2,1)}) %all-reduce.2.cloned.1.call-update) | async-done | bytes 327696 | tf_op jit(solution)/shard_map/psum | solution.py:65
  446.4 1.0 slice.16
  447.4 0.1 copy.46
  447.5 0.1 reshape.127
  447.6 4.0 fusion
  451.6 0.2 copy-done.6
  451.8 7.3 %fusion.20 = (bf16[1,2,512,768]{3,2,1,0:T(8,128)(2,1)S(1)}, bf16[1,2,512,768]{3,2,1,0:T(8,128)(2,1)S(1)}) fusion(bf16[2,512,1536]{2,1,0:T(8,128)(2,1)S(1)} %bitcast.56, bf16[2,512,2048]{2,1,0:T(8,128)(2,1)S(1)} %fusion, bf16[1,2,768,2048]{3,2,1,0:T(8,128)(2,1)} %param.12), kind=kOutput, calls=%fused_computation.31 | convolution fusion | flops 3233021952 | bytes 16777216 | tf_op jit(solution)/shard_map/jsd,jfd->jsf/dot_general | solution.py:100
  459.1 1.9 pad_maximum_fusion
  461.0 0.3 copy.53
  461.4 0.1 reshape.125
  461.5 2.2 fusion.22
  (25 shorter events, 0.2 us)
Async XLA Ops:
  14.4 9.2 %copy-start.7 = (bf16[1,2,2048]{2,1,0:T(2,128)(2,1)S(1)}, bf16[1,2,2048]{2,1,0:T(2,128)(2,1)}, u32[]{:S(2)}) copy-start(bf16[1,2,2048]{2,1,0:T(2,128)(2,1)} %param.13) | copy-start | bytes 24580
  14.4 10.1 %copy-start.3 = (bf16[1,128,2048]{2,1,0:T(8,128)(2,1)S(1)}, bf16[1,128,2048]{2,1,0:T(8,128)(2,1)}, u32[]{:S(2)}) copy-start(bf16[1,128,2048]{2,1,0:T(8,128)(2,1)} %param.7) | copy-start | bytes 1572868
  14.4 104.5 %all-to-all-start = ((bf16[2,32,16,2048]{3,2,0,1:T(8,128)(2,1)}), bf16[2,32,16,2048]{3,2,0,1:T(8,128)(2,1)}, u32[]{:S(2)}, u32[]{:S(2)}) async-start(bf16[2,32,16,2048]{3,2,0,1:T(8,128)(2,1)} %copy.47), calls=%async_computation | async-start | bytes 8388608 | tf_op jit(solution)/shard_map/all_to_all | solution.py:46
  23.6 108.1 %collective-permute-start = (bf16[2,2048]{1,0:T(2,128)(2,1)S(1)}, bf16[2,2048]{1,0:T(2,128)(2,1)S(1)}, u32[]{:S(2)}, u32[]{:S(2)}) collective-permute-start(bf16[2,2048]{1,0:T(2,128)(2,1)S(1)} %bitcast.57), channel_id=1, source_target_pairs={{0,224},{32,0},{64,32},{96,64},{128,96},{160,128},{192,160},{224,1... | collective-permute-start | bytes 24584 | tf_op jit(solution)/shard_map/ppermute | solution.py:9
  24.5 437.0 %collective-permute-start.1 = (bf16[128,2048]{1,0:T(8,128)(2,1)S(1)}, bf16[128,2048]{1,0:T(8,128)(2,1)}, u32[]{:S(2)}, u32[]{:S(2)}) collective-permute-start(bf16[128,2048]{1,0:T(8,128)(2,1)S(1)} %bitcast.48), channel_id=1, source_target_pairs={{0,224},{32,0},{64,32},{96,64},{128,96},{160,128},{192,160},{224,1... | collective-permute-start | bytes 1572872 | tf_op jit(solution)/shard_map/ppermute | solution.py:9
  118.8 6.6 %copy-start.2 = (bf16[2,512,2048]{2,1,0:T(8,128)(2,1)S(1)}, bf16[2,512,2048]{2,1,0:T(8,128)(2,1)}, u32[]{:S(2)}) copy-start(bf16[2,512,2048]{2,1,0:T(8,128)(2,1)} %fusion.7) | copy-start | bytes 12582916
  122.2 3.2 copy-start
  125.4 5.7 %copy-start.4 = (f32[1,128,8]{1,2,0:T(8,128)S(1)}, f32[1,128,8]{1,2,0:T(8,128)}, u32[]{:S(2)}) copy-start(f32[1,128,8]{1,2,0:T(8,128)} %param.10) | copy-start | bytes 12292
  127.1 11.7 %all-to-all-start.1 = ((f32[2,32,16]{2,0,1:T(2,128)}), f32[2,32,16]{2,0,1:T(2,128)S(1)}, u32[]{:S(2)}, u32[]{:S(2)}) async-start(f32[2,32,16]{2,0,1:T(2,128)} %copy.50), calls=%async_computation.1 | async-start | bytes 65536 | tf_op jit(solution)/shard_map/all_to_all | solution.py:88
  130.9 315.5 %all-reduce.2.cloned.1.call-start = ((), (), s32[]{:S(2)}) async-start(), calls=%async_computation.2 | async-start | bytes 2621440 | tf_op jit(solution)/shard_map/psum | solution.py:65
  140.9 4.3 copy-start.5
  143.8 1.1 copy-start.1
  145.3 316.2 %collective-permute-start.2 = (bf16[128,64]{0,1:T(8,128)(2,1)S(1)}, bf16[128,64]{0,1:T(8,128)(2,1)S(1)}, u32[]{:S(2)}, u32[]{:S(2)}) collective-permute-start(bf16[128,64]{0,1:T(8,128)(2,1)S(1)} %select_reduce_fusion.2), channel_id=1, source_target_pairs={{0,224},{32,0},{64,32},{96,64},{128,96},{160,128},{192,160},{224,1... | collective-permute-start | bytes 49160 | tf_op jit(solution)/shard_map/ppermute | solution.py:9
  447.6 4.3 copy-start.6
  459.1 1.9 slice-start
Sparse Core Ops, SparseCore 0:
  145.0 301.3 all-reduce.1

commit v3 on v2

--- a/solution.py
+++ b/solution.py
@@ -19,10 +19,8 @@
     expert_total = local_experts * groups
     capacity = tok_rows * top_count // expert_total
     total_rows = expert_total * capacity
+    chunk = width // capacity
     features = grad_out[0]
-
-    next_features = passed_along(features, "pipe", -1)
-    next_router = passed_along(router_weight[0], "pipe", -1)
 
     route_ids = expert_ids[0]
     kept_pairs = slot_ids[0] < capacity
@@ -43,36 +41,22 @@
         axis=1,
     )
 
+    gate_cols = jnp.zeros((total_rows, 128), jnp.bfloat16).at[:, 0].set(slot_gate.astype(jnp.bfloat16))
+    router_chunks = jnp.broadcast_to(
+        router_weight[0].reshape(local_experts, 1, capacity, chunk),
+        (local_experts, groups, capacity, chunk),
+    ).reshape(total_rows, chunk)
+    payload = jnp.concatenate([token_rows, router_chunks, gate_cols], axis=1)
     arrived = lax.all_to_all(
-        token_rows.reshape(local_experts, groups, capacity, -1),
+        payload.reshape(local_experts, groups, capacity, -1),
         "expert",
         split_axis=1,
         concat_axis=1,
         tiled=True,
     )
-
-    me = lax.axis_index("expert")
-    gate_table = (
-        slot_gate.reshape(local_experts, groups, capacity)
-        .transpose(1, 0, 2)
-        .reshape(1, total_rows)
-        .astype(jnp.bfloat16)
-    )
-    own_block = jnp.concatenate([gate_table, next_router.reshape(1, local_experts * width)], axis=1)
-    blocks = lax.dynamic_update_slice(
-        jnp.zeros((groups, own_block.shape[1]), jnp.bfloat16), own_block, (me, 0)
-    )
-    gathered = lax.psum(blocks, "expert")
-    gate_in = (
-        lax.dynamic_slice_in_dim(gathered[:, :total_rows], me * local_experts * capacity, local_experts * capacity, axis=1)
-        .reshape(groups, local_experts, capacity)
-        .transpose(1, 0, 2)
-        .reshape(local_experts, groups * capacity)
-        .astype(jnp.float32)
-    )
-    next_router_full = gathered[:, total_rows:].reshape(expert_total, width)
-
-    rows_in = arrived.reshape(local_experts, groups * capacity, -1).astype(jnp.float32)
+    gate_in = arrived[..., width + chunk].reshape(local_experts, groups * capacity).astype(jnp.float32)
+    router_full = arrived[..., width : width + chunk].transpose(1, 0, 2, 3).reshape(expert_total, width)
+    rows_in = arrived[..., :width].reshape(local_experts, groups * capacity, width).astype(jnp.float32)
 
     pre_saved = saved_pre[0]
     gate_part = pre_saved[..., :hidden_width].astype(jnp.float32)
@@ -110,9 +94,9 @@
     logit_grad = jnp.sum(
         jnp.where(chosen, select_grad[:, :, None], jnp.float32(0.0)), axis=1
     ).astype(jnp.bfloat16)
-    next_logit_grad = passed_along(logit_grad, "pipe", -1)
-    router_part = jnp.dot(next_logit_grad, next_router_full, preferred_element_type=jnp.float32)
-    outgoing = (next_features.astype(jnp.float32) + router_part).astype(jnp.bfloat16)
+    router_part = jnp.dot(logit_grad, router_full, preferred_element_type=jnp.float32)
+    section_grad = (features.astype(jnp.float32) + router_part).astype(jnp.bfloat16)
+    outgoing = passed_along(section_grad, "pipe", -1)
     return (pre_grad[None], outgoing[None])
 
 

time: 472 us -> 182 us (0.39)
  waiting for transfers between devices: 392 us -> 123 us
  between operations: 14.3 us -> 0.82 us
    psum x1 -> x0, waiting for transfers between devices: 300 us -> none  [per_device(): gathered = lax.psum(blocks, 'expert')]
    ppermute x3 -> x1, waiting for transfers between devices: 0.01 us -> 19.1 us  [passed_along(): lax.ppermute(value, axis, [(i, (i + by) % peers) for i in range(peers)])]
    all_to_all x1, waiting for transfers between devices: 84.5 us -> 98.4 us  [per_device(): lax.all_to_all(payload.reshape(local_experts, groups, capacity, -1), 'exp...]
  transfers between devices with their start and end apart: 6 -> 3, of which waited for: 3 -> 3; matrix products, arithmetic and copies ran while one was open for 7% -> 12% of each run, Pallas kernels for 0% -> 0%
where the time goes in v3:
time: 182 us
  waiting for transfers between devices  123 us (68%)
  matrix products  20.1 us (11%)
  local copies, waits for them, and re-layouts  14.6 us (8%)
  starting transfers between devices  14.2 us (8%)
  other arithmetic  9.5 us (5%)
    all_to_all x1, waiting for transfers between devices, per_device(): lax.all_to_all(payload.reshape(local_experts, groups, capacity, -1), 'exp...  98.4 us
    ppermute x1, waiting for transfers between devices, passed_along(): lax.ppermute(value, axis, [(i, (i + by) % peers) for i in range(peers)])  19.1 us
    dot_general x1, matrix products, per_device(): jnp.einsum('jsd,jfd->jsf', scaled_rows, weights, preferred_element_type=j...  9.36 us
    all_to_all x1, starting transfers between devices, per_device(): lax.all_to_all(payload.reshape(local_experts, groups, capacity, -1), 'exp...  9.3 us
    dot_general x1, matrix products, per_device(): jnp.einsum('jsf,jfd->jsd', hidden, weights, preferred_element_type=jnp.fl...  8.11 us
    unnamed x17, local copies, waits for them, and re-layouts  5.67 us
    all_to_all x1, waiting for transfers between devices, per_device(): lax.all_to_all(row_scores.reshape(local_experts, groups, capacity), 'expe...  5.21 us
    all_to_all x1, starting transfers between devices, per_device(): lax.all_to_all(row_scores.reshape(local_experts, groups, capacity), 'expe...  3.85 us
  transfers between devices with their start and end apart: 3, of which 3 were waited for; matrix products, arithmetic and copies ran while one was open for 12% of the time, Pallas kernels for 0%

profile of v3, /device:TPU:6, one launch (start us, length us, event | category | flops | bytes accessed | tf_op | source)
XLA Modules:
  0.0 182.0 jit_solution(13284540372381284558)
XLA Ops:
  0.6 0.6 compare_reduce_fusion
  1.3 0.7 convert_convert_fusion
  2.0 0.7 copy.99
  2.7 0.1 copy.79
  2.8 0.1 reshape.145
  2.8 0.7 fusion.33
  3.6 0.1 copy.78
  3.7 0.1 eq.45
  3.8 1.9 %fusion.8 = pred[1024,128]{1,0:T(8,128)(4,1)S(1)} fusion(s32[128,8]{0,1:T(8,128)S(1)} %bitcast.53), kind=kLoop, calls=%fused_computation.17 | loop fusion | flops 1966080 | bytes 135168 | tf_op jit(solution)/shard_map/reduce_or | solution.py:35
  5.7 0.5 select_reduce_fusion.1
  6.2 0.7 convert_select_fusion
  6.9 0.2 reshape.148
  7.1 0.1 scatter.4.clone
  7.1 2.3 %convolution_convert_fusion = bf16[1024,2048]{1,0:T(8,128)(2,1)S(1)} fusion(pred[1024,128]{1,0:T(8,128)(4,1)S(1)} %fusion.8, bf16[1,128,2048]{2,1,0:T(8,128)(2,1)} %param.9), kind=kOutput, calls=%fused_computation.21 | convolution fusion | flops 538968064 | bytes 4849664 | tf_op jit(solution)/shard_map/dot_general | solution.py:36
  9.5 0.4 pad_maximum_fusion
  9.9 2.7 %copy.81 = bf16[2,32,16,2304]{3,2,0,1:T(8,128)(2,1)} copy(bf16[2,32,16,2304]{3,2,1,0:T(8,128)(2,1)S(1)} %pad_maximum_fusion) | data formatting | bytes 9437184 | tf_op jit(solution)/shard_map/concatenate | solution.py:49
  12.6 9.3 %all-to-all-start = ((bf16[2,32,16,2304]{3,2,0,1:T(8,128)(2,1)}), bf16[2,32,16,2304]{3,2,0,1:T(8,128)(2,1)}, u32[]{:S(2)}, u32[]{:S(2)}) async-start(bf16[2,32,16,2304]{3,2,0,1:T(8,128)(2,1)} %copy.81), calls=%async_computation | async-start | bytes 9437184 | tf_op jit(solution)/shard_map/all_to_all | solution.py:50
  21.9 8.1 %fusion.9 = bf16[2,512,2048]{2,1,0:T(8,128)(2,1)} fusion(bf16[1,2,768,2048]{3,2,1,0:T(8,128)(2,1)} %param.14, bf16[2,512,1536]{2,1,0:T(8,128)(2,1)S(1)} %bitcast.58), kind=kOutput, calls=%fused_computation.20 | convolution fusion | flops 3229614080 | bytes 13631488 | tf_op jit(solution)/shard_map/jsf,jfd->jsd/dot_general | solution.py:68
  30.0 98.4 %all-to-all-done = bf16[2,32,16,2304]{3,2,0,1:T(8,128)(2,1)} async-done(((bf16[2,32,16,2304]{3,2,0,1:T(8,128)(2,1)}), bf16[2,32,16,2304]{3,2,0,1:T(8,128)(2,1)}, u32[]{:S(2)}, u32[]{:S(2)}) %all-to-all-start) | async-done | bytes 4718624 | tf_op jit(solution)/shard_map/all_to_all | solution.py:50
  128.5 2.5 %slice.35 = bf16[2,32,16,2048]{3,2,0,1:T(8,128)(2,1)S(1)} slice(bf16[2,32,16,2304]{3,2,0,1:T(8,128)(2,1)} %all-to-all-done), slice={[0:2], [0:32], [0:16], [0:2048]} | slice | bytes 8388608 | tf_op jit(solution)/shard_map/slice | solution.py:59
  131.0 0.6 copy.90
  131.6 2.1 %copy-done = bf16[2,32,16,2048]{3,2,1,0:T(8,128)(2,1)} copy-done((bf16[2,32,16,2048]{3,2,1,0:T(8,128)(2,1)}, bf16[2,32,16,2048]{3,2,1,0:T(8,128)(2,1)S(1)}, u32[]{:S(2)}) %copy-start) | copy-done | bytes 4194328
  133.7 1.0 copy-done.1
  134.7 1.3 fusion.1
  135.9 0.1 reshape.142
  136.0 0.6 copy.86
  136.7 3.9 %all-to-all-start.1 = ((f32[2,32,16]{2,0,1:T(2,128)}), f32[2,32,16]{2,0,1:T(2,128)S(1)}, u32[]{:S(2)}, u32[]{:S(2)}) async-start(f32[2,32,16]{2,0,1:T(2,128)} %copy.86), calls=%async_computation.1 | async-start | bytes 65536 | tf_op jit(solution)/shard_map/all_to_all | solution.py:72
  140.5 0.0 copy-done.3
  140.5 0.1 copy.85
  140.6 1.0 slice.34
  141.6 0.4 copy.89
  142.0 0.1 copy.83
  142.1 0.1 reshape.146
  142.2 1.0 slice.38
  143.1 5.2 %all-to-all-done.1 = f32[2,32,16]{2,0,1:T(2,128)S(1)} async-done(((f32[2,32,16]{2,0,1:T(2,128)}), f32[2,32,16]{2,0,1:T(2,128)S(1)}, u32[]{:S(2)}, u32[]{:S(2)}) %all-to-all-start.1) | async-done | bytes 4128 | tf_op jit(solution)/shard_map/all_to_all | solution.py:72
  148.4 0.1 broadcast_in_dim.64
  148.4 0.5 select_reduce_fusion
  149.0 0.1 reshape.143
  149.1 0.1 fusion.28
  149.2 0.1 bitcast_multiply_fusion
  149.3 0.0 copy-done.4
  149.3 0.1 select_reduce_fusion.2
  149.4 0.3 fusion.20
  149.7 1.1 collective-permute-start
  150.8 9.4 %fusion.23 = (bf16[1,2,512,768]{3,2,1,0:T(8,128)(2,1)S(1)}, bf16[1,2,512,768]{3,2,1,0:T(8,128)(2,1)S(1)}) fusion(bf16[2,512,1536]{2,1,0:T(8,128)(2,1)} %bitcast.57, bf16[1,2,768,2048]{3,2,1,0:T(8,128)(2,1)} %param.14, bf16[2,512,2048]{2,1,0:T(8,128)(2,1)} %bitcast.49, f32[2,512]{1,0:T(2,128)S(1)} %reshape.146), kind=kOutput, calls=%fused_computation.35 | convolution fusion | flops 3239313408 | bytes 16781312 | tf_op jit(solution)/shard_map/jsd,jfd->jsf/dot_general | solution.py:84
  160.2 1.9 %pad_maximum_fusion.1 = bf16[1,2,512,1536]{3,2,1,0:T(8,128)(2,1)} fusion(bf16[1,2,512,768]{3,2,1,0:T(8,128)(2,1)S(1)} %get-tuple-element.15, bf16[1,2,512,768]{3,2,1,0:T(8,128)(2,1)S(1)} %get-tuple-element.14), kind=kLoop, calls=%fused_computation.30 | loop fusion | flops 6291456 | bytes 6291456 | tf_op jit(solution)/shard_map/concatenate | solution.py:87
  162.1 19.1 %collective-permute-done = bf16[128,2048]{1,0:T(8,128)(2,1)S(1)} collective-permute-done((bf16[128,2048]{1,0:T(8,128)(2,1)S(1)}, bf16[128,2048]{1,0:T(8,128)(2,1)S(1)}, u32[]{:S(2)}, u32[]{:S(2)}) %collective-permute-start) | collective-permute-done | bytes 524320 | tf_op jit(solution)/shard_map/ppermute | solution.py:9
  181.2 0.8 copy.101
  (11 shorter events, 0.1 us)
Async XLA Ops:
  12.6 9.3 %copy-start.5 = (bf16[1,2,512,1536]{3,2,1,0:T(8,128)(2,1)S(1)}, bf16[1,2,512,1536]{3,2,1,0:T(8,128)(2,1)}, u32[]{:S(2)}) copy-start(bf16[1,2,512,1536]{3,2,1,0:T(8,128)(2,1)} %param.13) | copy-start | bytes 9437188
  12.6 115.9 %all-to-all-start = ((bf16[2,32,16,2304]{3,2,0,1:T(8,128)(2,1)}), bf16[2,32,16,2304]{3,2,0,1:T(8,128)(2,1)}, u32[]{:S(2)}, u32[]{:S(2)}) async-start(bf16[2,32,16,2304]{3,2,0,1:T(8,128)(2,1)} %copy.81), calls=%async_computation | async-start | bytes 9437184 | tf_op jit(solution)/shard_map/all_to_all | solution.py:50
  131.0 3.7 %copy-start.1 = (bf16[2,512,2048]{2,1,0:T(8,128)(2,1)S(1)}, bf16[2,512,2048]{2,1,0:T(8,128)(2,1)}, u32[]{:S(2)}) copy-start(bf16[2,512,2048]{2,1,0:T(8,128)(2,1)} %fusion.9) | copy-start | bytes 12582916
  131.6 2.1 %copy-start = (bf16[2,32,16,2048]{3,2,1,0:T(8,128)(2,1)}, bf16[2,32,16,2048]{3,2,1,0:T(8,128)(2,1)S(1)}, u32[]{:S(2)}) copy-start(bf16[2,32,16,2048]{3,2,1,0:T(8,128)(2,1)S(1)} %copy.90) | copy-start | bytes 12582916
  134.7 5.9 %copy-start.3 = (f32[1,128,8]{1,2,0:T(8,128)S(1)}, f32[1,128,8]{1,2,0:T(8,128)}, u32[]{:S(2)}) copy-start(f32[1,128,8]{1,2,0:T(8,128)} %param.12) | copy-start | bytes 12292
  134.7 14.7 %copy-start.4 = (s32[1,128,8]{1,2,0:T(8,128)S(1)}, s32[1,128,8]{1,2,0:T(8,128)}, u32[]{:S(2)}) copy-start(s32[1,128,8]{1,2,0:T(8,128)} %param.10) | copy-start | bytes 12292
  134.7 14.7 %copy-start.2 = (bf16[1,128,2048]{2,1,0:T(8,128)(2,1)S(1)}, bf16[1,128,2048]{2,1,0:T(8,128)(2,1)}, u32[]{:S(2)}) copy-start(bf16[1,128,2048]{2,1,0:T(8,128)(2,1)} %param.9) | copy-start | bytes 1572868
  136.7 11.7 %all-to-all-start.1 = ((f32[2,32,16]{2,0,1:T(2,128)}), f32[2,32,16]{2,0,1:T(2,128)S(1)}, u32[]{:S(2)}, u32[]{:S(2)}) async-start(f32[2,32,16]{2,0,1:T(2,128)} %copy.86), calls=%async_computation.1 | async-start | bytes 65536 | tf_op jit(solution)/shard_map/all_to_all | solution.py:72
  149.7 31.5 %collective-permute-start = (bf16[128,2048]{1,0:T(8,128)(2,1)S(1)}, bf16[128,2048]{1,0:T(8,128)(2,1)S(1)}, u32[]{:S(2)}, u32[]{:S(2)}) collective-permute-start(bf16[128,2048]{1,0:T(8,128)(2,1)S(1)} %fusion.20), channel_id=1, source_target_pairs={{0,224},{32,0},{64,32},{96,64},{128,96},{160,128},{192,160},{224,1... | collective-permute-start | bytes 1572872 | tf_op jit(solution)/shard_map/ppermute | solution.py:9

commit v4 on v3

v4 whole, which is shorter than its diff:
```python
import jax
import jax.numpy as jnp
import numpy as np
from jax import lax
from jax.sharding import Mesh, PartitionSpec as P

EXPERT_AXES = ("y", "zl", "core")
RING_AXES = ("y", "core")


def passed_along(value, axis, by):
    peers = lax.axis_size(axis)
    return lax.ppermute(value, axis, [(i, (i + by) % peers) for i in range(peers)])


def per_device(grad_out, expert_ids, slot_ids, gate_weights, saved_pre, down_weight, router_weight):
    ring_y = lax.axis_size("y")
    ring_z = lax.axis_size("zl")
    ring_c = lax.axis_size("core")
    groups = ring_y * ring_z * ring_c
    ring = ring_y * ring_c
    local_experts = down_weight.shape[1]
    hidden_width = down_weight.shape[2]
    tok_rows = grad_out.shape[1]
    width = grad_out.shape[2]
    top_count = expert_ids.shape[2]
    expert_total = local_experts * groups
    capacity = tok_rows * top_count // expert_total
    total_rows = expert_total * capacity
    features = grad_out[0]
    my_z = lax.axis_index("zl")

    route_ids = expert_ids[0]
    kept_pairs = slot_ids[0] < capacity
    destination = (
        route_ids % local_experts * (groups * capacity)
        + route_ids // local_experts * capacity
        + jnp.minimum(slot_ids[0], capacity - 1)
    )
    pair_dest = jnp.where(kept_pairs, destination, total_rows)
    row_ids = jnp.arange(total_rows, dtype=jnp.int32)
    matches = (pair_dest[None, :, :] == row_ids[:, None, None]).reshape(total_rows, tok_rows * top_count)

    router_flat = router_weight[0].reshape(tok_rows, local_experts * width // tok_rows)
    extras = jnp.concatenate(
        [
            route_ids.astype(jnp.bfloat16),
            slot_ids[0].astype(jnp.bfloat16),
            gate_weights[0].astype(jnp.bfloat16),
            jnp.zeros((tok_rows, 32 - 3 * top_count), jnp.bfloat16),
            router_flat,
            jnp.zeros((tok_rows, 128 - 32 - router_flat.shape[1]), jnp.bfloat16),
        ],
        axis=1,
    )
    own = jnp.concatenate([features, extras], axis=1)
    stage_a = lax.all_to_all(
        jnp.broadcast_to(own[None], (ring_z,) + own.shape), "zl", split_axis=0, concat_axis=0, tiled=True
    )
    near_rows = stage_a[..., :width].reshape(ring_z * tok_rows, width)
    near_ids = stage_a[..., width : width + top_count].astype(jnp.int32)
    near_slots = stage_a[..., width + top_count : width + 2 * top_count].astype(jnp.int32)
    near_gates = stage_a[..., width + 2 * top_count : width + 3 * top_count].astype(jnp.float32)
    near_router = stage_a[..., width + 32 : width + 32 + router_flat.shape[1]].reshape(
        ring_z, local_experts, width
    )

    dev = near_ids // local_experts
    dest_y = dev // (ring_z * ring_c)
    dest_z = dev // ring_c % ring_z
    dest_c = dev % ring_c
    dest_j = near_ids % local_experts
    source_z = jnp.arange(ring_z, dtype=jnp.int32)[:, None, None]
    ring_rows = ring * local_experts * ring_z * capacity
    near_dest = (
        ((dest_y * ring_c + dest_c) * local_experts + dest_j) * ring_z + source_z
    ) * capacity + jnp.minimum(near_slots, capacity - 1)
    near_dest = jnp.where((near_slots < capacity) & (dest_z == my_z), near_dest, ring_rows)
    ring_ids = jnp.arange(ring_rows, dtype=jnp.int32)
    near_hit = near_dest.reshape(ring_z * tok_rows, top_count)[None, :, :] == ring_ids[:, None, None]
    near_onehot = jnp.any(near_hit, axis=2).astype(jnp.bfloat16)
    ring_tokens = jnp.dot(near_onehot, near_rows, preferred_element_type=jnp.float32).astype(jnp.bfloat16)
    ring_gate = jnp.sum(
        jnp.where(near_hit, near_gates.reshape(ring_z * tok_rows, top_count)[None], jnp.float32(0.0)),
        axis=(1, 2),
    )
    rows_per_dest = local_experts * ring_z * capacity
    router_cols = jnp.broadcast_to(
        near_router.reshape(1, rows_per_dest, ring_z * local_experts * width // rows_per_dest),
        (ring, rows_per_dest, ring_z * local_experts * width // rows_per_dest),
    ).reshape(ring_rows, -1)
    gate_cols = jnp.zeros((ring_rows, 128), jnp.bfloat16).at[:, 0].set(ring_gate.astype(jnp.bfloat16))
    payload = jnp.concatenate([ring_tokens, router_cols, gate_cols], axis=1)
    arrived = lax.all_to_all(
        payload.reshape(ring, rows_per_dest, -1), RING_AXES, split_axis=0, concat_axis=0, tiled=True
    ).reshape(ring_y, ring_c, local_experts, ring_z, capacity, -1)
    arrived_rows = arrived.transpose(2, 0, 3, 1, 4, 5).reshape(local_experts, groups * capacity, -1)
    rows_in = arrived_rows[..., :width].astype(jnp.float32)
    router_w = router_cols.shape[1]
    gate_in = arrived_rows[..., width + router_w].astype(jnp.float32)
    router_full = (
        arrived[:, :, :, :, :, width : width + router_w]
        .reshape(ring_y, ring_c, ring_z, local_experts, width)
        .transpose(0, 2, 1, 3, 4)
        .reshape(expert_total, width)
    )

    pre_saved = saved_pre[0]
    gate_part = pre_saved[..., :hidden_width].astype(jnp.float32)
    up_part = pre_saved[..., hidden_width:].astype(jnp.float32)
    sigmoid_gate = jax.nn.sigmoid(gate_part)
    silu_gate = gate_part * sigmoid_gate
    hidden = (silu_gate * up_part).astype(jnp.bfloat16)
    weights = down_weight[0]
    expert_out = jnp.einsum(
        "jsf,jfd->jsd", hidden, weights, preferred_element_type=jnp.float32
    ).astype(jnp.bfloat16)
    row_scores = jnp.sum(rows_in * lax.optimization_barrier(expert_out).astype(jnp.float32), axis=-1)
    returned = lax.all_to_all(
        row_scores.reshape(local_experts, groups, capacity),
        EXPERT_AXES,
        split_axis=1,
        concat_axis=1,
        tiled=True,
    )
    pair_scores = jnp.sum(
        jnp.where(matches, returned.reshape(total_rows)[:, None], jnp.float32(0.0)), axis=0
    ).reshape(tok_rows, top_count)

    scaled_rows = (gate_in[..., None] * rows_in).astype(jnp.bfloat16)
    row_grad = jnp.einsum("jsd,jfd->jsf", scaled_rows, weights, preferred_element_type=jnp.float32)
    gate_grad = row_grad * up_part * sigmoid_gate * (1.0 + gate_part * (1.0 - sigmoid_gate))
    up_grad = row_grad * silu_gate
    pre_grad = jnp.concatenate([gate_grad, up_grad], axis=-1).astype(jnp.bfloat16)

    gate_values = gate_weights[0]
    weighted_sum = jnp.sum(gate_values * pair_scores, axis=-1, keepdims=True)
    select_grad = gate_values * (pair_scores - weighted_sum)
    expert_columns = jnp.arange(expert_total, dtype=jnp.int32)
    chosen = route_ids[:, :, None] == expert_columns[None, None, :]
    logit_grad = jnp.sum(
        jnp.where(chosen, select_grad[:, :, None], jnp.float32(0.0)), axis=1
    ).astype(jnp.bfloat16)
    router_part = jnp.dot(logit_grad, router_full, preferred_element_type=jnp.float32)
    section_grad = (features.astype(jnp.float32) + router_part).astype(jnp.bfloat16)
    outgoing = passed_along(section_grad, "pipe", -1)
    return (pre_grad[None], outgoing[None])


def ring_shape(mesh):
    row = mesh.devices[0]
    try:
        ys = sorted({d.coords[1] for d in row})
        zs = sorted({d.coords[2] for d in row})
        cs = sorted({d.core_on_chip for d in row})
        return len(ys), len(zs), len(cs)
    except AttributeError:
        return 4, row.size // 8, 2


def solution(mesh):
    ring_y, ring_z, ring_c = ring_shape(mesh)
    fine = Mesh(
        np.asarray(mesh.devices).reshape(mesh.devices.shape[0], ring_y, ring_z, ring_c),
        ("pipe",) + EXPERT_AXES,
    )
    in_specs = (
        P("pipe", EXPERT_AXES, None),
        P("pipe", EXPERT_AXES, None),
        P("pipe", EXPERT_AXES, None),
        P("pipe", EXPERT_AXES, None),
        P("pipe", EXPERT_AXES, None, None),
        P("pipe", EXPERT_AXES, None, None),
        P("pipe", EXPERT_AXES, None),
    )
    out_specs = (P("pipe", EXPERT_AXES, None, None), P("pipe", EXPERT_AXES, None))
    return jax.shard_map(
        per_device, mesh=fine, in_specs=in_specs, out_specs=out_specs, check_vma=False
    )
```

time: 182 us -> 200 us (1.099); the launches traced: 182 us -> 196 us
  other arithmetic: 9.5 us -> 19.9 us
  waiting for transfers between devices: 123 us -> 116 us
  local copies, waits for them, and re-layouts: 14.6 us -> 20.8 us
  matrix products: 20.1 us -> 23.1 us
    reduce_or x1, other arithmetic: 1.92 us -> 8.07 us  [per_device(): near_onehot = jnp.any(near_hit, axis=2).astype(jnp.bfloat16)]
    ppermute x1, waiting for transfers between devices: 19.1 us -> 14.9 us  [passed_along(): lax.ppermute(value, axis, [(i, (i + by) % peers) for i in range(peers)])]
    transpose x0 -> x2, local copies, waits for them, and re-layouts: none -> 3.26 us  [the longest x1 3.02 us: per_device(): arrived.transpose(2, 0, 3, 1, 4, 5)]
    all_to_all x2 -> x3, waiting for transfers between devices: 104 us -> 101 us  [the longest x1 50.4 us: per_device(): lax.all_to_all(jnp.broadcast_to(own[None], (ring_z,) + own.shape), 'zl',...]
    reduce_sum x1, other arithmetic: 0.5 us -> 3.06 us  [per_device(): jnp.sum(jnp.where(near_hit, near_gates.reshape(ring_z * tok_rows, top_cou...]
    slice x3 -> x5, local copies, waits for them, and re-layouts: 4.43 us -> 6.56 us  [the longest x2 5.46 us: per_device(): near_rows = stage_a[..., :width].reshape(ring_z * tok_rows, width)]
    all_to_all x2 -> x3, starting transfers between devices: 13.2 us -> 14.6 us  [the longest x1 5.89 us: per_device(): lax.all_to_all(jnp.broadcast_to(own[None], (ring_z,) + own.shape), 'zl',...]
    unnamed x17 -> x14, local copies, waits for them, and re-layouts: 5.67 us -> 5.34 us
  transfers between devices with their start and end apart: 3 -> 4, of which waited for: 3 -> 4; matrix products, arithmetic and copies ran while one was open for 12% -> 12% of each run, Pallas kernels for 0% -> 0%
where the time goes in v4:
time: 200 us; the launch traced here: 196 us
  waiting for transfers between devices  116 us (58%)
  matrix products  23.1 us (12%)
  local copies, waits for them, and re-layouts  20.8 us (10%)
  other arithmetic  19.9 us (10%)
  starting transfers between devices  15.5 us (8%)
    all_to_all x1, waiting for transfers between devices, per_device(): lax.all_to_all(jnp.broadcast_to(own[None], (ring_z,) + own.shape), 'zl',...  50.4 us
    all_to_all x1, waiting for transfers between devices, per_device(): lax.all_to_all(payload.reshape(ring, rows_per_dest, -1), RING_AXES, split...  45.6 us
    ppermute x1, waiting for transfers between devices, passed_along(): lax.ppermute(value, axis, [(i, (i + by) % peers) for i in range(peers)])  14.9 us
    dot_general x1, matrix products, per_device(): jnp.einsum('jsf,jfd->jsd', hidden, weights, preferred_element_type=jnp.fl...  9.46 us
    dot_general x1, matrix products, per_device(): jnp.einsum('jsd,jfd->jsf', scaled_rows, weights, preferred_element_type=j...  9.36 us
    reduce_or x1, other arithmetic, per_device(): near_onehot = jnp.any(near_hit, axis=2).astype(jnp.bfloat16)  8.07 us
    all_to_all x1, starting transfers between devices, per_device(): lax.all_to_all(jnp.broadcast_to(own[None], (ring_z,) + own.shape), 'zl',...  5.89 us
    slice x2, local copies, waits for them, and re-layouts, per_device(): near_rows = stage_a[..., :width].reshape(ring_z * tok_rows, width)  5.46 us
  transfers between devices with their start and end apart: 4, of which 4 were waited for; matrix products, arithmetic and copies ran while one was open for 12% of the time, Pallas kernels for 0%

profile of v4, /device:TPU:6, one launch (start us, length us, event | category | flops | bytes accessed | tf_op | source)
XLA Modules:
  0.0 196.0 jit_solution(3629280202833048322)
XLA Ops:
  0.6 0.8 copy.63
  1.4 0.8 copy.61
  2.2 0.8 copy.62
  3.0 0.8 reshape_squeeze.3
  3.8 1.2 concatenate.28
  5.0 0.3 copy.64
  5.4 1.7 broadcast_in_dim.85
  7.0 5.9 %all-to-all-start = ((bf16[4,128,2176]{1,2,0:T(8,128)(2,1)}), bf16[4,128,2176]{1,2,0:T(8,128)(2,1)S(1)}, u32[]{:S(2)}, u32[]{:S(2)}) async-start(bf16[4,128,2176]{1,2,0:T(8,128)(2,1)} %broadcast_in_dim.85), calls=%async_computation | async-start | bytes 4456448 | tf_op jit(solution)/shard_map/all_to_all | solution.py:57
  12.9 0.6 compare_reduce_fusion
  13.5 50.4 %all-to-all-done = bf16[4,128,2176]{1,2,0:T(8,128)(2,1)S(1)} async-done(((bf16[4,128,2176]{1,2,0:T(8,128)(2,1)}), bf16[4,128,2176]{1,2,0:T(8,128)(2,1)S(1)}, u32[]{:S(2)}, u32[]{:S(2)}) %all-to-all-start) | async-done | bytes 2228256 | tf_op jit(solution)/shard_map/all_to_all | solution.py:57
  64.0 8.1 %fusion = pred[1024,512]{1,0:T(8,128)(4,1)S(1)} fusion(s32[512,8]{0,1:T(8,128)S(1)} %fusion.31), kind=kLoop, calls=%fused_computation.2 | loop fusion | flops 7864320 | bytes 540672 | tf_op jit(solution)/shard_map/reduce_or | solution.py:81
  72.0 1.5 slice.56
  73.5 4.0 %copy.65 = bf16[4,128,2048]{2,1,0:T(8,128)(2,1)} copy(bf16[4,128,2048]{1,2,0:T(8,128)(2,1)} %slice.56) | data formatting | bytes 4194304 | tf_op jit(solution)/shard_map/slice | solution.py:60
  77.5 3.1 %select_reduce_fusion = bf16[1024]{0:T(1024)(128)(2,1)S(1)} fusion(f32[512,8]{0,1:T(8,128)S(1)} %fusion.50, s32[512,8]{0,1:T(8,128)S(1)} %fusion.31), kind=kLoop, calls=%fused_computation | loop fusion | flops 12581888 | bytes 34816 | tf_op jit(solution)/shard_map/reduce_sum | solution.py:83
  80.6 0.7 convert_select_fusion.1
  81.2 0.2 reshape.146
  81.5 0.1 copy.66
  81.6 0.1 broadcast_in_dim.87
  81.8 3.9 %convolution_convert_fusion = bf16[1024,2048]{1,0:T(8,128)(2,1)S(1)} fusion(pred[1024,512]{1,0:T(8,128)(4,1)S(1)} %fusion, bf16[512,2048]{1,0:T(8,128)(2,1)} %bitcast.53), kind=kOutput, calls=%fused_computation.20 | convolution fusion | flops 2149580800 | bytes 6815744 | tf_op jit(solution)/shard_map/dot_general | solution.py:82
  85.8 2.4 %pad_maximum_fusion = bf16[8,128,2304]{2,1,0:T(8,128)(2,1)} fusion(bf16[8,128,128]{2,1,0:T(8,128)(2,1)S(1)} %bitcast.55, bf16[8,128,128]{2,1,0:T(8,128)(2,1)S(1)} %broadcast_in_dim.88, bf16[8,128,2048]{2,1,0:T(8,128)(2,1)S(1)} %bitcast.52), kind=kLoop, calls=%fused_computation.14 | loop fusion | flops 14155776 | bytes 9437184 | tf_op jit(solution)/shard_map/concatenate | solution.py:93
  88.2 4.6 %all-to-all-start.1 = ((bf16[8,128,2304]{2,1,0:T(8,128)(2,1)}), bf16[8,128,2304]{2,1,0:T(8,128)(2,1)}, u32[]{:S(2)}, u32[]{:S(2)}) async-start(bf16[8,128,2304]{2,1,0:T(8,128)(2,1)} %pad_maximum_fusion), calls=%async_computation.1 | async-start | bytes 9437184 | tf_op jit(solution)/shard_map/all_to_all | solution.py:94
  92.8 9.5 %fusion.9 = bf16[2,512,2048]{2,1,0:T(8,128)(2,1)} fusion(bf16[1,2,768,2048]{3,2,1,0:T(8,128)(2,1)} %param.14, bf16[2,512,1536]{2,1,0:T(8,128)(2,1)} %bitcast.59), kind=kOutput, calls=%fused_computation.21 | convolution fusion | flops 3229614080 | bytes 13631488 | tf_op jit(solution)/shard_map/jsf,jfd->jsd/dot_general | solution.py:115
  102.3 0.1 copy.70
  102.4 0.1 eq.65
  102.5 45.6 %all-to-all-done.1 = bf16[8,128,2304]{2,1,0:T(8,128)(2,1)} async-done(((bf16[8,128,2304]{2,1,0:T(8,128)(2,1)}), bf16[8,128,2304]{2,1,0:T(8,128)(2,1)}, u32[]{:S(2)}, u32[]{:S(2)}) %all-to-all-start.1) | async-done | bytes 4718624 | tf_op jit(solution)/shard_map/all_to_all | solution.py:94
  148.0 3.0 %copy.68 = bf16[2,4,4,2,16,2304]{5,4,3,2,1,0:T(8,128)(2,1)S(1)} copy(bf16[2,4,4,2,16,2304]{5,4,2,0,3,1:T(8,128)(2,1)} %bitcast.10) | data formatting | bytes 9437184 | tf_op jit(solution)/shard_map/transpose | solution.py:97
  151.0 2.2 %copy-done = bf16[2,4,4,2,16,2304]{5,4,3,2,1,0:T(8,128)(2,1)} copy-done((bf16[2,4,4,2,16,2304]{5,4,3,2,1,0:T(8,128)(2,1)}, bf16[2,4,4,2,16,2304]{5,4,3,2,1,0:T(8,128)(2,1)S(1)}, u32[]{:S(2)}) %copy-start) | copy-done | bytes 4718616
  153.2 1.2 fusion.2
  154.4 0.1 reshape.140
  154.5 0.6 copy.71
  155.1 4.1 %all-to-all-start.2 = ((f32[2,32,16]{2,0,1:T(2,128)}), f32[2,32,16]{2,0,1:T(2,128)S(1)}, u32[]{:S(2)}, u32[]{:S(2)}) async-start(f32[2,32,16]{2,0,1:T(2,128)} %copy.71), calls=%async_computation.2 | async-start | bytes 65536 | tf_op jit(solution)/shard_map/all_to_all | solution.py:119
  159.2 1.1 convert_reduce_fusion
  160.3 1.0 slice.63
  161.3 0.1 reshape.142
  161.3 0.2 copy.74
  161.6 0.1 reshape.143
  161.7 5.1 %all-to-all-done.2 = f32[2,32,16]{2,0,1:T(2,128)S(1)} async-done(((f32[2,32,16]{2,0,1:T(2,128)}), f32[2,32,16]{2,0,1:T(2,128)S(1)}, u32[]{:S(2)}, u32[]{:S(2)}) %all-to-all-start.2) | async-done | bytes 4128 | tf_op jit(solution)/shard_map/all_to_all | solution.py:119
  166.8 0.1 broadcast_in_dim.94
  166.9 0.5 select_reduce_fusion.1
  167.4 0.1 reshape.141
  167.5 0.1 fusion.26
  167.6 0.1 bitcast_multiply_fusion
  167.8 0.3 fusion.21
  168.2 0.9 collective-permute-start
  169.1 9.4 %fusion.24 = (bf16[1,2,512,768]{3,2,1,0:T(8,128)(2,1)S(1)}, bf16[1,2,512,768]{3,2,1,0:T(8,128)(2,1)S(1)}) fusion(bf16[2,512,1536]{2,1,0:T(8,128)(2,1)} %bitcast.60, bf16[1,2,768,2048]{3,2,1,0:T(8,128)(2,1)} %param.14, f32[2,512]{1,0:T(2,128)S(1)} %convert_reduce_fusion, bf16[2,512,2304]{2,1,0:T(8,128)(2,1)} %bitcast.51), kind=kOutput, calls=%fused_computation.36 | convolution fusion | flops 3239313408 | bytes 16781312 | tf_op jit(solution)/shard_map/jsd,jfd->jsf/dot_general | solution.py:131
  178.4 1.9 pad_maximum_fusion.1
  180.3 14.9 %collective-permute-done = bf16[128,2048]{1,0:T(8,128)(2,1)S(1)} collective-permute-done((bf16[128,2048]{1,0:T(8,128)(2,1)S(1)}, bf16[128,2048]{1,0:T(8,128)(2,1)S(1)}, u32[]{:S(2)}, u32[]{:S(2)}) %collective-permute-start) | collective-permute-done | bytes 524320 | tf_op jit(solution)/shard_map/ppermute | solution.py:13
  195.2 0.8 copy.79
  (22 shorter events, 0.3 us)
Async XLA Ops:
  7.0 56.9 %all-to-all-start = ((bf16[4,128,2176]{1,2,0:T(8,128)(2,1)}), bf16[4,128,2176]{1,2,0:T(8,128)(2,1)S(1)}, u32[]{:S(2)}, u32[]{:S(2)}) async-start(bf16[4,128,2176]{1,2,0:T(8,128)(2,1)} %broadcast_in_dim.85), calls=%async_computation | async-start | bytes 4456448 | tf_op jit(solution)/shard_map/all_to_all | solution.py:57
  88.2 59.9 %all-to-all-start.1 = ((bf16[8,128,2304]{2,1,0:T(8,128)(2,1)}), bf16[8,128,2304]{2,1,0:T(8,128)(2,1)}, u32[]{:S(2)}, u32[]{:S(2)}) async-start(bf16[8,128,2304]{2,1,0:T(8,128)(2,1)} %pad_maximum_fusion), calls=%async_computation.1 | async-start | bytes 9437184 | tf_op jit(solution)/shard_map/all_to_all | solution.py:94
  92.7 9.5 %copy-start.3 = (s32[1,128,8]{1,2,0:T(8,128)S(1)}, s32[1,128,8]{1,2,0:T(8,128)}, u32[]{:S(2)}) copy-start(s32[1,128,8]{1,2,0:T(8,128)} %param.10) | copy-start | bytes 12292
  92.8 9.5 %copy-start.4 = (s32[1,128,8]{1,2,0:T(8,128)S(1)}, s32[1,128,8]{1,2,0:T(8,128)}, u32[]{:S(2)}) copy-start(s32[1,128,8]{1,2,0:T(8,128)} %param.11) | copy-start | bytes 12292
  148.0 5.2 %copy-start.1 = (bf16[2,512,2048]{2,1,0:T(8,128)(2,1)S(1)}, bf16[2,512,2048]{2,1,0:T(8,128)(2,1)}, u32[]{:S(2)}) copy-start(bf16[2,512,2048]{2,1,0:T(8,128)(2,1)} %fusion.9) | copy-start | bytes 12582916
  151.0 2.2 %copy-start = (bf16[2,4,4,2,16,2304]{5,4,3,2,1,0:T(8,128)(2,1)}, bf16[2,4,4,2,16,2304]{5,4,3,2,1,0:T(8,128)(2,1)S(1)}, u32[]{:S(2)}) copy-start(bf16[2,4,4,2,16,2304]{5,4,3,2,1,0:T(8,128)(2,1)S(1)} %copy.68) | copy-start | bytes 14155780
  153.2 14.6 %copy-start.2 = (bf16[1,128,2048]{2,1,0:T(8,128)(2,1)S(1)}, bf16[1,128,2048]{2,1,0:T(8,128)(2,1)}, u32[]{:S(2)}) copy-start(bf16[1,128,2048]{2,1,0:T(8,128)(2,1)} %param.9) | copy-start | bytes 1572868
  155.1 11.7 %all-to-all-start.2 = ((f32[2,32,16]{2,0,1:T(2,128)}), f32[2,32,16]{2,0,1:T(2,128)S(1)}, u32[]{:S(2)}, u32[]{:S(2)}) async-start(f32[2,32,16]{2,0,1:T(2,128)} %copy.71), calls=%async_computation.2 | async-start | bytes 65536 | tf_op jit(solution)/shard_map/all_to_all | solution.py:119
  168.2 27.1 %collective-permute-start = (bf16[128,2048]{1,0:T(8,128)(2,1)S(1)}, bf16[128,2048]{1,0:T(8,128)(2,1)S(1)}, u32[]{:S(2)}, u32[]{:S(2)}) collective-permute-start(bf16[128,2048]{1,0:T(8,128)(2,1)S(1)} %fusion.21), channel_id=1, source_target_pairs={{0,224},{32,0},{64,32},{96,64},{128,96},{160,128},{192,160},{224,1... | collective-permute-start | bytes 1572872 | tf_op jit(solution)/shard_map/ppermute | solution.py:13

commit v5 on v3

--- a/solution.py
+++ b/solution.py
@@ -24,12 +24,7 @@
 
     route_ids = expert_ids[0]
     kept_pairs = slot_ids[0] < capacity
-    destination = (
-        route_ids % local_experts * (groups * capacity)
-        + route_ids // local_experts * capacity
-        + jnp.minimum(slot_ids[0], capacity - 1)
-    )
-    pair_dest = jnp.where(kept_pairs, destination, total_rows)
+    pair_dest = jnp.where(kept_pairs, route_ids * capacity + jnp.minimum(slot_ids[0], capacity - 1), total_rows)
     row_ids = jnp.arange(total_rows, dtype=jnp.int32)
     token_hit = pair_dest[None, :, :] == row_ids[:, None, None]
     token_onehot = jnp.any(token_hit, axis=2).astype(jnp.bfloat16)
@@ -43,20 +38,22 @@
 
     gate_cols = jnp.zeros((total_rows, 128), jnp.bfloat16).at[:, 0].set(slot_gate.astype(jnp.bfloat16))
     router_chunks = jnp.broadcast_to(
-        router_weight[0].reshape(local_experts, 1, capacity, chunk),
-        (local_experts, groups, capacity, chunk),
+        router_weight[0].reshape(1, local_experts * capacity, chunk),
+        (groups, local_experts * capacity, chunk),
     ).reshape(total_rows, chunk)
     payload = jnp.concatenate([token_rows, router_chunks, gate_cols], axis=1)
     arrived = lax.all_to_all(
-        payload.reshape(local_experts, groups, capacity, -1),
+        payload.reshape(groups, local_experts * capacity, -1),
         "expert",
-        split_axis=1,
-        concat_axis=1,
+        split_axis=0,
+        concat_axis=0,
         tiled=True,
     )
-    gate_in = arrived[..., width + chunk].reshape(local_experts, groups * capacity).astype(jnp.float32)
-    router_full = arrived[..., width : width + chunk].transpose(1, 0, 2, 3).reshape(expert_total, width)
-    rows_in = arrived[..., :width].reshape(local_experts, groups * capacity, width).astype(jnp.float32)
+    gate_in = arrived[..., width + chunk].reshape(groups, local_experts, capacity).astype(jnp.float32)
+    router_full = arrived[..., width : width + chunk].reshape(expert_total, width)
+    rows_in = arrived[..., :width].reshape(groups, local_experts, capacity, width).astype(jnp.float32)
+
+    next_pack = passed_along(jnp.concatenate([features, router_full], axis=0), "pipe", -1)
 
     pre_saved = saved_pre[0]
     gate_part = pre_saved[..., :hidden_width].astype(jnp.float32)
@@ -68,12 +65,15 @@
     expert_out = jnp.einsum(
         "jsf,jfd->jsd", hidden, weights, preferred_element_type=jnp.float32
     ).astype(jnp.bfloat16)
-    row_scores = jnp.sum(rows_in * lax.optimization_barrier(expert_out).astype(jnp.float32), axis=-1)
+    expert_out = lax.optimization_barrier(expert_out).reshape(local_experts, groups, capacity, width)
+    row_scores = jnp.sum(
+        rows_in * expert_out.transpose(1, 0, 2, 3).astype(jnp.float32), axis=-1
+    )
     returned = lax.all_to_all(
-        row_scores.reshape(local_experts, groups, capacity),
+        row_scores.reshape(groups, local_experts * capacity),
         "expert",
-        split_axis=1,
-        concat_axis=1,
+        split_axis=0,
+        concat_axis=0,
         tiled=True,
     )
     pair_scores = jnp.sum(
@@ -81,7 +81,9 @@
     ).reshape(tok_rows, top_count)
 
     scaled_rows = (gate_in[..., None] * rows_in).astype(jnp.bfloat16)
-    row_grad = jnp.einsum("jsd,jfd->jsf", scaled_rows, weights, preferred_element_type=jnp.float32)
+    row_grad = jnp.einsum(
+        "gjsd,jfd->jgsf", scaled_rows, weights, preferred_element_type=jnp.float32
+    ).reshape(local_experts, groups * capacity, hidden_width)
     gate_grad = row_grad * up_part * sigmoid_gate * (1.0 + gate_part * (1.0 - sigmoid_gate))
     up_grad = row_grad * silu_gate
     pre_grad = jnp.concatenate([gate_grad, up_grad], axis=-1).astype(jnp.bfloat16)
@@ -94,9 +96,9 @@
     logit_grad = jnp.sum(
         jnp.where(chosen, select_grad[:, :, None], jnp.float32(0.0)), axis=1
     ).astype(jnp.bfloat16)
-    router_part = jnp.dot(logit_grad, router_full, preferred_element_type=jnp.float32)
-    section_grad = (features.astype(jnp.float32) + router_part).astype(jnp.bfloat16)
-    outgoing = passed_along(section_grad, "pipe", -1)
+    next_logit_grad = passed_along(logit_grad, "pipe", -1)
+    router_part = jnp.dot(next_logit_grad, next_pack[tok_rows:], preferred_element_type=jnp.float32)
+    outgoing = (next_pack[:tok_rows].astype(jnp.float32) + router_part).astype(jnp.bfloat16)
     return (pre_grad[None], outgoing[None])
 
 

time: 182 us -> 198 us (1.088)
  the two profiles are of different devices: /device:TPU:6 before, /device:TPU:79 now
where the time goes in v5:
time: 198 us
  waiting for transfers between devices  129 us (65%)
  other arithmetic  23.4 us (12%)
  starting transfers between devices  17.9 us (9%)
  matrix products  17.7 us (9%)
  local copies, waits for them, and re-layouts  8.72 us (4%)
    all_to_all x1, waiting for transfers between devices, per_device(): lax.all_to_all(payload.reshape(groups, local_experts * capacity, -1), 'ex...  91.4 us
    ppermute x2, waiting for transfers between devices, passed_along(): lax.ppermute(value, axis, [(i, (i + by) % peers) for i in range(peers)])  36.1 us
    all_to_all x1, starting transfers between devices, per_device(): lax.all_to_all(payload.reshape(groups, local_experts * capacity, -1), 'ex...  8.82 us
    all_to_all x1, starting transfers between devices, per_device(): lax.all_to_all(row_scores.reshape(groups, local_experts * capacity), 'exp...  7.9 us
    dot_general x1, matrix products, per_device(): jnp.einsum('jsf,jfd->jsd', hidden, weights, preferred_element_type=jnp.fl...  6.73 us
    dot_general x1, matrix products, per_device(): jnp.einsum('gjsd,jfd->jgsf', scaled_rows, weights, preferred_element_type...  6.42 us
    reduce_sum x1, other arithmetic, per_device(): jnp.sum(rows_in * expert_out.transpose(1, 0, 2, 3).astype(jnp.float32), a...  4.44 us
    convert_element_type x1, other arithmetic, per_device(): expert_out.transpose(1, 0, 2, 3).astype(jnp.float32)  4.28 us
  transfers between devices with their start and end apart: 4, of which 3 were waited for; matrix products, arithmetic and copies ran while one was open for 9% of the time, Pallas kernels for 0%

profile of v5, /device:TPU:79, one launch (start us, length us, event | category | flops | bytes accessed | tf_op | source)
XLA Modules:
  0.0 197.9 jit_solution(6319372217343810556)
XLA Ops:
  0.6 0.6 compare_reduce_fusion
  1.3 0.7 convert_convert_fusion
  2.0 0.1 copy.54
  2.1 0.1 reshape.153
  2.2 0.7 add_select_fusion
  2.9 0.1 copy.53
  3.0 0.1 eq.43
  3.1 0.5 select_reduce_fusion.1
  3.6 0.7 convert_select_fusion
  4.2 0.2 reshape.158
  4.4 0.7 broadcast_in_dim.60
  5.2 1.9 fusion.7
  7.1 0.1 scatter.4.clone
  7.1 2.3 %convolution_convert_fusion = bf16[1024,2048]{1,0:T(8,128)(2,1)S(1)} fusion(pred[1024,128]{1,0:T(8,128)(4,1)S(1)} %fusion.7, bf16[1,128,2048]{2,1,0:T(8,128)(2,1)} %param.9), kind=kOutput, calls=%fused_computation.21 | convolution fusion | flops 538968064 | bytes 4849664 | tf_op jit(solution)/shard_map/dot_general | solution.py:31
  9.5 2.4 %pad_maximum_fusion = bf16[32,32,2304]{2,1,0:T(8,128)(2,1)} fusion(bf16[32,32,128]{2,1,0:T(8,128)(2,1)S(1)} %bitcast.54, bf16[32,32,128]{2,1,0:T(8,128)(2,1)S(1)} %broadcast_in_dim.61, bf16[32,32,2048]{2,1,0:T(8,128)(2,1)S(1)} %bitcast.47), kind=kLoop, calls=%fused_computation.11 | loop fusion | flops 14155776 | bytes 9437184 | tf_op jit(solution)/shard_map/concatenate | solution.py:44
  11.8 8.8 %all-to-all-start = ((bf16[32,32,2304]{2,1,0:T(8,128)(2,1)}), bf16[32,32,2304]{2,1,0:T(8,128)(2,1)}, u32[]{:S(2)}, u32[]{:S(2)}) async-start(bf16[32,32,2304]{2,1,0:T(8,128)(2,1)} %pad_maximum_fusion), calls=%async_computation | async-start | bytes 9437184 | tf_op jit(solution)/shard_map/all_to_all | solution.py:45
  20.7 0.1 copy.59
  20.8 6.7 %fusion.8 = bf16[2,512,2048]{2,1,0:T(8,128)(2,1)S(1)} fusion(bf16[1,2,768,2048]{3,2,1,0:T(8,128)(2,1)} %param.14, bf16[2,512,1536]{2,1,0:T(8,128)(2,1)S(1)} %bitcast.51), kind=kOutput, calls=%fused_computation.20 | convolution fusion | flops 3229614080 | bytes 13631488 | tf_op jit(solution)/shard_map/jsf,jfd->jsd/dot_general | solution.py:65
  27.5 4.3 %bitcast_convert_fusion = f32[2,32,16,2048]{3,2,1,0:T(8,128)} fusion(bf16[2,512,2048]{2,1,0:T(8,128)(2,1)S(1)} %fusion.8), kind=kLoop, calls=%fused_computation.48 | loop fusion | flops 2097152 | bytes 12582912 | tf_op jit(solution)/shard_map/convert_element_type | solution.py:70
  31.8 91.4 %all-to-all-done = bf16[32,32,2304]{2,1,0:T(8,128)(2,1)} async-done(((bf16[32,32,2304]{2,1,0:T(8,128)(2,1)}), bf16[32,32,2304]{2,1,0:T(8,128)(2,1)}, u32[]{:S(2)}, u32[]{:S(2)}) %all-to-all-start) | async-done | bytes 4718624 | tf_op jit(solution)/shard_map/all_to_all | solution.py:45
  123.2 1.0 slice.42
  124.2 0.4 copy.65
  124.6 0.1 copy.57
  124.7 6.4 %fusion.2 = f32[2,32,16,768]{3,2,1,0:T(8,128)S(1)} fusion(bf16[1,2,768,2048]{3,2,1,0:T(8,128)(2,1)} %param.14, f32[32,2,16]{2,1,0:T(2,128)S(1)} %copy.57, bf16[32,32,2304]{2,1,0:T(8,128)(2,1)} %all-to-all-done), kind=kOutput, calls=%fused_computation.4 | convolution fusion | flops 3227516928 | bytes 13635584 | tf_op jit(solution)/shard_map/gjsd,jfd->jgsf/dot_general | solution.py:84
  131.1 1.8 fusion.13
  133.0 1.0 slice.46
  133.9 0.8 reshape.151
  134.8 2.5 %slice.43 = bf16[32,32,2048]{2,1,0:T(8,128)(2,1)S(1)} slice(bf16[32,32,2304]{2,1,0:T(8,128)(2,1)} %all-to-all-done), slice={[0:32], [0:32], [0:2048]} | slice | bytes 8388608 | tf_op jit(solution)/shard_map/slice | solution.py:54
  137.3 0.0 copy-start.2
  137.3 4.4 %fusion.1 = f32[32,2,16]{2,1,0:T(2,128)S(1)} fusion(bf16[32,2,16,2048]{3,2,1,0:T(8,128)(2,1)S(1)} %bitcast.48, f32[2,32,16,2048]{3,2,1,0:T(8,128)} %bitcast_convert_fusion), kind=kLoop, calls=%fused_computation.3 | loop fusion | flops 6290432 | bytes 12587008 | tf_op jit(solution)/shard_map/reduce_sum | solution.py:69
  141.7 0.1 copy.61
  141.8 0.7 copy.62
  142.5 7.9 %all-to-all-start.1 = ((f32[32,1,32]{2,1,0:T(1,128)}), f32[32,1,32]{2,1,0:T(1,128)S(1)}, u32[]{:S(2)}, u32[]{:S(2)}) async-start(f32[32,1,32]{2,1,0:T(1,128)} %copy.62), calls=%async_computation.1 | async-start | bytes 32768 | tf_op jit(solution)/shard_map/all_to_all | solution.py:72
  150.4 2.0 %pad_maximum_fusion.2 = bf16[192,2048]{1,0:T(8,128)(2,1)} fusion(bf16[64,2048]{1,0:T(8,128)(2,1)S(1)} %copy-done.2, bf16[128,2048]{1,0:T(8,128)(2,1)} %bitcast.53), kind=kLoop, calls=%fused_computation.35 | loop fusion | flops 1572864 | bytes 1572864 | tf_op jit(solution)/shard_map/concatenate | solution.py:56
  152.4 0.6 collective-permute-start
  152.9 1.9 all-to-all-done.1
  154.8 0.5 broadcast.88
  155.3 0.7 reduce.11
  156.0 0.1 broadcast_in_dim.64
  156.1 0.5 select_reduce_fusion
  156.6 0.1 reshape.152
  156.7 0.1 fusion.27
  156.8 0.1 bitcast_multiply_fusion.1
  157.0 0.1 select_reduce_fusion.2
  157.0 0.6 collective-permute-start.1
  157.6 1.9 pad_maximum_fusion.1
  159.6 36.1 %collective-permute-done.1 = bf16[128,64]{0,1:T(8,128)(2,1)S(1)} collective-permute-done((bf16[128,64]{0,1:T(8,128)(2,1)S(1)}, bf16[128,64]{0,1:T(8,128)(2,1)S(1)}, u32[]{:S(2)}, u32[]{:S(2)}) %collective-permute-start.1) | collective-permute-done | bytes 16416 | tf_op jit(solution)/shard_map/ppermute | solution.py:9
  195.6 2.2 %fusion.22 = bf16[1,128,2048]{2,1,0:T(8,128)(2,1)} fusion(bf16[192,2048]{1,0:T(8,128)(2,1)} %collective-permute-done, bf16[128,64]{0,1:T(8,128)(2,1)S(1)} %collective-permute-done.1), kind=kOutput, calls=%fused_computation.36 | convolution fusion | flops 34340864 | bytes 1327104 | tf_op jit(solution)/shard_map/dot_general | solution.py:100
  (12 shorter events, 0.1 us)
Async XLA Ops:
  11.8 8.8 %copy-start.3 = (f32[1,128,8]{1,2,0:T(8,128)S(1)}, f32[1,128,8]{1,2,0:T(8,128)}, u32[]{:S(2)}) copy-start(f32[1,128,8]{1,2,0:T(8,128)} %param.12) | copy-start | bytes 12292
  11.8 8.9 %copy-start = (bf16[1,2,512,1536]{3,2,1,0:T(8,128)(2,1)S(1)}, bf16[1,2,512,1536]{3,2,1,0:T(8,128)(2,1)}, u32[]{:S(2)}) copy-start(bf16[1,2,512,1536]{3,2,1,0:T(8,128)(2,1)} %param.13) | copy-start | bytes 9437188
  11.8 111.4 %all-to-all-start = ((bf16[32,32,2304]{2,1,0:T(8,128)(2,1)}), bf16[32,32,2304]{2,1,0:T(8,128)(2,1)}, u32[]{:S(2)}, u32[]{:S(2)}) async-start(bf16[32,32,2304]{2,1,0:T(8,128)(2,1)} %pad_maximum_fusion), calls=%async_computation | async-start | bytes 9437184 | tf_op jit(solution)/shard_map/all_to_all | solution.py:45
  124.7 6.4 %copy-start.1 = (bf16[1,2,512,1536]{3,2,1,0:T(8,128)(2,1)S(1)}, bf16[1,2,512,1536]{3,2,1,0:T(8,128)(2,1)}, u32[]{:S(2)}) copy-start(bf16[1,2,512,1536]{3,2,1,0:T(8,128)(2,1)} %param.13) | copy-start | bytes 9437188
  137.3 13.1 %copy-start.2 = (bf16[64,2048]{1,0:T(8,128)(2,1)S(1)}, bf16[64,2048]{1,0:T(8,128)(2,1)}, u32[]{:S(2)}) copy-start(bf16[64,2048]{1,0:T(8,128)(2,1)} %reshape.151) | copy-start | bytes 786436
  137.3 19.7 %copy-start.4 = (s32[1,128,8]{1,2,0:T(8,128)S(1)}, s32[1,128,8]{1,2,0:T(8,128)}, u32[]{:S(2)}) copy-start(s32[1,128,8]{1,2,0:T(8,128)} %param.10) | copy-start | bytes 12292
  142.5 12.3 %all-to-all-start.1 = ((f32[32,1,32]{2,1,0:T(1,128)}), f32[32,1,32]{2,1,0:T(1,128)S(1)}, u32[]{:S(2)}, u32[]{:S(2)}) async-start(f32[32,1,32]{2,1,0:T(1,128)} %copy.62), calls=%async_computation.1 | async-start | bytes 32768 | tf_op jit(solution)/shard_map/all_to_all | solution.py:72
  152.4 43.3 %collective-permute-start = (bf16[192,2048]{1,0:T(8,128)(2,1)}, bf16[192,2048]{1,0:T(8,128)(2,1)}, u32[]{:S(2)}, u32[]{:S(2)}) collective-permute-start(bf16[192,2048]{1,0:T(8,128)(2,1)} %pad_maximum_fusion.2), channel_id=1, source_target_pairs={{0,224},{32,0},{64,32},{96,64},{128,96},{160,128},{192,160},{224,1... | collective-permute-start | bytes 2359304 | tf_op jit(solution)/shard_map/ppermute | solution.py:9
  157.0 38.6 %collective-permute-start.1 = (bf16[128,64]{0,1:T(8,128)(2,1)S(1)}, bf16[128,64]{0,1:T(8,128)(2,1)S(1)}, u32[]{:S(2)}, u32[]{:S(2)}) collective-permute-start(bf16[128,64]{0,1:T(8,128)(2,1)S(1)} %select_reduce_fusion.2), channel_id=1, source_target_pairs={{0,224},{32,0},{64,32},{96,64},{128,96},{160,128},{192,160},{224,1... | collective-permute-start | bytes 49160 | tf_op jit(solution)/shard_map/ppermute | solution.py:9

commit v6 on v5

--- a/solution.py
+++ b/solution.py
@@ -53,8 +53,6 @@
     router_full = arrived[..., width : width + chunk].reshape(expert_total, width)
     rows_in = arrived[..., :width].reshape(groups, local_experts, capacity, width).astype(jnp.float32)
 
-    next_pack = passed_along(jnp.concatenate([features, router_full], axis=0), "pipe", -1)
-
     pre_saved = saved_pre[0]
     gate_part = pre_saved[..., :hidden_width].astype(jnp.float32)
     up_part = pre_saved[..., hidden_width:].astype(jnp.float32)
@@ -96,9 +94,9 @@
     logit_grad = jnp.sum(
         jnp.where(chosen, select_grad[:, :, None], jnp.float32(0.0)), axis=1
     ).astype(jnp.bfloat16)
-    next_logit_grad = passed_along(logit_grad, "pipe", -1)
-    router_part = jnp.dot(next_logit_grad, next_pack[tok_rows:], preferred_element_type=jnp.float32)
-    outgoing = (next_pack[:tok_rows].astype(jnp.float32) + router_part).astype(jnp.bfloat16)
+    router_part = jnp.dot(logit_grad, router_full, preferred_element_type=jnp.float32)
+    section_grad = (features.astype(jnp.float32) + router_part).astype(jnp.bfloat16)
+    outgoing = passed_along(section_grad, "pipe", -1)
     return (pre_grad[None], outgoing[None])
 
 

time: 198 us -> 186 us (0.939)
  waiting for transfers between devices: 129 us -> 117 us
  other arithmetic: 23.4 us -> 19.1 us
  local copies, waits for them, and re-layouts: 8.72 us -> 11.7 us
    ppermute x2 -> x1, waiting for transfers between devices: 36.1 us -> 25.6 us  [passed_along(): lax.ppermute(value, axis, [(i, (i + by) % peers) for i in range(peers)])]
    reduce_sum x1, other arithmetic: 4.44 us -> 0.89 us  [per_device(): jnp.sum(rows_in * expert_out.transpose(1, 0, 2, 3).astype(jnp.float32), a...]
    dot_general x1, matrix products: 6.42 us -> 9.19 us  [per_device(): jnp.einsum('gjsd,jfd->jgsf', scaled_rows, weights, preferred_element_type...]
    unnamed x12 -> x11, local copies, waits for them, and re-layouts: 0.51 us -> 3.27 us
    concatenate x1 -> x0, other arithmetic: 1.98 us -> none  [per_device(): jnp.concatenate([features, router_full], axis=0)]
  transfers between devices with their start and end apart: 4 -> 3, of which waited for: 3 -> 2; matrix products, arithmetic and copies ran while one was open for 9% -> 15% of each run, Pallas kernels for 0% -> 0%
where the time goes in v6:
time: 186 us
  waiting for transfers between devices  117 us (63%)
  matrix products  19.6 us (11%)
  other arithmetic  19.1 us (10%)
  starting transfers between devices  17.4 us (9%)
  local copies, waits for them, and re-layouts  11.7 us (6%)
    all_to_all x1, waiting for transfers between devices, per_device(): lax.all_to_all(payload.reshape(groups, local_experts * capacity, -1), 'ex...  91.4 us
    ppermute x1, waiting for transfers between devices, passed_along(): lax.ppermute(value, axis, [(i, (i + by) % peers) for i in range(peers)])  25.6 us
    dot_general x1, matrix products, per_device(): jnp.einsum('gjsd,jfd->jgsf', scaled_rows, weights, preferred_element_type...  9.19 us
    all_to_all x1, starting transfers between devices, per_device(): lax.all_to_all(payload.reshape(groups, local_experts * capacity, -1), 'ex...  8.82 us
    all_to_all x1, starting transfers between devices, per_device(): lax.all_to_all(row_scores.reshape(groups, local_experts * capacity), 'exp...  7.91 us
    dot_general x1, matrix products, per_device(): jnp.einsum('jsf,jfd->jsd', hidden, weights, preferred_element_type=jnp.fl...  6.7 us
    another operation x3, other arithmetic  4.31 us
    convert_element_type x1, other arithmetic, per_device(): expert_out.transpose(1, 0, 2, 3).astype(jnp.float32)  4.28 us
  transfers between devices with their start and end apart: 3, of which 2 were waited for; matrix products, arithmetic and copies ran while one was open for 15% of the time, Pallas kernels for 0%

profile of v6, /device:TPU:79, one launch (start us, length us, event | category | flops | bytes accessed | tf_op | source)
XLA Modules:
  0.0 185.7 jit_solution(10418326336567123186)
XLA Ops:
  0.6 0.6 compare_reduce_fusion
  1.3 0.7 convert_convert_fusion
  2.0 0.1 copy.53
  2.1 0.1 reshape.153
  2.2 0.7 add_select_fusion
  2.9 0.1 copy.52
  3.0 0.1 eq.43
  3.1 0.5 select_reduce_fusion.1
  3.6 0.7 convert_select_fusion
  4.2 0.2 reshape.158
  4.4 0.7 broadcast_in_dim.60
  5.2 1.9 %fusion.7 = pred[1024,128]{1,0:T(8,128)(4,1)S(1)} fusion(s32[128,8]{0,1:T(8,128)S(1)} %bitcast.57), kind=kLoop, calls=%fused_computation.17 | loop fusion | flops 1966080 | bytes 135168 | tf_op jit(solution)/shard_map/reduce_or | solution.py:30
  7.1 0.1 scatter.4.clone
  7.1 2.3 %convolution_convert_fusion = bf16[1024,2048]{1,0:T(8,128)(2,1)S(1)} fusion(pred[1024,128]{1,0:T(8,128)(4,1)S(1)} %fusion.7, bf16[1,128,2048]{2,1,0:T(8,128)(2,1)} %param.9), kind=kOutput, calls=%fused_computation.21 | convolution fusion | flops 538968064 | bytes 4849664 | tf_op jit(solution)/shard_map/dot_general | solution.py:31
  9.5 2.4 %pad_maximum_fusion = bf16[32,32,2304]{2,1,0:T(8,128)(2,1)} fusion(bf16[32,32,128]{2,1,0:T(8,128)(2,1)S(1)} %bitcast.54, bf16[32,32,128]{2,1,0:T(8,128)(2,1)S(1)} %broadcast_in_dim.61, bf16[32,32,2048]{2,1,0:T(8,128)(2,1)S(1)} %bitcast.48), kind=kLoop, calls=%fused_computation.11 | loop fusion | flops 14155776 | bytes 9437184 | tf_op jit(solution)/shard_map/concatenate | solution.py:44
  11.8 8.8 %all-to-all-start = ((bf16[32,32,2304]{2,1,0:T(8,128)(2,1)}), bf16[32,32,2304]{2,1,0:T(8,128)(2,1)}, u32[]{:S(2)}, u32[]{:S(2)}) async-start(bf16[32,32,2304]{2,1,0:T(8,128)(2,1)} %pad_maximum_fusion), calls=%async_computation | async-start | bytes 9437184 | tf_op jit(solution)/shard_map/all_to_all | solution.py:45
  20.7 0.1 copy.58
  20.8 6.7 %fusion.8 = bf16[2,512,2048]{2,1,0:T(8,128)(2,1)S(1)} fusion(bf16[1,2,768,2048]{3,2,1,0:T(8,128)(2,1)} %param.14, bf16[2,512,1536]{2,1,0:T(8,128)(2,1)S(1)} %bitcast.52), kind=kOutput, calls=%fused_computation.20 | convolution fusion | flops 3229614080 | bytes 13631488 | tf_op jit(solution)/shard_map/jsf,jfd->jsd/dot_general | solution.py:63
  27.5 4.3 %bitcast_convert_fusion = f32[2,32,16,2048]{3,2,1,0:T(8,128)} fusion(bf16[2,512,2048]{2,1,0:T(8,128)(2,1)S(1)} %fusion.8), kind=kLoop, calls=%fused_computation.47 | loop fusion | flops 2097152 | bytes 12582912 | tf_op jit(solution)/shard_map/convert_element_type | solution.py:68
  31.8 91.4 %all-to-all-done = bf16[32,32,2304]{2,1,0:T(8,128)(2,1)} async-done(((bf16[32,32,2304]{2,1,0:T(8,128)(2,1)}), bf16[32,32,2304]{2,1,0:T(8,128)(2,1)}, u32[]{:S(2)}, u32[]{:S(2)}) %all-to-all-start) | async-done | bytes 4718624 | tf_op jit(solution)/shard_map/all_to_all | solution.py:45
  123.2 1.0 slice.34
  124.2 0.4 copy.64
  124.6 0.1 copy.56
  124.7 2.7 %slice.35 = bf16[32,32,2048]{2,1,0:T(8,128)(2,1)S(1)} slice(bf16[32,32,2304]{2,1,0:T(8,128)(2,1)} %all-to-all-done), slice={[0:32], [0:32], [0:2048]} | slice | bytes 8388608 | tf_op jit(solution)/shard_map/slice | solution.py:54
  127.3 2.0 %copy-done = f32[2,32,16,2048]{3,2,1,0:T(8,128)S(1)} copy-done((f32[2,32,16,2048]{3,2,1,0:T(8,128)S(1)}, f32[2,32,16,2048]{3,2,1,0:T(8,128)}, u32[]{:S(2)}) %copy-start) | copy-done | bytes 8388632
  129.3 0.9 fusion.1
  130.2 0.1 copy.60
  130.3 0.7 copy.61
  131.0 7.9 %all-to-all-start.1 = ((f32[32,1,32]{2,1,0:T(1,128)}), f32[32,1,32]{2,1,0:T(1,128)S(1)}, u32[]{:S(2)}, u32[]{:S(2)}) async-start(f32[32,1,32]{2,1,0:T(1,128)} %copy.61), calls=%async_computation.1 | async-start | bytes 32768 | tf_op jit(solution)/shard_map/all_to_all | solution.py:70
  138.9 0.0 copy-start.3
  138.9 9.2 %fusion.2 = f32[2,32,16,768]{3,2,1,0:T(8,128)} fusion(bf16[1,2,768,2048]{3,2,1,0:T(8,128)(2,1)} %param.14, f32[32,2,16]{2,1,0:T(2,128)S(1)} %copy.56, bf16[32,32,2304]{2,1,0:T(8,128)(2,1)} %all-to-all-done), kind=kOutput, calls=%fused_computation.4 | convolution fusion | flops 3227516928 | bytes 13635584 | tf_op jit(solution)/shard_map/gjsd,jfd->jgsf/dot_general | solution.py:82
  148.1 1.0 slice.38
  149.1 0.8 reshape.152
  149.9 0.0 all-to-all-done.1
  149.9 0.6 broadcast.88
  150.5 0.7 reduce.11
  151.2 0.1 broadcast_in_dim.64
  151.3 0.5 select_reduce_fusion
  151.8 0.1 reshape.151
  151.9 0.1 fusion.24
  152.0 0.1 bitcast_multiply_fusion.1
  152.2 0.1 select_reduce_fusion.2
  152.2 1.4 fusion.20
  153.7 0.6 collective-permute-start
  154.3 3.0 %fusion.13 = (bf16[2,512,768]{2,1,0:T(8,128)(2,1)S(1)}, bf16[2,512,768]{2,1,0:T(8,128)(2,1)S(1)}) fusion(f32[2,32,16,768]{3,2,1,0:T(8,128)} %fusion.2, bf16[2,512,1536]{2,1,0:T(8,128)(2,1)S(1)} %bitcast.53), kind=kLoop, calls=%fused_computation.24 | loop fusion | flops 11796480 | bytes 9437184 | tf_op jit(solution)/shard_map/convert.8
  157.3 1.9 %pad_maximum_fusion.1 = bf16[1,2,512,1536]{3,2,1,0:T(8,128)(2,1)} fusion(bf16[1,2,512,768]{3,2,1,0:T(8,128)(2,1)S(1)} %bitcast.51, bf16[1,2,512,768]{3,2,1,0:T(8,128)(2,1)S(1)} %bitcast.50), kind=kLoop, calls=%fused_computation.30 | loop fusion | flops 6291456 | bytes 6291456 | tf_op jit(solution)/shard_map/concatenate | solution.py:87
  159.2 25.6 %collective-permute-done = bf16[128,2048]{1,0:T(8,128)(2,1)S(1)} collective-permute-done((bf16[128,2048]{1,0:T(8,128)(2,1)S(1)}, bf16[128,2048]{1,0:T(8,128)(2,1)S(1)}, u32[]{:S(2)}, u32[]{:S(2)}) %collective-permute-start) | collective-permute-done | bytes 524320 | tf_op jit(solution)/shard_map/ppermute | solution.py:9
  184.9 0.8 copy.70
  (8 shorter events, 0.1 us)
Async XLA Ops:
  11.8 8.8 %copy-start.2 = (f32[1,128,8]{1,2,0:T(8,128)S(1)}, f32[1,128,8]{1,2,0:T(8,128)}, u32[]{:S(2)}) copy-start(f32[1,128,8]{1,2,0:T(8,128)} %param.12) | copy-start | bytes 12292
  11.8 8.9 %copy-start.1 = (bf16[1,2,512,1536]{3,2,1,0:T(8,128)(2,1)S(1)}, bf16[1,2,512,1536]{3,2,1,0:T(8,128)(2,1)}, u32[]{:S(2)}) copy-start(bf16[1,2,512,1536]{3,2,1,0:T(8,128)(2,1)} %param.13) | copy-start | bytes 9437188
  11.8 111.4 %all-to-all-start = ((bf16[32,32,2304]{2,1,0:T(8,128)(2,1)}), bf16[32,32,2304]{2,1,0:T(8,128)(2,1)}, u32[]{:S(2)}, u32[]{:S(2)}) async-start(bf16[32,32,2304]{2,1,0:T(8,128)(2,1)} %pad_maximum_fusion), calls=%async_computation | async-start | bytes 9437184 | tf_op jit(solution)/shard_map/all_to_all | solution.py:45
  124.7 4.6 %copy-start = (f32[2,32,16,2048]{3,2,1,0:T(8,128)S(1)}, f32[2,32,16,2048]{3,2,1,0:T(8,128)}, u32[]{:S(2)}) copy-start(f32[2,32,16,2048]{3,2,1,0:T(8,128)} %bitcast_convert_fusion) | copy-start | bytes 25165828
  131.0 18.9 %all-to-all-start.1 = ((f32[32,1,32]{2,1,0:T(1,128)}), f32[32,1,32]{2,1,0:T(1,128)S(1)}, u32[]{:S(2)}, u32[]{:S(2)}) async-start(f32[32,1,32]{2,1,0:T(1,128)} %copy.61), calls=%async_computation.1 | async-start | bytes 32768 | tf_op jit(solution)/shard_map/all_to_all | solution.py:70
  138.9 13.3 %copy-start.3 = (s32[1,128,8]{1,2,0:T(8,128)S(1)}, s32[1,128,8]{1,2,0:T(8,128)}, u32[]{:S(2)}) copy-start(s32[1,128,8]{1,2,0:T(8,128)} %param.10) | copy-start | bytes 12292
  153.7 31.2 %collective-permute-start = (bf16[128,2048]{1,0:T(8,128)(2,1)S(1)}, bf16[128,2048]{1,0:T(8,128)(2,1)S(1)}, u32[]{:S(2)}, u32[]{:S(2)}) collective-permute-start(bf16[128,2048]{1,0:T(8,128)(2,1)S(1)} %fusion.20), channel_id=1, source_target_pairs={{0,224},{32,0},{64,32},{96,64},{128,96},{160,128},{192,160},{224,1... | collective-permute-start | bytes 1572872 | tf_op jit(solution)/shard_map/ppermute | solution.py:9

commit v7 on v5

--- a/solution.py
+++ b/solution.py
@@ -9,7 +9,7 @@
     return lax.ppermute(value, axis, [(i, (i + by) % peers) for i in range(peers)])
 
 
-def per_device(grad_out, expert_ids, slot_ids, gate_weights, saved_pre, down_weight, router_weight):
+def section_step(grad_out, expert_ids, slot_ids, gate_weights, saved_pre, down_weight, router_weight):
     groups = lax.axis_size("expert")
     local_experts = down_weight.shape[1]
     hidden_width = down_weight.shape[2]
@@ -113,6 +113,4 @@
         P("pipe", "expert", None),
     )
     out_specs = (P("pipe", "expert", None, None), P("pipe", "expert", None))
-    return jax.shard_map(
-        per_device, mesh=mesh, in_specs=in_specs, out_specs=out_specs, check_vma=False
-    )
+    return jax.shard_map(section_step, mesh=mesh, in_specs=in_specs, out_specs=out_specs, check_vma=False)

time: 198 us -> 198 us (level)
  no operation moved by 1% of the time
where the time goes in v7:
time: 198 us
  waiting for transfers between devices  129 us (65%)
  other arithmetic  23.4 us (12%)
  starting transfers between devices  17.9 us (9%)
  matrix products  17.7 us (9%)
  local copies, waits for them, and re-layouts  8.72 us (4%)
    all_to_all x1, waiting for transfers between devices, section_step(): lax.all_to_all(payload.reshape(groups, local_experts * capacity, -1), 'ex...  91.4 us
    ppermute x2, waiting for transfers between devices, passed_along(): lax.ppermute(value, axis, [(i, (i + by) % peers) for i in range(peers)])  36.1 us
    all_to_all x1, starting transfers between devices, section_step(): lax.all_to_all(payload.reshape(groups, local_experts * capacity, -1), 'ex...  8.82 us
    all_to_all x1, starting transfers between devices, section_step(): lax.all_to_all(row_scores.reshape(groups, local_experts * capacity), 'exp...  7.9 us
    dot_general x1, matrix products, section_step(): jnp.einsum('jsf,jfd->jsd', hidden, weights, preferred_element_type=jnp.fl...  6.73 us
    dot_general x1, matrix products, section_step(): jnp.einsum('gjsd,jfd->jgsf', scaled_rows, weights, preferred_element_type...  6.42 us
    reduce_sum x1, other arithmetic, section_step(): jnp.sum(rows_in * expert_out.transpose(1, 0, 2, 3).astype(jnp.float32), a...  4.44 us
    convert_element_type x1, other arithmetic, section_step(): expert_out.transpose(1, 0, 2, 3).astype(jnp.float32)  4.28 us
  transfers between devices with their start and end apart: 4, of which 3 were waited for; matrix products, arithmetic and copies ran while one was open for 9% of the time, Pallas kernels for 0%

profile of v7, /device:TPU:79, one launch (start us, length us, event | category | flops | bytes accessed | tf_op | source)
XLA Modules:
  0.0 197.9 jit_solution(6319372217343810556)
XLA Ops:
  0.6 0.6 compare_reduce_fusion
  1.3 0.7 convert_convert_fusion
  2.0 0.1 copy.54
  2.1 0.1 reshape.153
  2.2 0.7 add_select_fusion
  2.9 0.1 copy.53
  3.0 0.1 eq.43
  3.1 0.5 select_reduce_fusion.1
  3.6 0.7 convert_select_fusion
  4.2 0.2 reshape.158
  4.4 0.7 broadcast_in_dim.60
  5.2 1.9 fusion.7
  7.1 0.1 scatter.4.clone
  7.1 2.3 %convolution_convert_fusion = bf16[1024,2048]{1,0:T(8,128)(2,1)S(1)} fusion(pred[1024,128]{1,0:T(8,128)(4,1)S(1)} %fusion.7, bf16[1,128,2048]{2,1,0:T(8,128)(2,1)} %param.9), kind=kOutput, calls=%fused_computation.21 | convolution fusion | flops 538968064 | bytes 4849664 | tf_op jit(solution)/shard_map/dot_general | solution.py:31
  9.5 2.4 %pad_maximum_fusion = bf16[32,32,2304]{2,1,0:T(8,128)(2,1)} fusion(bf16[32,32,128]{2,1,0:T(8,128)(2,1)S(1)} %bitcast.54, bf16[32,32,128]{2,1,0:T(8,128)(2,1)S(1)} %broadcast_in_dim.61, bf16[32,32,2048]{2,1,0:T(8,128)(2,1)S(1)} %bitcast.47), kind=kLoop, calls=%fused_computation.11 | loop fusion | flops 14155776 | bytes 9437184 | tf_op jit(solution)/shard_map/concatenate | solution.py:44
  11.8 8.8 %all-to-all-start = ((bf16[32,32,2304]{2,1,0:T(8,128)(2,1)}), bf16[32,32,2304]{2,1,0:T(8,128)(2,1)}, u32[]{:S(2)}, u32[]{:S(2)}) async-start(bf16[32,32,2304]{2,1,0:T(8,128)(2,1)} %pad_maximum_fusion), calls=%async_computation | async-start | bytes 9437184 | tf_op jit(solution)/shard_map/all_to_all | solution.py:45
  20.7 0.1 copy.59
  20.8 6.7 %fusion.8 = bf16[2,512,2048]{2,1,0:T(8,128)(2,1)S(1)} fusion(bf16[1,2,768,2048]{3,2,1,0:T(8,128)(2,1)} %param.14, bf16[2,512,1536]{2,1,0:T(8,128)(2,1)S(1)} %bitcast.51), kind=kOutput, calls=%fused_computation.20 | convolution fusion | flops 3229614080 | bytes 13631488 | tf_op jit(solution)/shard_map/jsf,jfd->jsd/dot_general | solution.py:65
  27.5 4.3 %bitcast_convert_fusion = f32[2,32,16,2048]{3,2,1,0:T(8,128)} fusion(bf16[2,512,2048]{2,1,0:T(8,128)(2,1)S(1)} %fusion.8), kind=kLoop, calls=%fused_computation.48 | loop fusion | flops 2097152 | bytes 12582912 | tf_op jit(solution)/shard_map/convert_element_type | solution.py:70
  31.8 91.4 %all-to-all-done = bf16[32,32,2304]{2,1,0:T(8,128)(2,1)} async-done(((bf16[32,32,2304]{2,1,0:T(8,128)(2,1)}), bf16[32,32,2304]{2,1,0:T(8,128)(2,1)}, u32[]{:S(2)}, u32[]{:S(2)}) %all-to-all-start) | async-done | bytes 4718624 | tf_op jit(solution)/shard_map/all_to_all | solution.py:45
  123.2 1.0 slice.42
  124.2 0.4 copy.65
  124.6 0.1 copy.57
  124.7 6.4 %fusion.2 = f32[2,32,16,768]{3,2,1,0:T(8,128)S(1)} fusion(bf16[1,2,768,2048]{3,2,1,0:T(8,128)(2,1)} %param.14, f32[32,2,16]{2,1,0:T(2,128)S(1)} %copy.57, bf16[32,32,2304]{2,1,0:T(8,128)(2,1)} %all-to-all-done), kind=kOutput, calls=%fused_computation.4 | convolution fusion | flops 3227516928 | bytes 13635584 | tf_op jit(solution)/shard_map/gjsd,jfd->jgsf/dot_general | solution.py:84
  131.1 1.8 fusion.13
  133.0 1.0 slice.46
  133.9 0.8 reshape.151
  134.8 2.5 %slice.43 = bf16[32,32,2048]{2,1,0:T(8,128)(2,1)S(1)} slice(bf16[32,32,2304]{2,1,0:T(8,128)(2,1)} %all-to-all-done), slice={[0:32], [0:32], [0:2048]} | slice | bytes 8388608 | tf_op jit(solution)/shard_map/slice | solution.py:54
  137.3 0.0 copy-start.2
  137.3 4.4 %fusion.1 = f32[32,2,16]{2,1,0:T(2,128)S(1)} fusion(bf16[32,2,16,2048]{3,2,1,0:T(8,128)(2,1)S(1)} %bitcast.48, f32[2,32,16,2048]{3,2,1,0:T(8,128)} %bitcast_convert_fusion), kind=kLoop, calls=%fused_computation.3 | loop fusion | flops 6290432 | bytes 12587008 | tf_op jit(solution)/shard_map/reduce_sum | solution.py:69
  141.7 0.1 copy.61
  141.8 0.7 copy.62
  142.5 7.9 %all-to-all-start.1 = ((f32[32,1,32]{2,1,0:T(1,128)}), f32[32,1,32]{2,1,0:T(1,128)S(1)}, u32[]{:S(2)}, u32[]{:S(2)}) async-start(f32[32,1,32]{2,1,0:T(1,128)} %copy.62), calls=%async_computation.1 | async-start | bytes 32768 | tf_op jit(solution)/shard_map/all_to_all | solution.py:72
  150.4 2.0 %pad_maximum_fusion.2 = bf16[192,2048]{1,0:T(8,128)(2,1)} fusion(bf16[64,2048]{1,0:T(8,128)(2,1)S(1)} %copy-done.2, bf16[128,2048]{1,0:T(8,128)(2,1)} %bitcast.53), kind=kLoop, calls=%fused_computation.35 | loop fusion | flops 1572864 | bytes 1572864 | tf_op jit(solution)/shard_map/concatenate | solution.py:56
  152.4 0.6 collective-permute-start
  152.9 1.9 all-to-all-done.1
  154.8 0.5 broadcast.88
  155.3 0.7 reduce.11
  156.0 0.1 broadcast_in_dim.64
  156.1 0.5 select_reduce_fusion
  156.6 0.1 reshape.152
  156.7 0.1 fusion.27
  156.8 0.1 bitcast_multiply_fusion.1
  157.0 0.1 select_reduce_fusion.2
  157.0 0.6 collective-permute-start.1
  157.6 1.9 pad_maximum_fusion.1
  159.6 36.1 %collective-permute-done.1 = bf16[128,64]{0,1:T(8,128)(2,1)S(1)} collective-permute-done((bf16[128,64]{0,1:T(8,128)(2,1)S(1)}, bf16[128,64]{0,1:T(8,128)(2,1)S(1)}, u32[]{:S(2)}, u32[]{:S(2)}) %collective-permute-start.1) | collective-permute-done | bytes 16416 | tf_op jit(solution)/shard_map/ppermute | solution.py:9
  195.6 2.2 %fusion.22 = bf16[1,128,2048]{2,1,0:T(8,128)(2,1)} fusion(bf16[192,2048]{1,0:T(8,128)(2,1)} %collective-permute-done, bf16[128,64]{0,1:T(8,128)(2,1)S(1)} %collective-permute-done.1), kind=kOutput, calls=%fused_computation.36 | convolution fusion | flops 34340864 | bytes 1327104 | tf_op jit(solution)/shard_map/dot_general | solution.py:100
  (12 shorter events, 0.1 us)
Async XLA Ops:
  11.8 8.8 %copy-start.3 = (f32[1,128,8]{1,2,0:T(8,128)S(1)}, f32[1,128,8]{1,2,0:T(8,128)}, u32[]{:S(2)}) copy-start(f32[1,128,8]{1,2,0:T(8,128)} %param.12) | copy-start | bytes 12292
  11.8 8.9 %copy-start = (bf16[1,2,512,1536]{3,2,1,0:T(8,128)(2,1)S(1)}, bf16[1,2,512,1536]{3,2,1,0:T(8,128)(2,1)}, u32[]{:S(2)}) copy-start(bf16[1,2,512,1536]{3,2,1,0:T(8,128)(2,1)} %param.13) | copy-start | bytes 9437188
  11.8 111.4 %all-to-all-start = ((bf16[32,32,2304]{2,1,0:T(8,128)(2,1)}), bf16[32,32,2304]{2,1,0:T(8,128)(2,1)}, u32[]{:S(2)}, u32[]{:S(2)}) async-start(bf16[32,32,2304]{2,1,0:T(8,128)(2,1)} %pad_maximum_fusion), calls=%async_computation | async-start | bytes 9437184 | tf_op jit(solution)/shard_map/all_to_all | solution.py:45
  124.7 6.4 %copy-start.1 = (bf16[1,2,512,1536]{3,2,1,0:T(8,128)(2,1)S(1)}, bf16[1,2,512,1536]{3,2,1,0:T(8,128)(2,1)}, u32[]{:S(2)}) copy-start(bf16[1,2,512,1536]{3,2,1,0:T(8,128)(2,1)} %param.13) | copy-start | bytes 9437188
  137.3 13.1 %copy-start.2 = (bf16[64,2048]{1,0:T(8,128)(2,1)S(1)}, bf16[64,2048]{1,0:T(8,128)(2,1)}, u32[]{:S(2)}) copy-start(bf16[64,2048]{1,0:T(8,128)(2,1)} %reshape.151) | copy-start | bytes 786436
  137.3 19.7 %copy-start.4 = (s32[1,128,8]{1,2,0:T(8,128)S(1)}, s32[1,128,8]{1,2,0:T(8,128)}, u32[]{:S(2)}) copy-start(s32[1,128,8]{1,2,0:T(8,128)} %param.10) | copy-start | bytes 12292
  142.5 12.3 %all-to-all-start.1 = ((f32[32,1,32]{2,1,0:T(1,128)}), f32[32,1,32]{2,1,0:T(1,128)S(1)}, u32[]{:S(2)}, u32[]{:S(2)}) async-start(f32[32,1,32]{2,1,0:T(1,128)} %copy.62), calls=%async_computation.1 | async-start | bytes 32768 | tf_op jit(solution)/shard_map/all_to_all | solution.py:72
  152.4 43.3 %collective-permute-start = (bf16[192,2048]{1,0:T(8,128)(2,1)}, bf16[192,2048]{1,0:T(8,128)(2,1)}, u32[]{:S(2)}, u32[]{:S(2)}) collective-permute-start(bf16[192,2048]{1,0:T(8,128)(2,1)} %pad_maximum_fusion.2), channel_id=1, source_target_pairs={{0,224},{32,0},{64,32},{96,64},{128,96},{160,128},{192,160},{224,1... | collective-permute-start | bytes 2359304 | tf_op jit(solution)/shard_map/ppermute | solution.py:9
  157.0 38.6 %collective-permute-start.1 = (bf16[128,64]{0,1:T(8,128)(2,1)S(1)}, bf16[128,64]{0,1:T(8,128)(2,1)S(1)}, u32[]{:S(2)}, u32[]{:S(2)}) collective-permute-start(bf16[128,64]{0,1:T(8,128)(2,1)S(1)} %select_reduce_fusion.2), channel_id=1, source_target_pairs={{0,224},{32,0},{64,32},{96,64},{128,96},{160,128},{192,160},{224,1... | collective-permute-start | bytes 49160 | tf_op jit(solution)/shard_map/ppermute | solution.py:9

commit v8 on v7

--- a/solution.py
+++ b/solution.py
@@ -37,8 +37,9 @@
     )
 
     gate_cols = jnp.zeros((total_rows, 128), jnp.bfloat16).at[:, 0].set(slot_gate.astype(jnp.bfloat16))
+    next_router = passed_along(router_weight[0], "pipe", -1)
     router_chunks = jnp.broadcast_to(
-        router_weight[0].reshape(1, local_experts * capacity, chunk),
+        next_router.reshape(1, local_experts * capacity, chunk),
         (groups, local_experts * capacity, chunk),
     ).reshape(total_rows, chunk)
     payload = jnp.concatenate([token_rows, router_chunks, gate_cols], axis=1)
@@ -53,7 +54,8 @@
     router_full = arrived[..., width : width + chunk].reshape(expert_total, width)
     rows_in = arrived[..., :width].reshape(groups, local_experts, capacity, width).astype(jnp.float32)
 
-    next_pack = passed_along(jnp.concatenate([features, router_full], axis=0), "pipe", -1)
+    held, router_full = lax.optimization_barrier((features, router_full))
+    next_features = passed_along(held, "pipe", -1)
 
     pre_saved = saved_pre[0]
     gate_part = pre_saved[..., :hidden_width].astype(jnp.float32)
@@ -97,8 +99,8 @@
         jnp.where(chosen, select_grad[:, :, None], jnp.float32(0.0)), axis=1
     ).astype(jnp.bfloat16)
     next_logit_grad = passed_along(logit_grad, "pipe", -1)
-    router_part = jnp.dot(next_logit_grad, next_pack[tok_rows:], preferred_element_type=jnp.float32)
-    outgoing = (next_pack[:tok_rows].astype(jnp.float32) + router_part).astype(jnp.bfloat16)
+    router_part = jnp.dot(next_logit_grad, router_full, preferred_element_type=jnp.float32)
+    outgoing = (next_features.astype(jnp.float32) + router_part).astype(jnp.bfloat16)
     return (pre_grad[None], outgoing[None])
 
 

time: 198 us -> 188 us (0.949)
  waiting for transfers between devices: 129 us -> 117 us
  other arithmetic: 23.4 us -> 20.9 us
  local copies, waits for them, and re-layouts: 8.72 us -> 11 us
    ppermute x2 -> x3, waiting for transfers between devices: 36.1 us -> 25.8 us  [passed_along(): lax.ppermute(value, axis, [(i, (i + by) % peers) for i in range(peers)])]
    reduce_sum x1, other arithmetic: 4.44 us -> 0.89 us  [section_step(): jnp.sum(rows_in * expert_out.transpose(1, 0, 2, 3).astype(jnp.float32), a...]
    concatenate x1, other arithmetic: 2.36 us -> 4.76 us  [section_step(): payload = jnp.concatenate([token_rows, router_chunks, gate_cols], axis=1)]
    concatenate x1 -> x0, other arithmetic: 1.98 us -> none  [section_step(): jnp.concatenate([features, router_full], axis=0)]
  transfers between devices with their start and end apart: 4 -> 5, of which waited for: 3 -> 2; matrix products, arithmetic and copies ran while one was open for 9% -> 20% of each run, Pallas kernels for 0% -> 0%
where the time goes in v8:
time: 188 us
  waiting for transfers between devices  117 us (62%)
  other arithmetic  20.9 us (11%)
  matrix products  19.5 us (10%)
  starting transfers between devices  18.2 us (10%)
  local copies, waits for them, and re-layouts  11 us (6%)
    all_to_all x1, waiting for transfers between devices, section_step(): lax.all_to_all(payload.reshape(groups, local_experts * capacity, -1), 'ex...  91.4 us
    ppermute x3, waiting for transfers between devices, passed_along(): lax.ppermute(value, axis, [(i, (i + by) % peers) for i in range(peers)])  25.8 us
    all_to_all x1, starting transfers between devices, section_step(): lax.all_to_all(payload.reshape(groups, local_experts * capacity, -1), 'ex...  9.1 us
    all_to_all x1, starting transfers between devices, section_step(): lax.all_to_all(row_scores.reshape(groups, local_experts * capacity), 'exp...  7.92 us
    dot_general x1, matrix products, section_step(): jnp.einsum('jsf,jfd->jsd', hidden, weights, preferred_element_type=jnp.fl...  6.7 us
    dot_general x1, matrix products, section_step(): jnp.einsum('gjsd,jfd->jgsf', scaled_rows, weights, preferred_element_type...  6.41 us
    concatenate x1, other arithmetic, section_step(): payload = jnp.concatenate([token_rows, router_chunks, gate_cols], axis=1)  4.76 us
    convert_element_type x1, other arithmetic, section_step(): expert_out.transpose(1, 0, 2, 3).astype(jnp.float32)  4.28 us
  transfers between devices with their start and end apart: 5, of which 2 were waited for; matrix products, arithmetic and copies ran while one was open for 20% of the time, Pallas kernels for 0%

profile of v8, /device:TPU:79, one launch (start us, length us, event | category | flops | bytes accessed | tf_op | source)
XLA Modules:
  0.0 187.7 jit_solution(11555480196443979531)
XLA Ops:
  0.6 0.6 collective-permute-start
  1.3 0.6 compare_reduce_fusion
  1.9 0.7 convert_convert_fusion
  2.6 0.1 copy.53
  2.7 0.1 reshape.154
  2.8 0.7 add_select_fusion
  3.5 0.1 copy.52
  3.6 0.1 eq.43
  3.7 1.9 %fusion.7 = pred[1024,128]{1,0:T(8,128)(4,1)S(1)} fusion(s32[128,8]{0,1:T(8,128)S(1)} %bitcast.58), kind=kLoop, calls=%fused_computation.17 | loop fusion | flops 1966080 | bytes 135168 | tf_op jit(solution)/shard_map/reduce_or | solution.py:30
  5.6 0.5 select_reduce_fusion.1
  6.1 4.2 %convolution_convert_fusion = bf16[1024,2048]{1,0:T(8,128)(2,1)} fusion(pred[1024,128]{1,0:T(8,128)(4,1)S(1)} %fusion.7, bf16[1,128,2048]{2,1,0:T(8,128)(2,1)} %param.9), kind=kOutput, calls=%fused_computation.21 | convolution fusion | flops 538968064 | bytes 4849664 | tf_op jit(solution)/shard_map/dot_general | solution.py:31
  10.3 0.6 convert_select_fusion
  11.0 0.2 reshape.159
  11.2 0.1 scatter.4.clone
  11.3 4.8 %pad_maximum_fusion = bf16[32,32,2304]{2,1,0:T(8,128)(2,1)} fusion(bf16[32,32,128]{2,1,0:T(8,128)(2,1)S(1)} %bitcast.55, bf16[32,32,128]{2,1,0:T(8,128)(2,1)S(1)} %broadcast_in_dim.61, bf16[32,32,2048]{2,1,0:T(8,128)(2,1)} %bitcast.49), kind=kLoop, calls=%fused_computation.11 | loop fusion | flops 14155776 | bytes 9437184 | tf_op jit(solution)/shard_map/concatenate | solution.py:45
  16.1 9.1 %all-to-all-start = ((bf16[32,32,2304]{2,1,0:T(8,128)(2,1)}), bf16[32,32,2304]{2,1,0:T(8,128)(2,1)}, u32[]{:S(2)}, u32[]{:S(2)}) async-start(bf16[32,32,2304]{2,1,0:T(8,128)(2,1)} %pad_maximum_fusion), calls=%async_computation | async-start | bytes 9437184 | tf_op jit(solution)/shard_map/all_to_all | solution.py:46
  25.2 0.1 copy.58
  25.3 6.7 %fusion.8 = bf16[2,512,2048]{2,1,0:T(8,128)(2,1)S(1)} fusion(bf16[1,2,768,2048]{3,2,1,0:T(8,128)(2,1)} %param.14, bf16[2,512,1536]{2,1,0:T(8,128)(2,1)S(1)} %bitcast.53), kind=kOutput, calls=%fused_computation.20 | convolution fusion | flops 3229614080 | bytes 13631488 | tf_op jit(solution)/shard_map/jsf,jfd->jsd/dot_general | solution.py:67
  32.0 4.3 %bitcast_convert_fusion = f32[2,32,16,2048]{3,2,1,0:T(8,128)} fusion(bf16[2,512,2048]{2,1,0:T(8,128)(2,1)S(1)} %fusion.8), kind=kLoop, calls=%fused_computation.45 | loop fusion | flops 2097152 | bytes 12582912 | tf_op jit(solution)/shard_map/convert_element_type | solution.py:72
  36.3 91.4 %all-to-all-done = bf16[32,32,2304]{2,1,0:T(8,128)(2,1)} async-done(((bf16[32,32,2304]{2,1,0:T(8,128)(2,1)}), bf16[32,32,2304]{2,1,0:T(8,128)(2,1)}, u32[]{:S(2)}, u32[]{:S(2)}) %all-to-all-start) | async-done | bytes 4718624 | tf_op jit(solution)/shard_map/all_to_all | solution.py:46
  127.8 1.0 slice.34
  128.7 0.4 copy.64
  129.1 0.1 copy.56
  129.2 2.7 %slice.35 = bf16[32,32,2048]{2,1,0:T(8,128)(2,1)S(1)} slice(bf16[32,32,2304]{2,1,0:T(8,128)(2,1)} %all-to-all-done), slice={[0:32], [0:32], [0:2048]} | slice | bytes 8388608 | tf_op jit(solution)/shard_map/slice | solution.py:55
  131.9 2.0 %copy-done = f32[2,32,16,2048]{3,2,1,0:T(8,128)S(1)} copy-done((f32[2,32,16,2048]{3,2,1,0:T(8,128)S(1)}, f32[2,32,16,2048]{3,2,1,0:T(8,128)}, u32[]{:S(2)}) %copy-start) | copy-done | bytes 8388632
  133.9 0.9 fusion.1
  134.7 0.1 copy.60
  134.8 0.7 copy.61
  135.5 7.9 %all-to-all-start.1 = ((f32[32,1,32]{2,1,0:T(1,128)}), f32[32,1,32]{2,1,0:T(1,128)S(1)}, u32[]{:S(2)}, u32[]{:S(2)}) async-start(f32[32,1,32]{2,1,0:T(1,128)} %copy.61), calls=%async_computation.1 | async-start | bytes 32768 | tf_op jit(solution)/shard_map/all_to_all | solution.py:74
  143.4 0.0 copy-start.2
  143.4 6.4 %fusion.2 = f32[2,32,16,768]{3,2,1,0:T(8,128)S(1)} fusion(bf16[1,2,768,2048]{3,2,1,0:T(8,128)(2,1)} %param.14, f32[32,2,16]{2,1,0:T(2,128)S(1)} %copy.56, bf16[32,32,2304]{2,1,0:T(8,128)(2,1)} %all-to-all-done), kind=kOutput, calls=%fused_computation.4 | convolution fusion | flops 3227516928 | bytes 13635584 | tf_op jit(solution)/shard_map/gjsd,jfd->jgsf/dot_general | solution.py:86
  149.9 1.8 fusion.13
  151.7 1.0 slice.38
  152.7 0.8 reshape.152
  153.5 0.3 collective-permute-start.1
  153.8 0.5 broadcast.88
  154.3 0.7 reduce.11
  155.0 0.1 broadcast_in_dim.64
  155.1 0.5 select_reduce_fusion
  155.6 0.1 reshape.153
  155.7 0.1 fusion.23
  155.8 0.7 bitcast_multiply_fusion.1
  156.5 0.9 copy.62
  157.4 0.1 select_reduce_fusion.2
  157.5 0.3 collective-permute-start.2
  157.8 1.9 %pad_maximum_fusion.1 = bf16[1,2,512,1536]{3,2,1,0:T(8,128)(2,1)} fusion(bf16[1,2,512,768]{3,2,1,0:T(8,128)(2,1)S(1)} %bitcast.52, bf16[1,2,512,768]{3,2,1,0:T(8,128)(2,1)S(1)} %bitcast.51), kind=kLoop, calls=%fused_computation.30 | loop fusion | flops 6291456 | bytes 6291456 | tf_op jit(solution)/shard_map/concatenate | solution.py:91
  159.7 25.8 %collective-permute-done.2 = bf16[128,64]{0,1:T(8,128)(2,1)S(1)} collective-permute-done((bf16[128,64]{0,1:T(8,128)(2,1)S(1)}, bf16[128,64]{0,1:T(8,128)(2,1)S(1)}, u32[]{:S(2)}, u32[]{:S(2)}) %collective-permute-start.2) | collective-permute-done | bytes 16416 | tf_op jit(solution)/shard_map/ppermute | solution.py:9
  185.5 2.2 %fusion.22 = bf16[1,128,2048]{2,1,0:T(8,128)(2,1)} fusion(bf16[128,2048]{1,0:T(8,128)(2,1)} %collective-permute-done.1, bf16[128,64]{0,1:T(8,128)(2,1)S(1)} %collective-permute-done.2, bf16[64,2048]{1,0:T(8,128)(2,1)S(1)} %copy-done.3), kind=kOutput, calls=%fused_computation.35 | convolution fusion | flops 34340864 | bytes 1327104 | tf_op jit(solution)/shard_map/dot_general | solution.py:102
  (15 shorter events, 0.1 us)
Async XLA Ops:
  0.6 10.6 %collective-permute-start = (bf16[2,2048]{1,0:T(2,128)(2,1)}, bf16[2,2048]{1,0:T(2,128)(2,1)S(1)}, u32[]{:S(2)}, u32[]{:S(2)}) collective-permute-start(bf16[2,2048]{1,0:T(2,128)(2,1)} %bitcast.61), channel_id=1, source_target_pairs={{0,224},{32,0},{64,32},{96,64},{128,96},{160,128},{192,160},{224,1... | collective-permute-start | bytes 24584 | tf_op jit(solution)/shard_map/ppermute | solution.py:9
  16.1 9.1 %copy-start.4 = (f32[1,128,8]{1,2,0:T(8,128)S(1)}, f32[1,128,8]{1,2,0:T(8,128)}, u32[]{:S(2)}) copy-start(f32[1,128,8]{1,2,0:T(8,128)} %param.12) | copy-start | bytes 12292
  16.1 9.2 %copy-start.1 = (bf16[1,2,512,1536]{3,2,1,0:T(8,128)(2,1)S(1)}, bf16[1,2,512,1536]{3,2,1,0:T(8,128)(2,1)}, u32[]{:S(2)}) copy-start(bf16[1,2,512,1536]{3,2,1,0:T(8,128)(2,1)} %param.13) | copy-start | bytes 9437188
  16.1 111.6 %all-to-all-start = ((bf16[32,32,2304]{2,1,0:T(8,128)(2,1)}), bf16[32,32,2304]{2,1,0:T(8,128)(2,1)}, u32[]{:S(2)}, u32[]{:S(2)}) async-start(bf16[32,32,2304]{2,1,0:T(8,128)(2,1)} %pad_maximum_fusion), calls=%async_computation | async-start | bytes 9437184 | tf_op jit(solution)/shard_map/all_to_all | solution.py:46
  129.2 4.6 %copy-start = (f32[2,32,16,2048]{3,2,1,0:T(8,128)S(1)}, f32[2,32,16,2048]{3,2,1,0:T(8,128)}, u32[]{:S(2)}) copy-start(f32[2,32,16,2048]{3,2,1,0:T(8,128)} %bitcast_convert_fusion) | copy-start | bytes 25165828
  135.5 18.3 %all-to-all-start.1 = ((f32[32,1,32]{2,1,0:T(1,128)}), f32[32,1,32]{2,1,0:T(1,128)S(1)}, u32[]{:S(2)}, u32[]{:S(2)}) async-start(f32[32,1,32]{2,1,0:T(1,128)} %copy.61), calls=%async_computation.1 | async-start | bytes 32768 | tf_op jit(solution)/shard_map/all_to_all | solution.py:74
  143.4 6.4 %copy-start.2 = (bf16[1,2,512,1536]{3,2,1,0:T(8,128)(2,1)S(1)}, bf16[1,2,512,1536]{3,2,1,0:T(8,128)(2,1)}, u32[]{:S(2)}) copy-start(bf16[1,2,512,1536]{3,2,1,0:T(8,128)(2,1)} %param.13) | copy-start | bytes 9437188
  149.9 7.5 %copy-start.5 = (s32[1,128,8]{1,2,0:T(8,128)S(1)}, s32[1,128,8]{1,2,0:T(8,128)}, u32[]{:S(2)}) copy-start(s32[1,128,8]{1,2,0:T(8,128)} %param.10) | copy-start | bytes 12292
  153.5 32.0 %copy-start.3 = (bf16[64,2048]{1,0:T(8,128)(2,1)S(1)}, bf16[64,2048]{1,0:T(8,128)(2,1)}, u32[]{:S(2)}) copy-start(bf16[64,2048]{1,0:T(8,128)(2,1)} %reshape.152) | copy-start | bytes 786436
  153.5 32.0 %collective-permute-start.1 = (bf16[128,2048]{1,0:T(8,128)(2,1)}, bf16[128,2048]{1,0:T(8,128)(2,1)}, u32[]{:S(2)}, u32[]{:S(2)}) collective-permute-start(bf16[128,2048]{1,0:T(8,128)(2,1)} %bitcast.56), channel_id=1, source_target_pairs={{0,224},{32,0},{64,32},{96,64},{128,96},{160,128},{192,160},{224,1... | collective-permute-start | bytes 1572872 | tf_op jit(solution)/shard_map/ppermute | solution.py:9
  157.5 28.1 %collective-permute-start.2 = (bf16[128,64]{0,1:T(8,128)(2,1)S(1)}, bf16[128,64]{0,1:T(8,128)(2,1)S(1)}, u32[]{:S(2)}, u32[]{:S(2)}) collective-permute-start(bf16[128,64]{0,1:T(8,128)(2,1)S(1)} %select_reduce_fusion.2), channel_id=1, source_target_pairs={{0,224},{32,0},{64,32},{96,64},{128,96},{160,128},{192,160},{224,1... | collective-permute-start | bytes 49160 | tf_op jit(solution)/shard_map/ppermute | solution.py:9

commit v9 on v8

--- a/solution.py
+++ b/solution.py
@@ -28,7 +28,6 @@
     row_ids = jnp.arange(total_rows, dtype=jnp.int32)
     token_hit = pair_dest[None, :, :] == row_ids[:, None, None]
     token_onehot = jnp.any(token_hit, axis=2).astype(jnp.bfloat16)
-    token_rows = jnp.dot(token_onehot, features, preferred_element_type=jnp.float32).astype(jnp.bfloat16)
     matches = token_hit.reshape(total_rows, tok_rows * top_count)
     gate_low = gate_weights[0].astype(jnp.bfloat16)
     slot_gate = jnp.sum(
@@ -42,7 +41,14 @@
         next_router.reshape(1, local_experts * capacity, chunk),
         (groups, local_experts * capacity, chunk),
     ).reshape(total_rows, chunk)
-    payload = jnp.concatenate([token_rows, router_chunks, gate_cols], axis=1)
+    wide_features = jnp.concatenate([features, jnp.zeros((tok_rows, chunk + 128), features.dtype)], axis=1)
+    extras = jnp.concatenate(
+        [jnp.zeros((total_rows, width), jnp.float32), router_chunks.astype(jnp.float32), gate_cols.astype(jnp.float32)],
+        axis=1,
+    )
+    payload = (
+        jnp.dot(token_onehot, wide_features, preferred_element_type=jnp.float32) + extras
+    ).astype(jnp.bfloat16)
     arrived = lax.all_to_all(
         payload.reshape(groups, local_experts * capacity, -1),
         "expert",

time: 188 us -> 186 us (0.989)
  other arithmetic: 20.9 us -> 16.2 us
  waiting for transfers between devices: 117 us -> 120 us
    concatenate x1 -> x0, other arithmetic: 4.76 us -> none  [section_step(): payload = jnp.concatenate([token_rows, router_chunks, gate_cols], axis=1)]
    ppermute x3, waiting for transfers between devices: 25.8 us -> 28.7 us  [passed_along(): lax.ppermute(value, axis, [(i, (i + by) % peers) for i in range(peers)])]
  transfers between devices with their start and end apart: 5 -> 5, of which waited for: 2 -> 3; matrix products, arithmetic and copies ran while one was open for 20% -> 17% of each run, Pallas kernels for 0% -> 0%
where the time goes in v9:
time: 186 us
  waiting for transfers between devices  120 us (65%)
  matrix products  19.2 us (10%)
  starting transfers between devices  18.6 us (10%)
  other arithmetic  16.2 us (9%)
  local copies, waits for them, and re-layouts  11 us (6%)
    all_to_all x1, waiting for transfers between devices, section_step(): lax.all_to_all(payload.reshape(groups, local_experts * capacity, -1), 'ex...  91.4 us
    ppermute x3, waiting for transfers between devices, passed_along(): lax.ppermute(value, axis, [(i, (i + by) % peers) for i in range(peers)])  28.7 us
    all_to_all x1, starting transfers between devices, section_step(): lax.all_to_all(payload.reshape(groups, local_experts * capacity, -1), 'ex...  9.97 us
    all_to_all x1, starting transfers between devices, section_step(): lax.all_to_all(row_scores.reshape(groups, local_experts * capacity), 'exp...  7.91 us
    dot_general x1, matrix products, section_step(): jnp.einsum('jsf,jfd->jsd', hidden, weights, preferred_element_type=jnp.fl...  6.73 us
    dot_general x1, matrix products, section_step(): jnp.einsum('gjsd,jfd->jgsf', scaled_rows, weights, preferred_element_type...  6.41 us
    convert_element_type x1, other arithmetic, section_step(): expert_out.transpose(1, 0, 2, 3).astype(jnp.float32)  4.28 us
    dot_general x1, matrix products, section_step(): jnp.dot(token_onehot, wide_features, preferred_element_type=jnp.float32)  3.92 us
  transfers between devices with their start and end apart: 5, of which 3 were waited for; matrix products, arithmetic and copies ran while one was open for 17% of the time, Pallas kernels for 0%

profile of v9, /device:TPU:79, one launch (start us, length us, event | category | flops | bytes accessed | tf_op | source)
XLA Modules:
  0.0 185.9 jit_solution(6129560376173751323)
XLA Ops:
  0.6 0.6 collective-permute-start
  1.3 0.6 compare_reduce_fusion
  1.9 0.7 convert_convert_fusion
  2.6 0.1 copy.50
  2.7 0.1 reshape.157
  2.8 0.7 add_select_fusion
  3.5 0.1 copy.49
  3.6 0.1 eq.43
  3.7 0.5 select_reduce_fusion.1
  4.2 0.7 convert_select_fusion
  4.9 0.2 reshape.162
  5.1 1.9 %fusion.8 = pred[1024,128]{1,0:T(8,128)(4,1)S(1)} fusion(s32[128,8]{0,1:T(8,128)S(1)} %bitcast.55), kind=kLoop, calls=%fused_computation.18 | loop fusion | flops 1966080 | bytes 135168 | tf_op jit(solution)/shard_map/reduce_or | solution.py:30
  7.1 2.4 %collective-permute-done = bf16[2,2048]{1,0:T(2,128)(2,1)S(1)} collective-permute-done((bf16[2,2048]{1,0:T(2,128)(2,1)}, bf16[2,2048]{1,0:T(2,128)(2,1)S(1)}, u32[]{:S(2)}, u32[]{:S(2)}) %collective-permute-start) | collective-permute-done | bytes 8224 | tf_op jit(solution)/shard_map/ppermute | solution.py:9
  9.4 0.1 broadcast_in_dim.63
  9.5 3.9 %fusion = bf16[1024,2304]{1,0:T(8,128)(2,1)} fusion(f32[1024,128]{1,0:T(8,128)S(1)} %pad_convert_fusion, f32[1024,128]{1,0:T(8,128)S(1)} %bitcast.53, pred[1024,128]{1,0:T(8,128)(4,1)S(1)} %fusion.8, f32[2304]{0:T(1024)S(1)} %pad.6.clone, bf16[128,2048]{1,0:T(8,128)(2,1)} %bitcast.58), kind=kOutput, calls=%fused_computation.3 | convolution fusion | flops 613416960 | bytes 6431744 | tf_op jit(solution)/shard_map/dot_general | solution.py:50
  13.4 10.0 %all-to-all-start = ((bf16[32,32,2304]{2,1,0:T(8,128)(2,1)}), bf16[32,32,2304]{2,1,0:T(8,128)(2,1)}, u32[]{:S(2)}, u32[]{:S(2)}) async-start(bf16[32,32,2304]{2,1,0:T(8,128)(2,1)} %bitcast.50), calls=%async_computation | async-start | bytes 9437184 | tf_op jit(solution)/shard_map/all_to_all | solution.py:52
  23.4 0.1 copy.55
  23.5 6.7 %fusion.9 = bf16[2,512,2048]{2,1,0:T(8,128)(2,1)S(1)} fusion(bf16[1,2,768,2048]{3,2,1,0:T(8,128)(2,1)} %param.14, bf16[2,512,1536]{2,1,0:T(8,128)(2,1)S(1)} %bitcast.51), kind=kOutput, calls=%fused_computation.21 | convolution fusion | flops 3229614080 | bytes 13631488 | tf_op jit(solution)/shard_map/jsf,jfd->jsd/dot_general | solution.py:73
  30.3 4.3 %bitcast_convert_fusion = f32[2,32,16,2048]{3,2,1,0:T(8,128)} fusion(bf16[2,512,2048]{2,1,0:T(8,128)(2,1)S(1)} %fusion.9), kind=kLoop, calls=%fused_computation.47 | loop fusion | flops 2097152 | bytes 12582912 | tf_op jit(solution)/shard_map/convert_element_type | solution.py:78
  34.5 91.4 %all-to-all-done = bf16[32,32,2304]{2,1,0:T(8,128)(2,1)} async-done(((bf16[32,32,2304]{2,1,0:T(8,128)(2,1)}), bf16[32,32,2304]{2,1,0:T(8,128)(2,1)}, u32[]{:S(2)}, u32[]{:S(2)}) %all-to-all-start) | async-done | bytes 4718624 | tf_op jit(solution)/shard_map/all_to_all | solution.py:52
  126.0 1.0 slice.34
  126.9 0.4 copy.61
  127.3 0.1 copy.53
  127.4 2.7 %slice.35 = bf16[32,32,2048]{2,1,0:T(8,128)(2,1)S(1)} slice(bf16[32,32,2304]{2,1,0:T(8,128)(2,1)} %all-to-all-done), slice={[0:32], [0:32], [0:2048]} | slice | bytes 8388608 | tf_op jit(solution)/shard_map/slice | solution.py:61
  130.1 2.0 %copy-done = f32[2,32,16,2048]{3,2,1,0:T(8,128)S(1)} copy-done((f32[2,32,16,2048]{3,2,1,0:T(8,128)S(1)}, f32[2,32,16,2048]{3,2,1,0:T(8,128)}, u32[]{:S(2)}) %copy-start) | copy-done | bytes 8388632
  132.1 0.9 fusion.2
  132.9 0.1 copy.57
  133.0 0.7 copy.58
  133.7 7.9 %all-to-all-start.1 = ((f32[32,1,32]{2,1,0:T(1,128)}), f32[32,1,32]{2,1,0:T(1,128)S(1)}, u32[]{:S(2)}, u32[]{:S(2)}) async-start(f32[32,1,32]{2,1,0:T(1,128)} %copy.58), calls=%async_computation.1 | async-start | bytes 32768 | tf_op jit(solution)/shard_map/all_to_all | solution.py:80
  141.6 0.0 copy-start.2
  141.6 6.4 %fusion.3 = f32[2,32,16,768]{3,2,1,0:T(8,128)S(1)} fusion(bf16[1,2,768,2048]{3,2,1,0:T(8,128)(2,1)} %param.14, f32[32,2,16]{2,1,0:T(2,128)S(1)} %copy.53, bf16[32,32,2304]{2,1,0:T(8,128)(2,1)} %all-to-all-done), kind=kOutput, calls=%fused_computation.6 | convolution fusion | flops 3227516928 | bytes 13635584 | tf_op jit(solution)/shard_map/gjsd,jfd->jgsf/dot_general | solution.py:92
  148.1 0.0 copy-start.5
  148.1 1.8 fusion.14
  149.9 1.0 slice.38
  150.9 0.8 reshape.154
  151.7 0.5 broadcast.93
  152.2 0.7 reduce.11
  152.9 0.1 broadcast_in_dim.66
  153.0 0.5 select_reduce_fusion
  153.5 0.1 reshape.155
  153.6 0.1 fusion.25
  153.7 0.7 bitcast_multiply_fusion.1
  154.5 0.9 copy.59
  155.4 0.1 select_reduce_fusion.2
  155.4 0.1 collective-permute-start.2
  155.5 1.9 %pad_maximum_fusion = bf16[1,2,512,1536]{3,2,1,0:T(8,128)(2,1)} fusion(bf16[1,2,512,768]{3,2,1,0:T(8,128)(2,1)S(1)} %bitcast.49, bf16[1,2,512,768]{3,2,1,0:T(8,128)(2,1)S(1)} %bitcast.48), kind=kLoop, calls=%fused_computation.30 | loop fusion | flops 6291456 | bytes 6291456 | tf_op jit(solution)/shard_map/concatenate | solution.py:97
  157.4 26.3 %collective-permute-done.2 = bf16[128,64]{0,1:T(8,128)(2,1)S(1)} collective-permute-done((bf16[128,64]{0,1:T(8,128)(2,1)S(1)}, bf16[128,64]{0,1:T(8,128)(2,1)S(1)}, u32[]{:S(2)}, u32[]{:S(2)}) %collective-permute-start.2) | collective-permute-done | bytes 16416 | tf_op jit(solution)/shard_map/ppermute | solution.py:9
  183.7 2.2 %fusion.24 = bf16[1,128,2048]{2,1,0:T(8,128)(2,1)} fusion(bf16[128,2048]{1,0:T(8,128)(2,1)} %collective-permute-done.1, bf16[128,64]{0,1:T(8,128)(2,1)S(1)} %collective-permute-done.2, bf16[64,2048]{1,0:T(8,128)(2,1)S(1)} %copy-done.3), kind=kOutput, calls=%fused_computation.36 | convolution fusion | flops 34340864 | bytes 1327104 | tf_op jit(solution)/shard_map/dot_general | solution.py:108
  (16 shorter events, 0.1 us)
Async XLA Ops:
  0.6 8.8 %collective-permute-start = (bf16[2,2048]{1,0:T(2,128)(2,1)}, bf16[2,2048]{1,0:T(2,128)(2,1)S(1)}, u32[]{:S(2)}, u32[]{:S(2)}) collective-permute-start(bf16[2,2048]{1,0:T(2,128)(2,1)} %bitcast.60), channel_id=1, source_target_pairs={{0,224},{32,0},{64,32},{96,64},{128,96},{160,128},{192,160},{224,1... | collective-permute-start | bytes 24584 | tf_op jit(solution)/shard_map/ppermute | solution.py:9
  13.4 10.0 %copy-start.4 = (f32[1,128,8]{1,2,0:T(8,128)S(1)}, f32[1,128,8]{1,2,0:T(8,128)}, u32[]{:S(2)}) copy-start(f32[1,128,8]{1,2,0:T(8,128)} %param.12) | copy-start | bytes 12292
  13.4 10.1 %copy-start.1 = (bf16[1,2,512,1536]{3,2,1,0:T(8,128)(2,1)S(1)}, bf16[1,2,512,1536]{3,2,1,0:T(8,128)(2,1)}, u32[]{:S(2)}) copy-start(bf16[1,2,512,1536]{3,2,1,0:T(8,128)(2,1)} %param.13) | copy-start | bytes 9437188
  13.4 112.5 %all-to-all-start = ((bf16[32,32,2304]{2,1,0:T(8,128)(2,1)}), bf16[32,32,2304]{2,1,0:T(8,128)(2,1)}, u32[]{:S(2)}, u32[]{:S(2)}) async-start(bf16[32,32,2304]{2,1,0:T(8,128)(2,1)} %bitcast.50), calls=%async_computation | async-start | bytes 9437184 | tf_op jit(solution)/shard_map/all_to_all | solution.py:52
  127.4 4.6 %copy-start = (f32[2,32,16,2048]{3,2,1,0:T(8,128)S(1)}, f32[2,32,16,2048]{3,2,1,0:T(8,128)}, u32[]{:S(2)}) copy-start(f32[2,32,16,2048]{3,2,1,0:T(8,128)} %bitcast_convert_fusion) | copy-start | bytes 25165828
  133.7 18.0 %all-to-all-start.1 = ((f32[32,1,32]{2,1,0:T(1,128)}), f32[32,1,32]{2,1,0:T(1,128)S(1)}, u32[]{:S(2)}, u32[]{:S(2)}) async-start(f32[32,1,32]{2,1,0:T(1,128)} %copy.58), calls=%async_computation.1 | async-start | bytes 32768 | tf_op jit(solution)/shard_map/all_to_all | solution.py:80
  141.6 6.4 %copy-start.2 = (bf16[1,2,512,1536]{3,2,1,0:T(8,128)(2,1)S(1)}, bf16[1,2,512,1536]{3,2,1,0:T(8,128)(2,1)}, u32[]{:S(2)}) copy-start(bf16[1,2,512,1536]{3,2,1,0:T(8,128)(2,1)} %param.13) | copy-start | bytes 9437188
  148.1 7.3 %copy-start.5 = (s32[1,128,8]{1,2,0:T(8,128)S(1)}, s32[1,128,8]{1,2,0:T(8,128)}, u32[]{:S(2)}) copy-start(s32[1,128,8]{1,2,0:T(8,128)} %param.10) | copy-start | bytes 12292
  151.7 32.0 %copy-start.3 = (bf16[64,2048]{1,0:T(8,128)(2,1)S(1)}, bf16[64,2048]{1,0:T(8,128)(2,1)}, u32[]{:S(2)}) copy-start(bf16[64,2048]{1,0:T(8,128)(2,1)} %reshape.154) | copy-start | bytes 786436
  151.7 32.0 %collective-permute-start.1 = (bf16[128,2048]{1,0:T(8,128)(2,1)}, bf16[128,2048]{1,0:T(8,128)(2,1)}, u32[]{:S(2)}, u32[]{:S(2)}) collective-permute-start(bf16[128,2048]{1,0:T(8,128)(2,1)} %bitcast.59), channel_id=1, source_target_pairs={{0,224},{32,0},{64,32},{96,64},{128,96},{160,128},{192,160},{224,1... | collective-permute-start | bytes 1572872 | tf_op jit(solution)/shard_map/ppermute | solution.py:9
  155.4 28.3 %collective-permute-start.2 = (bf16[128,64]{0,1:T(8,128)(2,1)S(1)}, bf16[128,64]{0,1:T(8,128)(2,1)S(1)}, u32[]{:S(2)}, u32[]{:S(2)}) collective-permute-start(bf16[128,64]{0,1:T(8,128)(2,1)S(1)} %select_reduce_fusion.2), channel_id=1, source_target_pairs={{0,224},{32,0},{64,32},{96,64},{128,96},{160,128},{192,160},{224,1... | collective-permute-start | bytes 49160 | tf_op jit(solution)/shard_map/ppermute | solution.py:9

commit v10 on v9

--- a/solution.py
+++ b/solution.py
@@ -58,7 +58,8 @@
     )
     gate_in = arrived[..., width + chunk].reshape(groups, local_experts, capacity).astype(jnp.float32)
     router_full = arrived[..., width : width + chunk].reshape(expert_total, width)
-    rows_in = arrived[..., :width].reshape(groups, local_experts, capacity, width).astype(jnp.float32)
+    wide = arrived.shape[-1]
+    rows_in = arrived.reshape(groups, local_experts, capacity, wide).astype(jnp.float32)
 
     held, router_full = lax.optimization_barrier((features, router_full))
     next_features = passed_along(held, "pipe", -1)
@@ -73,7 +74,9 @@
     expert_out = jnp.einsum(
         "jsf,jfd->jsd", hidden, weights, preferred_element_type=jnp.float32
     ).astype(jnp.bfloat16)
-    expert_out = lax.optimization_barrier(expert_out).reshape(local_experts, groups, capacity, width)
+    expert_out = jnp.pad(lax.optimization_barrier(expert_out), ((0, 0), (0, 0), (0, wide - width)))
+    expert_out = expert_out.reshape(local_experts, groups, capacity, wide)
+    wide_weights = jnp.pad(weights, ((0, 0), (0, 0), (0, wide - width)))
     row_scores = jnp.sum(
         rows_in * expert_out.transpose(1, 0, 2, 3).astype(jnp.float32), axis=-1
     )
@@ -90,7 +93,7 @@
 
     scaled_rows = (gate_in[..., None] * rows_in).astype(jnp.bfloat16)
     row_grad = jnp.einsum(
-        "gjsd,jfd->jgsf", scaled_rows, weights, preferred_element_type=jnp.float32
+        "gjsd,jfd->jgsf", scaled_rows, wide_weights, preferred_element_type=jnp.float32
     ).reshape(local_experts, groups * capacity, hidden_width)
     gate_grad = row_grad * up_part * sigmoid_gate * (1.0 + gate_part * (1.0 - sigmoid_gate))
     up_grad = row_grad * silu_gate

time: 186 us -> 177 us (0.952)
  waiting for transfers between devices: 120 us -> 109 us
  other arithmetic: 16.2 us -> 21.9 us
  local copies, waits for them, and re-layouts: 11 us -> 5.61 us
    ppermute x3, waiting for transfers between devices: 28.7 us -> 18.4 us  [passed_along(): lax.ppermute(value, axis, [(i, (i + by) % peers) for i in range(peers)])]
    reduce_sum x1, other arithmetic: 0.89 us -> 6.12 us  [section_step(): jnp.sum(rows_in * expert_out.transpose(1, 0, 2, 3).astype(jnp.float32), a...]
    slice x1 -> x0, local copies, waits for them, and re-layouts: 2.66 us -> none  [section_step(): arrived[..., :width].reshape(groups, local_experts, capacity, width)]
    unnamed x14 -> x10, local copies, waits for them, and re-layouts: 2.48 us -> 0.5 us
  transfers between devices with their start and end apart: 5 -> 5, of which waited for: 3 -> 3; matrix products, arithmetic and copies ran while one was open for 17% -> 19% of each run, Pallas kernels for 0% -> 0%
where the time goes in v10:
time: 177 us; the launch traced here: 176 us
  waiting for transfers between devices  109 us (62%)
  other arithmetic  21.9 us (12%)
  matrix products  19.7 us (11%)
  starting transfers between devices  18.8 us (11%)
  local copies, waits for them, and re-layouts  5.61 us (3%)
    all_to_all x1, waiting for transfers between devices, section_step(): lax.all_to_all(payload.reshape(groups, local_experts * capacity, -1), 'ex...  90.9 us
    ppermute x3, waiting for transfers between devices, passed_along(): lax.ppermute(value, axis, [(i, (i + by) % peers) for i in range(peers)])  18.4 us
    all_to_all x1, starting transfers between devices, section_step(): lax.all_to_all(payload.reshape(groups, local_experts * capacity, -1), 'ex...  9.97 us
    all_to_all x1, starting transfers between devices, section_step(): lax.all_to_all(row_scores.reshape(groups, local_experts * capacity), 'exp...  7.9 us
    dot_general x1, matrix products, section_step(): jnp.einsum('gjsd,jfd->jgsf', scaled_rows, wide_weights, preferred_element...  6.91 us
    dot_general x1, matrix products, section_step(): jnp.einsum('jsf,jfd->jsd', hidden, weights, preferred_element_type=jnp.fl...  6.7 us
    reduce_sum x1, other arithmetic, section_step(): jnp.sum(rows_in * expert_out.transpose(1, 0, 2, 3).astype(jnp.float32), a...  6.12 us
    convert_element_type x1, other arithmetic, section_step(): expert_out.transpose(1, 0, 2, 3).astype(jnp.float32)  4.79 us
  transfers between devices with their start and end apart: 5, of which 3 were waited for; matrix products, arithmetic and copies ran while one was open for 19% of the time, Pallas kernels for 0%

profile of v10, /device:TPU:79, one launch (start us, length us, event | category | flops | bytes accessed | tf_op | source)
XLA Modules:
  0.0 176.3 jit_solution(11478637051393128922)
XLA Ops:
  0.6 0.6 collective-permute-start
  1.3 0.6 compare_reduce_fusion
  1.9 0.7 add_select_fusion
  2.6 0.1 copy.49
  2.7 0.1 eq.43
  2.8 0.7 convert_convert_fusion
  3.5 0.1 copy.50
  3.6 0.1 reshape.157
  3.7 0.5 select_reduce_fusion.1
  4.2 0.7 convert_select_fusion
  4.9 0.2 reshape.162
  5.1 1.9 %fusion.7 = pred[1024,128]{1,0:T(8,128)(4,1)S(1)} fusion(s32[128,8]{0,1:T(8,128)S(1)} %bitcast.52), kind=kLoop, calls=%fused_computation.17 | loop fusion | flops 1966080 | bytes 135168 | tf_op jit(solution)/shard_map/reduce_or | solution.py:30
  7.1 2.4 %collective-permute-done = bf16[2,2048]{1,0:T(2,128)(2,1)S(1)} collective-permute-done((bf16[2,2048]{1,0:T(2,128)(2,1)}, bf16[2,2048]{1,0:T(2,128)(2,1)S(1)}, u32[]{:S(2)}, u32[]{:S(2)}) %collective-permute-start) | collective-permute-done | bytes 8224 | tf_op jit(solution)/shard_map/ppermute | solution.py:9
  9.4 0.1 broadcast_in_dim.63
  9.5 4.0 %fusion.2 = bf16[1024,2304]{1,0:T(8,128)(2,1)} fusion(f32[1024,128]{1,0:T(8,128)S(1)} %pad_convert_fusion, f32[1024,128]{1,0:T(8,128)S(1)} %bitcast.50, pred[1024,128]{1,0:T(8,128)(4,1)S(1)} %fusion.7, f32[2304]{0:T(1024)S(1)} %pad.16.clone, bf16[128,2048]{1,0:T(8,128)(2,1)} %bitcast.1), kind=kOutput, calls=%fused_computation.5 | convolution fusion | flops 613416960 | bytes 6431744 | tf_op jit(solution)/shard_map/dot_general | solution.py:50
  13.5 10.0 %all-to-all-start = ((bf16[32,32,2304]{2,1,0:T(8,128)(2,1)}), bf16[32,32,2304]{2,1,0:T(8,128)(2,1)}, u32[]{:S(2)}, u32[]{:S(2)}) async-start(bf16[32,32,2304]{2,1,0:T(8,128)(2,1)} %bitcast.47), calls=%async_computation | async-start | bytes 9437184 | tf_op jit(solution)/shard_map/all_to_all | solution.py:52
  23.5 0.1 copy.55
  23.6 6.7 %convolution_convert_fusion = bf16[2,512,2048]{2,1,0:T(8,128)(2,1)S(1)} fusion(bf16[2,512,1536]{2,1,0:T(8,128)(2,1)S(1)} %bitcast.48, bf16[1,2,768,2048]{3,2,1,0:T(8,128)(2,1)} %param.14), kind=kOutput, calls=%fused_computation.20 | convolution fusion | flops 3229614080 | bytes 13631488 | tf_op jit(solution)/shard_map/jsf,jfd->jsd/dot_general | solution.py:74
  30.3 4.8 %bitcast_convert_fusion = f32[2,32,16,2304]{3,2,1,0:T(8,128)} fusion(bf16[2,512,2048]{2,1,0:T(8,128)(2,1)S(1)} %convolution_convert_fusion), kind=kLoop, calls=%fused_computation.46 | loop fusion | flops 2359296 | bytes 13631488 | tf_op jit(solution)/shard_map/convert_element_type | solution.py:81
  35.1 90.9 %all-to-all-done = bf16[32,32,2304]{2,1,0:T(8,128)(2,1)} async-done(((bf16[32,32,2304]{2,1,0:T(8,128)(2,1)}), bf16[32,32,2304]{2,1,0:T(8,128)(2,1)}, u32[]{:S(2)}, u32[]{:S(2)}) %all-to-all-start) | async-done | bytes 4718624 | tf_op jit(solution)/shard_map/all_to_all | solution.py:52
  126.0 6.1 %fusion.1 = f32[32,2,16]{2,1,0:T(2,128)S(1)} fusion(bf16[32,2,16,2304]{3,2,1,0:T(8,128)(2,1)} %bitcast.16, f32[2,32,16,2304]{3,2,1,0:T(8,128)} %bitcast_convert_fusion), kind=kLoop, calls=%fused_computation.3 | loop fusion | flops 7076864 | bytes 14159872 | tf_op jit(solution)/shard_map/reduce_sum | solution.py:80
  132.1 0.1 copy.57
  132.2 0.7 copy.58
  132.9 7.9 %all-to-all-start.1 = ((f32[32,1,32]{2,1,0:T(1,128)}), f32[32,1,32]{2,1,0:T(1,128)S(1)}, u32[]{:S(2)}, u32[]{:S(2)}) async-start(f32[32,1,32]{2,1,0:T(1,128)} %copy.58), calls=%async_computation.1 | async-start | bytes 32768 | tf_op jit(solution)/shard_map/all_to_all | solution.py:83
  140.8 1.0 slice.33
  141.8 0.1 reshape.154
  141.9 0.3 collective-permute-start.1
  142.2 1.0 slice.30
  143.1 0.4 copy.61
  143.5 0.1 copy.53
  143.6 0.0 copy-start.1
  143.6 6.9 %fusion.3 = f32[2,32,16,768]{3,2,1,0:T(8,128)S(1)} fusion(bf16[2,768,2048]{2,1,0:T(8,128)(2,1)} %bitcast.55, f32[32,2,16]{2,1,0:T(2,128)S(1)} %copy.53, bf16[32,32,2304]{2,1,0:T(8,128)(2,1)} %all-to-all-done), kind=kOutput, calls=%fused_computation.6 | convolution fusion | flops 3630956544 | bytes 14159872 | tf_op jit(solution)/shard_map/gjsd,jfd->jgsf/dot_general | solution.py:95
  150.6 0.0 copy-start.3
  150.6 1.8 %fusion.10 = (bf16[2,512,768]{2,1,0:T(8,128)(2,1)S(1)}, bf16[2,512,768]{2,1,0:T(8,128)(2,1)S(1)}) fusion(f32[2,32,16,768]{3,2,1,0:T(8,128)S(1)} %fusion.3, bf16[2,512,1536]{2,1,0:T(8,128)(2,1)S(1)} %bitcast.49), kind=kLoop, calls=%fused_computation.23 | loop fusion | flops 11796480 | bytes 9437184 | tf_op jit(solution)/shard_map/convert.9
  152.4 0.0 all-to-all-done.1
  152.4 0.5 broadcast.97
  152.9 0.7 reduce.11
  153.6 0.1 broadcast_in_dim.66
  153.7 0.5 select_reduce_fusion
  154.2 0.1 reshape.155
  154.3 0.1 fusion.21
  154.4 0.7 bitcast_multiply_fusion.1
  155.2 0.9 copy.59
  156.1 0.1 select_reduce_fusion.2
  156.1 0.1 collective-permute-start.2
  156.2 1.9 %pad_maximum_fusion = bf16[1,2,512,1536]{3,2,1,0:T(8,128)(2,1)} fusion(bf16[1,2,512,768]{3,2,1,0:T(8,128)(2,1)S(1)} %bitcast.46, bf16[1,2,512,768]{3,2,1,0:T(8,128)(2,1)S(1)} %bitcast.45), kind=kLoop, calls=%fused_computation.29 | loop fusion | flops 6291456 | bytes 6291456 | tf_op jit(solution)/shard_map/concatenate | solution.py:100
  158.1 16.1 %collective-permute-done.2 = bf16[128,64]{0,1:T(8,128)(2,1)S(1)} collective-permute-done((bf16[128,64]{0,1:T(8,128)(2,1)S(1)}, bf16[128,64]{0,1:T(8,128)(2,1)S(1)}, u32[]{:S(2)}, u32[]{:S(2)}) %collective-permute-start.2) | collective-permute-done | bytes 16416 | tf_op jit(solution)/shard_map/ppermute | solution.py:9
  174.2 2.2 %fusion.20 = bf16[1,128,2048]{2,1,0:T(8,128)(2,1)} fusion(bf16[128,2048]{1,0:T(8,128)(2,1)} %collective-permute-done.1, bf16[128,64]{0,1:T(8,128)(2,1)S(1)} %collective-permute-done.2, bf16[64,2048]{1,0:T(8,128)(2,1)S(1)} %reshape.154), kind=kOutput, calls=%fused_computation.35 | convolution fusion | flops 34340864 | bytes 1327104 | tf_op jit(solution)/shard_map/dot_general | solution.py:111
  (11 shorter events, 0.1 us)
Async XLA Ops:
  0.6 8.8 %collective-permute-start = (bf16[2,2048]{1,0:T(2,128)(2,1)}, bf16[2,2048]{1,0:T(2,128)(2,1)S(1)}, u32[]{:S(2)}, u32[]{:S(2)}) collective-permute-start(bf16[2,2048]{1,0:T(2,128)(2,1)} %bitcast.56), channel_id=1, source_target_pairs={{0,224},{32,0},{64,32},{96,64},{128,96},{160,128},{192,160},{224,1... | collective-permute-start | bytes 24584 | tf_op jit(solution)/shard_map/ppermute | solution.py:9
  13.5 10.0 %copy-start.2 = (f32[1,128,8]{1,2,0:T(8,128)S(1)}, f32[1,128,8]{1,2,0:T(8,128)}, u32[]{:S(2)}) copy-start(f32[1,128,8]{1,2,0:T(8,128)} %param.12) | copy-start | bytes 12292
  13.5 10.1 %copy-start = (bf16[1,2,512,1536]{3,2,1,0:T(8,128)(2,1)S(1)}, bf16[1,2,512,1536]{3,2,1,0:T(8,128)(2,1)}, u32[]{:S(2)}) copy-start(bf16[1,2,512,1536]{3,2,1,0:T(8,128)(2,1)} %param.13) | copy-start | bytes 9437188
  13.5 112.5 %all-to-all-start = ((bf16[32,32,2304]{2,1,0:T(8,128)(2,1)}), bf16[32,32,2304]{2,1,0:T(8,128)(2,1)}, u32[]{:S(2)}, u32[]{:S(2)}) async-start(bf16[32,32,2304]{2,1,0:T(8,128)(2,1)} %bitcast.47), calls=%async_computation | async-start | bytes 9437184 | tf_op jit(solution)/shard_map/all_to_all | solution.py:52
  132.9 19.5 %all-to-all-start.1 = ((f32[32,1,32]{2,1,0:T(1,128)}), f32[32,1,32]{2,1,0:T(1,128)S(1)}, u32[]{:S(2)}, u32[]{:S(2)}) async-start(f32[32,1,32]{2,1,0:T(1,128)} %copy.58), calls=%async_computation.1 | async-start | bytes 32768 | tf_op jit(solution)/shard_map/all_to_all | solution.py:83
  141.9 32.3 %collective-permute-start.1 = (bf16[128,2048]{1,0:T(8,128)(2,1)}, bf16[128,2048]{1,0:T(8,128)(2,1)}, u32[]{:S(2)}, u32[]{:S(2)}) collective-permute-start(bf16[128,2048]{1,0:T(8,128)(2,1)} %bitcast.1), channel_id=1, source_target_pairs={{0,224},{32,0},{64,32},{96,64},{128,96},{160,128},{192,160},{224,1... | collective-permute-start | bytes 1572872 | tf_op jit(solution)/shard_map/ppermute | solution.py:9
  143.6 6.9 %copy-start.1 = (bf16[1,2,512,1536]{3,2,1,0:T(8,128)(2,1)S(1)}, bf16[1,2,512,1536]{3,2,1,0:T(8,128)(2,1)}, u32[]{:S(2)}) copy-start(bf16[1,2,512,1536]{3,2,1,0:T(8,128)(2,1)} %param.13) | copy-start | bytes 9437188
  150.6 5.5 %copy-start.3 = (s32[1,128,8]{1,2,0:T(8,128)S(1)}, s32[1,128,8]{1,2,0:T(8,128)}, u32[]{:S(2)}) copy-start(s32[1,128,8]{1,2,0:T(8,128)} %param.10) | copy-start | bytes 12292
  156.1 18.1 %collective-permute-start.2 = (bf16[128,64]{0,1:T(8,128)(2,1)S(1)}, bf16[128,64]{0,1:T(8,128)(2,1)S(1)}, u32[]{:S(2)}, u32[]{:S(2)}) collective-permute-start(bf16[128,64]{0,1:T(8,128)(2,1)S(1)} %select_reduce_fusion.2), channel_id=1, source_target_pairs={{0,224},{32,0},{64,32},{96,64},{128,96},{160,128},{192,160},{224,1... | collective-permute-start | bytes 49160 | tf_op jit(solution)/shard_map/ppermute | solution.py:9

commit v11 on v10

--- a/solution.py
+++ b/solution.py
@@ -74,11 +74,13 @@
     expert_out = jnp.einsum(
         "jsf,jfd->jsd", hidden, weights, preferred_element_type=jnp.float32
     ).astype(jnp.bfloat16)
-    expert_out = jnp.pad(lax.optimization_barrier(expert_out), ((0, 0), (0, 0), (0, wide - width)))
-    expert_out = expert_out.reshape(local_experts, groups, capacity, wide)
+    expert_out = jnp.pad(expert_out, ((0, 0), (0, 0), (0, wide - width)))
+    expert_out = lax.optimization_barrier(
+        expert_out.reshape(local_experts, groups, capacity, wide).transpose(1, 0, 2, 3)
+    )
     wide_weights = jnp.pad(weights, ((0, 0), (0, 0), (0, wide - width)))
     row_scores = jnp.sum(
-        rows_in * expert_out.transpose(1, 0, 2, 3).astype(jnp.float32), axis=-1
+        rows_in * expert_out.astype(jnp.float32), axis=-1
     )
     returned = lax.all_to_all(
         row_scores.reshape(groups, local_experts * capacity),

time: 177 us -> 176 us (level)
  other arithmetic: 21.9 us -> 16.1 us
  local copies, waits for them, and re-layouts: 5.61 us -> 8.77 us
  waiting for transfers between devices: 109 us -> 111 us
    convert_element_type x1 -> x0, other arithmetic: 4.79 us -> none  [section_step(): expert_out.transpose(1, 0, 2, 3).astype(jnp.float32)]
    reshape x0 -> x1, local copies, waits for them, and re-layouts: none -> 2.77 us  [section_step(): expert_out.reshape(local_experts, groups, capacity, wide)]
where the time goes in v11:
time: 176 us; the launch traced here: 175 us
  waiting for transfers between devices  111 us (63%)
  matrix products  19.8 us (11%)
  starting transfers between devices  18.9 us (11%)
  other arithmetic  16.1 us (9%)
  local copies, waits for them, and re-layouts  8.77 us (5%)
    all_to_all x1, waiting for transfers between devices, section_step(): lax.all_to_all(payload.reshape(groups, local_experts * capacity, -1), 'ex...  92.6 us
    ppermute x3, waiting for transfers between devices, passed_along(): lax.ppermute(value, axis, [(i, (i + by) % peers) for i in range(peers)])  18.5 us
    all_to_all x1, starting transfers between devices, section_step(): lax.all_to_all(payload.reshape(groups, local_experts * capacity, -1), 'ex...  9.97 us
    all_to_all x1, starting transfers between devices, section_step(): lax.all_to_all(row_scores.reshape(groups, local_experts * capacity), 'exp...  7.91 us
    dot_general x1, matrix products, section_step(): jnp.einsum('gjsd,jfd->jgsf', scaled_rows, wide_weights, preferred_element...  6.91 us
    dot_general x1, matrix products, section_step(): jnp.einsum('jsf,jfd->jsd', hidden, weights, preferred_element_type=jnp.fl...  6.71 us
    reduce_sum x1, other arithmetic, section_step(): row_scores = jnp.sum(rows_in * expert_out.astype(jnp.float32), axis=-1)  5.08 us
    dot_general x1, matrix products, section_step(): jnp.dot(token_onehot, wide_features, preferred_element_type=jnp.float32)  4.01 us
  transfers between devices with their start and end apart: 5, of which 3 were waited for; matrix products, arithmetic and copies ran while one was open for 19% of the time, Pallas kernels for 0%

profile of v11, /device:TPU:79, one launch (start us, length us, event | category | flops | bytes accessed | tf_op | source)
XLA Modules:
  0.0 175.3 jit_solution(1678641560255650915)
XLA Ops:
  0.6 0.6 collective-permute-start
  1.3 0.6 compare_reduce_fusion
  1.9 0.7 add_select_fusion
  2.6 0.1 copy.49
  2.7 0.1 eq.43
  2.8 0.7 convert_convert_fusion
  3.5 0.1 copy.50
  3.6 0.1 reshape.158
  3.7 0.5 select_reduce_fusion.1
  4.2 0.7 convert_select_fusion
  4.8 0.2 reshape.162
  5.1 1.9 %fusion.7 = pred[1024,128]{1,0:T(8,128)(4,1)S(1)} fusion(s32[128,8]{0,1:T(8,128)S(1)} %bitcast.53), kind=kLoop, calls=%fused_computation.18 | loop fusion | flops 1966080 | bytes 135168 | tf_op jit(solution)/shard_map/reduce_or | solution.py:30
  7.0 2.4 %collective-permute-done = bf16[2,2048]{1,0:T(2,128)(2,1)S(1)} collective-permute-done((bf16[2,2048]{1,0:T(2,128)(2,1)}, bf16[2,2048]{1,0:T(2,128)(2,1)S(1)}, u32[]{:S(2)}, u32[]{:S(2)}) %collective-permute-start) | collective-permute-done | bytes 8224 | tf_op jit(solution)/shard_map/ppermute | solution.py:9
  9.4 0.1 broadcast_in_dim.63
  9.5 4.0 %fusion.2 = bf16[1024,2304]{1,0:T(8,128)(2,1)} fusion(f32[1024,128]{1,0:T(8,128)S(1)} %pad_convert_fusion, f32[1024,128]{1,0:T(8,128)S(1)} %bitcast.51, pred[1024,128]{1,0:T(8,128)(4,1)S(1)} %fusion.7, f32[2304]{0:T(1024)S(1)} %pad.16.clone, bf16[128,2048]{1,0:T(8,128)(2,1)} %bitcast.1), kind=kOutput, calls=%fused_computation.5 | convolution fusion | flops 613416960 | bytes 6431744 | tf_op jit(solution)/shard_map/dot_general | solution.py:50
  13.5 10.0 %all-to-all-start = ((bf16[32,32,2304]{2,1,0:T(8,128)(2,1)}), bf16[32,32,2304]{2,1,0:T(8,128)(2,1)}, u32[]{:S(2)}, u32[]{:S(2)}) async-start(bf16[32,32,2304]{2,1,0:T(8,128)(2,1)} %bitcast.48), calls=%async_computation | async-start | bytes 9437184 | tf_op jit(solution)/shard_map/all_to_all | solution.py:52
  23.5 0.1 copy.55
  23.6 6.7 %convolution_convert_fusion = bf16[2,512,2048]{2,1,0:T(8,128)(2,1)S(1)} fusion(bf16[2,512,1536]{2,1,0:T(8,128)(2,1)S(1)} %bitcast.49, bf16[1,2,768,2048]{3,2,1,0:T(8,128)(2,1)} %param.14), kind=kOutput, calls=%fused_computation.21 | convolution fusion | flops 3229614080 | bytes 13631488 | tf_op jit(solution)/shard_map/jsf,jfd->jsd/dot_general | solution.py:74
  30.3 0.4 pad.13
  30.7 2.8 %copy.65 = bf16[2,32,16,2304]{3,2,0,1:T(8,128)(2,1)} copy(bf16[2,32,16,2304]{3,2,1,0:T(8,128)(2,1)S(1)} %bitcast.45) | data formatting | bytes 9437184 | tf_op jit(solution)/shard_map/reshape | solution.py:79
  33.5 92.6 %all-to-all-done = bf16[32,32,2304]{2,1,0:T(8,128)(2,1)} async-done(((bf16[32,32,2304]{2,1,0:T(8,128)(2,1)}), bf16[32,32,2304]{2,1,0:T(8,128)(2,1)}, u32[]{:S(2)}, u32[]{:S(2)}) %all-to-all-start) | async-done | bytes 4718624 | tf_op jit(solution)/shard_map/all_to_all | solution.py:52
  126.0 5.1 %fusion.1 = f32[32,2,16]{2,1,0:T(2,128)S(1)} fusion(bf16[32,2,16,2304]{3,2,1,0:T(8,128)(2,1)} %bitcast.16, bf16[32,2,16,2304]{3,2,1,0:T(8,128)(2,1)} %bitcast.44), kind=kLoop, calls=%fused_computation.3 | loop fusion | flops 9436160 | bytes 9441280 | tf_op jit(solution)/shard_map/reduce_sum | solution.py:82
  131.1 0.1 copy.57
  131.2 0.7 copy.58
  131.9 7.9 %all-to-all-start.1 = ((f32[32,1,32]{2,1,0:T(1,128)}), f32[32,1,32]{2,1,0:T(1,128)S(1)}, u32[]{:S(2)}, u32[]{:S(2)}) async-start(f32[32,1,32]{2,1,0:T(1,128)} %copy.58), calls=%async_computation.1 | async-start | bytes 32768 | tf_op jit(solution)/shard_map/all_to_all | solution.py:85
  139.8 1.0 slice.33
  140.8 0.1 reshape.154
  140.9 0.3 collective-permute-start.1
  141.2 1.0 slice.30
  142.1 0.4 copy.61
  142.5 0.1 copy.53
  142.6 0.0 copy-start.1
  142.6 6.9 %fusion.3 = f32[2,32,16,768]{3,2,1,0:T(8,128)S(1)} fusion(bf16[2,768,2048]{2,1,0:T(8,128)(2,1)} %bitcast.56, f32[32,2,16]{2,1,0:T(2,128)S(1)} %copy.53, bf16[32,32,2304]{2,1,0:T(8,128)(2,1)} %all-to-all-done), kind=kOutput, calls=%fused_computation.6 | convolution fusion | flops 3630956544 | bytes 14159872 | tf_op jit(solution)/shard_map/gjsd,jfd->jgsf/dot_general | solution.py:97
  149.6 0.0 copy-start.3
  149.6 1.8 %fusion.10 = (bf16[2,512,768]{2,1,0:T(8,128)(2,1)S(1)}, bf16[2,512,768]{2,1,0:T(8,128)(2,1)S(1)}) fusion(f32[2,32,16,768]{3,2,1,0:T(8,128)S(1)} %fusion.3, bf16[2,512,1536]{2,1,0:T(8,128)(2,1)S(1)} %bitcast.50), kind=kLoop, calls=%fused_computation.24 | loop fusion | flops 11796480 | bytes 9437184 | tf_op jit(solution)/shard_map/convert.7
  151.4 0.5 broadcast.97
  151.9 0.7 reduce.11
  152.6 0.1 broadcast_in_dim.66
  152.7 0.5 select_reduce_fusion
  153.2 0.1 reshape.156
  153.3 0.1 fusion.21
  153.4 0.7 bitcast_multiply_fusion.1
  154.2 0.9 copy.59
  155.0 0.1 select_reduce_fusion.2
  155.1 0.1 collective-permute-start.2
  155.2 1.9 %pad_maximum_fusion = bf16[1,2,512,1536]{3,2,1,0:T(8,128)(2,1)} fusion(bf16[1,2,512,768]{3,2,1,0:T(8,128)(2,1)S(1)} %bitcast.47, bf16[1,2,512,768]{3,2,1,0:T(8,128)(2,1)S(1)} %bitcast.46), kind=kLoop, calls=%fused_computation.30 | loop fusion | flops 6291456 | bytes 6291456 | tf_op jit(solution)/shard_map/concatenate | solution.py:102
  157.1 16.1 %collective-permute-done.2 = bf16[128,64]{0,1:T(8,128)(2,1)S(1)} collective-permute-done((bf16[128,64]{0,1:T(8,128)(2,1)S(1)}, bf16[128,64]{0,1:T(8,128)(2,1)S(1)}, u32[]{:S(2)}, u32[]{:S(2)}) %collective-permute-start.2) | collective-permute-done | bytes 16416 | tf_op jit(solution)/shard_map/ppermute | solution.py:9
  173.2 2.2 %fusion.20 = bf16[1,128,2048]{2,1,0:T(8,128)(2,1)} fusion(bf16[128,2048]{1,0:T(8,128)(2,1)} %collective-permute-done.1, bf16[128,64]{0,1:T(8,128)(2,1)S(1)} %collective-permute-done.2, bf16[64,2048]{1,0:T(8,128)(2,1)S(1)} %reshape.154), kind=kOutput, calls=%fused_computation.36 | convolution fusion | flops 34340864 | bytes 1327104 | tf_op jit(solution)/shard_map/dot_general | solution.py:113
  (12 shorter events, 0.1 us)
Async XLA Ops:
  0.6 8.8 %collective-permute-start = (bf16[2,2048]{1,0:T(2,128)(2,1)}, bf16[2,2048]{1,0:T(2,128)(2,1)S(1)}, u32[]{:S(2)}, u32[]{:S(2)}) collective-permute-start(bf16[2,2048]{1,0:T(2,128)(2,1)} %bitcast.57), channel_id=1, source_target_pairs={{0,224},{32,0},{64,32},{96,64},{128,96},{160,128},{192,160},{224,1... | collective-permute-start | bytes 24584 | tf_op jit(solution)/shard_map/ppermute | solution.py:9
  13.5 10.0 %copy-start.2 = (f32[1,128,8]{1,2,0:T(8,128)S(1)}, f32[1,128,8]{1,2,0:T(8,128)}, u32[]{:S(2)}) copy-start(f32[1,128,8]{1,2,0:T(8,128)} %param.12) | copy-start | bytes 12292
  13.5 10.1 %copy-start = (bf16[1,2,512,1536]{3,2,1,0:T(8,128)(2,1)S(1)}, bf16[1,2,512,1536]{3,2,1,0:T(8,128)(2,1)}, u32[]{:S(2)}) copy-start(bf16[1,2,512,1536]{3,2,1,0:T(8,128)(2,1)} %param.13) | copy-start | bytes 9437188
  13.5 112.5 %all-to-all-start = ((bf16[32,32,2304]{2,1,0:T(8,128)(2,1)}), bf16[32,32,2304]{2,1,0:T(8,128)(2,1)}, u32[]{:S(2)}, u32[]{:S(2)}) async-start(bf16[32,32,2304]{2,1,0:T(8,128)(2,1)} %bitcast.48), calls=%async_computation | async-start | bytes 9437184 | tf_op jit(solution)/shard_map/all_to_all | solution.py:52
  131.9 19.5 %all-to-all-start.1 = ((f32[32,1,32]{2,1,0:T(1,128)}), f32[32,1,32]{2,1,0:T(1,128)S(1)}, u32[]{:S(2)}, u32[]{:S(2)}) async-start(f32[32,1,32]{2,1,0:T(1,128)} %copy.58), calls=%async_computation.1 | async-start | bytes 32768 | tf_op jit(solution)/shard_map/all_to_all | solution.py:85
  140.9 32.3 %collective-permute-start.1 = (bf16[128,2048]{1,0:T(8,128)(2,1)}, bf16[128,2048]{1,0:T(8,128)(2,1)}, u32[]{:S(2)}, u32[]{:S(2)}) collective-permute-start(bf16[128,2048]{1,0:T(8,128)(2,1)} %bitcast.1), channel_id=1, source_target_pairs={{0,224},{32,0},{64,32},{96,64},{128,96},{160,128},{192,160},{224,1... | collective-permute-start | bytes 1572872 | tf_op jit(solution)/shard_map/ppermute | solution.py:9
  142.6 6.9 %copy-start.1 = (bf16[1,2,512,1536]{3,2,1,0:T(8,128)(2,1)S(1)}, bf16[1,2,512,1536]{3,2,1,0:T(8,128)(2,1)}, u32[]{:S(2)}) copy-start(bf16[1,2,512,1536]{3,2,1,0:T(8,128)(2,1)} %param.13) | copy-start | bytes 9437188
  149.6 5.5 %copy-start.3 = (s32[1,128,8]{1,2,0:T(8,128)S(1)}, s32[1,128,8]{1,2,0:T(8,128)}, u32[]{:S(2)}) copy-start(s32[1,128,8]{1,2,0:T(8,128)} %param.10) | copy-start | bytes 12292
  155.1 18.1 %collective-permute-start.2 = (bf16[128,64]{0,1:T(8,128)(2,1)S(1)}, bf16[128,64]{0,1:T(8,128)(2,1)S(1)}, u32[]{:S(2)}, u32[]{:S(2)}) collective-permute-start(bf16[128,64]{0,1:T(8,128)(2,1)S(1)} %select_reduce_fusion.2), channel_id=1, source_target_pairs={{0,224},{32,0},{64,32},{96,64},{128,96},{160,128},{192,160},{224,1... | collective-permute-start | bytes 49160 | tf_op jit(solution)/shard_map/ppermute | solution.py:9
